TPU v7x, 256 devices: a whole 4x4x8 slice. The times are simulated.
256 devices in a mesh: dp: 16 (over z_lo, x, core), fsdp: 16 (over y, z_hi).
Axes of the slice: x: 4, y: 4, z: 8 (z_hi: 4, z_lo: 2; z = z_hi * 2 + z_lo), core: 2. Of those that a mesh axis runs over, the one named last changes fastest.
Arguments:
- hidden_in: bfloat16 [131072, 1536], P(('dp', 'fsdp')), may hold values from -6 to 6
- grad_out: bfloat16 [131072, 1536], P(('dp', 'fsdp')), may hold values from -6 to 6
- lengths: int32 [256, 3], P(('dp', 'fsdp')), may hold values from 1 to 510, as said below
- conv_kernel: float32 [5, 1536], replicated, may hold values from -3 to 3
- norm_gain: float32 [1536], replicated, may hold values from 0.5 to 2
- out_weight: bfloat16 [1536, 1536], P('fsdp'), may hold values from -0.15625 to 0.15625
Outputs:
- output: float32 [131072, 1536], P(('dp', 'fsdp'))
- grad_hidden: float32 [131072, 1536], P(('dp', 'fsdp'))
- grad_weight: float32 [1536, 1536], P('fsdp')
- grad_kernel: float32 [5, 1536], replicated
- grad_gain: float32 [1536], replicated
Inputs may be any that keep to these rules, and one draw needn't show every extreme that they name: `lengths`: each row sums to at most 512. A row whose sum exceeds (3) * 128 sums to exactly 512, holds 2 utterances of length 1 followed by one of length 510, and then the row with the same fsdp index whose dp index differs by half the dp axis sums to at most (2) * 128; every other row sums to at most (3) * 128. Some row in every draw sums to 512.
All inputs are finite; a program needn't handle non-finite values.
Results may differ from a plain program's by a relative error of at most 0.003.
Values may be sent and summed in bfloat16 or wider, within the bound.
No kernel may reach another device: no remote copies, remote signals or barrier semaphores. Data moves between devices by JAX's collectives and lax.ppermute only.
A program may use at most 128 MiB of HBM per device.

v0:
```python
import math

import jax
import jax.numpy as jnp
from jax import lax
from jax.sharding import PartitionSpec as P

BLOCK = 128


def tap_mask(lengths, frames, count):
    utt_ends = jnp.cumsum(lengths)
    position = jnp.arange(frames, dtype=jnp.int32)
    segment_id = jnp.sum((position[:, None] >= utt_ends[None, :]).astype(jnp.int32), axis=1)
    inside = position < utt_ends[-1]
    half_width = count // 2
    segment_pad = jnp.pad(segment_id, half_width, constant_values=-1)
    inside_pad = jnp.pad(inside, half_width, constant_values=False)
    rows_out = []
    for k in range(count):
        same = (segment_pad[k : k + frames] == segment_id) & inside_pad[k : k + frames] & inside
        rows_out.append(same.astype(jnp.float32))
    return jnp.stack(rows_out)


def conv_front(extended, taps, conv_kernel, norm_gain):
    length = taps.shape[2]
    mixed = jnp.zeros((taps.shape[0], length, extended.shape[2]), jnp.float32)
    for k in range(conv_kernel.shape[0]):
        mixed = (
            mixed
            + conv_kernel[k] * extended[:, k : k + length].astype(jnp.float32) * taps[:, k, :, None]
        )
    centred = mixed - jnp.mean(mixed, axis=-1, keepdims=True)
    inverse = lax.rsqrt(jnp.mean(centred * centred, axis=-1, keepdims=True) + 1e-05)
    normed = centred * inverse
    scaled = normed * norm_gain
    squash = jax.nn.sigmoid(scaled)
    live_rows = taps[:, conv_kernel.shape[0] // 2, :, None]
    activation = (scaled * squash * live_rows).astype(jnp.bfloat16)
    return (activation, normed, inverse, scaled, squash, live_rows)


def conv_back(
    extended, taps, conv_kernel, norm_gain, grad_act, normed, inverse, scaled, squash, live_rows
):
    length = taps.shape[2]
    grad_scaled = grad_act * live_rows * squash * (1.0 + scaled * (1.0 - squash))
    gain_grad = jnp.sum(grad_scaled * normed, axis=(0, 1))
    grad_normed = grad_scaled * norm_gain
    grad_pre = inverse * (
        grad_normed
        - jnp.mean(grad_normed, axis=-1, keepdims=True)
        - normed * jnp.mean(grad_normed * normed, axis=-1, keepdims=True)
    )
    grad_ext = jnp.zeros(extended.shape, jnp.float32)
    kernel_rows = []
    for k in range(conv_kernel.shape[0]):
        weighted = grad_pre * taps[:, k, :, None]
        kernel_rows.append(
            jnp.sum(weighted * extended[:, k : k + length].astype(jnp.float32), axis=(0, 1))
        )
        grad_ext = grad_ext.at[:, k : k + length].add(conv_kernel[k] * weighted)
    return (grad_ext, jnp.stack(kernel_rows), gain_grad)


def weight_terms(source, cotangent):
    return lax.dot_general(
        source, cotangent, (((0,), (0,)), ((), ())), preferred_element_type=jnp.float32
    )


def shards(hidden_in, grad_out, lengths, conv_kernel, norm_gain, out_weight):
    frames, chans = hidden_in.shape
    width = grad_out.shape[1]
    blocks = frames // BLOCK
    count = conv_kernel.shape[0]
    half_width = count // 2
    taps_all = tap_mask(lengths[0], frames, count)
    tap_blocks = taps_all.reshape(count, blocks, BLOCK).transpose(1, 0, 2).astype(jnp.bfloat16)
    rows_in = hidden_in.reshape(blocks, BLOCK, chans)
    edge = jnp.zeros((1, half_width, chans), hidden_in.dtype)
    before = jnp.concatenate([edge, rows_in[:-1, BLOCK - half_width :]], axis=0)
    after = jnp.concatenate([rows_in[1:, :half_width], edge], axis=0)
    extended = jnp.concatenate([before, rows_in, after], axis=1)
    cot_rows = grad_out.reshape(blocks, BLOCK, width)
    taps_float = tap_blocks.astype(jnp.float32)
    activation, normed, inverse, scaled, squash, live_rows = conv_front(
        extended, taps_float, conv_kernel, norm_gain
    )
    slots = extended.shape[0]
    flat_act = activation.reshape(slots * BLOCK, chans)
    flat_cot = cot_rows.reshape(slots * BLOCK, width)
    full_weight = lax.all_gather(out_weight, "fsdp", axis=0, tiled=True)
    produced = jnp.dot(flat_act, full_weight, preferred_element_type=jnp.float32)
    grad_act = lax.dot_general(
        flat_cot, full_weight, (((1,), (1,)), ((), ())), preferred_element_type=jnp.float32
    )
    grad_ext, kernel_grad, gain_grad = conv_back(
        extended,
        taps_float,
        conv_kernel,
        norm_gain,
        grad_act.reshape(slots, BLOCK, chans),
        normed,
        inverse,
        scaled,
        squash,
        live_rows,
    )
    slot_out = produced.reshape(slots, BLOCK, width)
    centre = grad_ext[:, half_width : half_width + BLOCK]
    centre = centre.at[:-1, BLOCK - half_width :].add(grad_ext[1:, :half_width])
    centre = centre.at[1:, :half_width].add(grad_ext[:-1, BLOCK + half_width :])
    grad_hidden = centre.reshape(frames, chans)
    output = slot_out.reshape(frames, width)
    dp_count = lax.axis_size("dp")
    fsdp_count = lax.axis_size("fsdp")
    factor = 1.0 / math.sqrt(frames * dp_count * fsdp_count)
    shard_sum = lax.psum_scatter(
        weight_terms(flat_act, flat_cot), "fsdp", scatter_dimension=0, tiled=True
    )
    weight_sum = lax.psum(shard_sum, "dp")
    kernel_sum, gain_sum = lax.psum((kernel_grad, gain_grad), ("dp", "fsdp"))
    return (output, grad_hidden, weight_sum * factor, kernel_sum * factor, gain_sum * factor)


def solution(mesh):
    placed = (
        P(("dp", "fsdp"), None),
        P(("dp", "fsdp"), None),
        P(("dp", "fsdp"), None),
        P(),
        P(),
        P("fsdp", None),
    )
    return jax.shard_map(
        shards,
        mesh=mesh,
        in_specs=placed,
        out_specs=(P(("dp", "fsdp"), None), P(("dp", "fsdp"), None), P("fsdp", None), P(), P()),
        check_vma=False,
    )
```

profile of v0, /device:TPU:1, one launch (start us, length us, event | category | flops | bytes accessed | tf_op | source)
XLA Modules:
  0.0 398.8 jit_solution(10195507988931592520)
XLA Ops:
  8.0 0.8 reduce-window.4
  12.2 1.1 slice_reduce_fusion.4
  14.8 1.0 fusion.29
  15.8 2.3 fusion.17
  18.1 3.1 fusion.27
  21.2 1.6 copy-done.2
  23.4 69.4 %all-gather.2.cloned.1.call-done = bf16[1536,1536]{1,0:T(8,128)(2,1)} async-done(((bf16[96,1536]{1,0:T(8,128)(2,1)}), bf16[1536,1536]{1,0:T(8,128)(2,1)}) %all-gather.2.cloned.1.call-update) | async-done | bytes 4718608 | tf_op jit(solution)/shard_map/all_gather | solution.py:94
  92.7 4.7 %fusion.32 = f32[512,1536]{1,0:T(8,128)S(1)} fusion(bf16[512,1536]{1,0:T(8,128)(2,1)S(1)} %copy-done, bf16[1536,1536]{1,0:T(8,128)(2,1)} %all-gather.2.cloned.1.call-done), kind=kOutput, calls=%fused_computation.101 | convolution fusion | flops 2415919104 | bytes 9437184 | tf_op jit(solution)/shard_map/dot_general | solution.py:96
  97.4 2.6 multiply_reduce_fusion
  100.1 6.6 %fusion.15 = (f32[1536]{0:T(1024)S(1)}, f32[1536]{0:T(1024)S(1)}, f32[1536]{0:T(1024)S(1)}, f32[1536]{0:T(1024)S(1)}, f32[1536]{0:T(1024)S(1)}, /*index=5*/f32[4,128,1536]{2,1,0:T(8,128)}, bf16[4,128,1536]{2,1,0:T(8,128)(2,1)S(1)}) fusion(f32[4,128]{1,0:T(4,128)S(1)} %get-tuple-element.116, bf16[4,130,1536]{2,1,0:T(8,128)(2,1)S(1)} %copy-done.5, ...), kind=kLoop, calls=%fused_computation.27 | loop fusion | flops 26731008 | bytes 18929664 | tf_op jit(solution)/shard_map/reduce_sum | solution.py:61
  106.6 1.2 copy-done.9
  107.8 5.2 %fusion.33 = f32[1536,1536]{1,0:T(8,128)} fusion(bf16[512,1536]{1,0:T(8,128)(2,1)S(1)} %bitcast.49, bf16[512,1536]{1,0:T(8,128)(2,1)S(1)} %copy-done), kind=kOutput, calls=%fused_computation.102 | convolution fusion | flops 2415919104 | bytes 12582912 | tf_op jit(solution)/shard_map/dot_general | solution.py:68
  114.6 2.2 multiply_multiply_fusion
  116.8 2.1 scatter-add.24
  118.9 1.0 copy-done.1
  119.9 2.3 multiply_add_fusion
  122.2 9.2 %scatter-add.25 = f32[4,132,1536]{2,1,0:T(8,128)} dynamic-update-slice(f32[4,132,1536]{2,1,0:T(8,128)} %scatter-add.24, f32[4,128,1536]{2,1,0:T(8,128)} %multiply_add_fusion, s32[]{:T(128)} %constant.213.clone.1, s32[]{:T(128)} %constant.221.clone.1, s32[]{:T(128)} %constant.213.clone.1) | dynamic-update-slice | bytes 6291460 | tf_op jit(solution)/shard_map/scatter-add | solution.py:63
  131.4 5.3 %slice_add_fusion.2 = f32[4,128,1536]{2,1,0:T(8,128)} fusion(f32[4,132,1536]{2,1,0:T(8,128)} %scatter-add.25, f32[4,128,1536]{2,1,0:T(8,128)} %get-tuple-element.106, f32[4,128]{1,0:T(4,128)S(1)} %get-tuple-element.118, f32[1536]{0:T(1024)S(1)} %get-tuple-element.100), kind=kLoop, calls=%fused_computation.30 | loop fusion | flops 2359296 | bytes 9445376 | tf_op jit(solution)/shard_map/add | solution.py:63
  136.6 9.0 %scatter-add.26 = f32[4,132,1536]{2,1,0:T(8,128)} dynamic-update-slice(f32[4,132,1536]{2,1,0:T(8,128)} %scatter-add.25, f32[4,128,1536]{2,1,0:T(8,128)} %slice_add_fusion.2, s32[]{:T(128)} %constant.213.clone.1, s32[]{:T(128)} %constant.222.clone.1, s32[]{:T(128)} %constant.213.clone.1) | dynamic-update-slice | bytes 6291460 | tf_op jit(solution)/shard_map/scatter-add | solution.py:63
  145.6 5.4 %slice_add_fusion.1 = f32[4,128,1536]{2,1,0:T(8,128)} fusion(f32[4,132,1536]{2,1,0:T(8,128)} %scatter-add.26, f32[4,128,1536]{2,1,0:T(8,128)} %get-tuple-element.106, f32[4,128]{1,0:T(4,128)S(1)} %get-tuple-element.117, f32[1536]{0:T(1024)S(1)} %get-tuple-element.103), kind=kLoop, calls=%fused_computation.29 | loop fusion | flops 2359296 | bytes 9445376 | tf_op jit(solution)/shard_map/add | solution.py:63
  151.0 9.0 %scatter-add.29 = f32[4,132,1536]{2,1,0:T(8,128)} dynamic-update-slice(f32[4,132,1536]{2,1,0:T(8,128)} %scatter-add.26, f32[4,128,1536]{2,1,0:T(8,128)} %slice_add_fusion.1, s32[]{:T(128)} %constant.213.clone.1, s32[]{:T(128)} %constant.223.clone.1, s32[]{:T(128)} %constant.213.clone.1) | dynamic-update-slice | bytes 6291460 | tf_op jit(solution)/shard_map/scatter-add | solution.py:63
  160.0 5.3 %slice_add_fusion = f32[4,128,1536]{2,1,0:T(8,128)} fusion(f32[4,132,1536]{2,1,0:T(8,128)} %scatter-add.29, f32[4,128,1536]{2,1,0:T(8,128)} %get-tuple-element.106, f32[4,128]{1,0:T(4,128)S(1)} %get-tuple-element.116, f32[1536]{0:T(1024)S(1)} %get-tuple-element.102), kind=kLoop, calls=%fused_computation.28 | loop fusion | flops 2359296 | bytes 9445376 | tf_op jit(solution)/shard_map/add | solution.py:63
  165.3 8.9 %scatter-add.30 = f32[4,132,1536]{2,1,0:T(8,128)} dynamic-update-slice(f32[4,132,1536]{2,1,0:T(8,128)} %scatter-add.29, f32[4,128,1536]{2,1,0:T(8,128)} %slice_add_fusion, s32[]{:T(128)} %constant.213.clone.1, s32[]{:T(128)} %constant.224.clone.1, s32[]{:T(128)} %constant.213.clone.1) | dynamic-update-slice | bytes 6291460 | tf_op jit(solution)/shard_map/scatter-add | solution.py:63
  174.2 2.4 slice.334
  176.7 1.7 copy-done.8
  178.3 2.9 add_select_fusion
  181.2 3.0 scatter-add.31
  184.3 84.7 %all-reduce.5 = (f32[5,1536]{1,0:T(8,128)S(1)}, f32[1536]{0:T(1024)S(1)}) all-reduce(f32[5,1536]{1,0:T(8,128)S(1)} %stack.35, f32[1536]{0:T(1024)S(1)} %get-tuple-element.89), channel_id=1, replica_groups=mesh['dp'=16,'fsdp'=16] {'dp','fsdp'}, use_global_device_ids=true, to_apply=%region_14.15 | all-reduce | flops 9216 | bytes 73728 | tf_op jit(solution)/shard_map/psum | solution.py:124
  270.2 1.6 fusion.18
  271.9 6.6 %fusion.31 = f32[512,1536]{1,0:T(8,128)} fusion(bf16[512,1536]{1,0:T(8,128)(2,1)S(1)} %bitcast.50, bf16[1536,1536]{1,0:T(8,128)(2,1)} %all-gather.2.cloned.1.call-done), kind=kOutput, calls=%fused_computation.100 | convolution fusion | flops 2415919104 | bytes 9437184 | tf_op jit(solution)/shard_map/dot_general | solution.py:95
  278.5 111.8 %all-reduce.8.cloned.1.call-done = f32[96,1536]{1,0:T(8,128)} async-done(((f32[96,1536]{1,0:T(8,128)}), f32[96,1536]{1,0:T(8,128)}) %all-reduce.8.cloned.1.call-update) | async-done | bytes 589840 | tf_op jit(solution)/shard_map/psum | solution.py:123
  390.3 1.9 broadcast_multiply_fusion
  (54 shorter events, 9.1 us)
Async XLA Ops:
  7.2 85.6 %copy-start = (bf16[512,1536]{1,0:T(8,128)(2,1)S(1)}, bf16[512,1536]{1,0:T(8,128)(2,1)}, u32[]{:S(2)}) copy-start(bf16[512,1536]{1,0:T(8,128)(2,1)} %param.21) | copy-start | bytes 4718596
  7.2 85.5 %all-gather.2.cloned.1.call-start = ((), (), s32[]{:S(2)}) async-start(), calls=%async_computation.1 | async-start | bytes 5013504 | tf_op jit(solution)/shard_map/all_gather | solution.py:94
  7.9 263.9 %reduce-scatter.2.cloned.1.call-start = ((), (), s32[]{:S(2)}) async-start(), calls=%async_computation.2 | async-start | bytes 10027008 | tf_op jit(solution)/shard_map/reduce_scatter | solution.py:120
  8.8 9.3 %copy-start.6 = (bf16[512,1536]{1,0:T(8,128)(2,1)S(1)}, bf16[512,1536]{1,0:T(8,128)(2,1)}, u32[]{:S(2)}) copy-start(bf16[512,1536]{1,0:T(8,128)(2,1)} %param.20) | copy-start | bytes 4718596
  18.1 3.1 copy-start.4
  21.2 1.7 copy-start.2
  23.4 74.0 %copy-start.11 = (f32[1536]{0:T(1024)S(1)}, f32[1536]{0:T(1024)}, u32[]{:S(2)}) copy-start(f32[1536]{0:T(1024)} %param.24) | copy-start | bytes 18436
  92.7 4.7 %copy-start.3 = (f32[4,128,1536]{2,1,0:T(8,128)S(1)}, f32[4,128,1536]{2,1,0:T(8,128)}, u32[]{:S(2)}) copy-start(f32[4,128,1536]{2,1,0:T(8,128)} %copy-done.2) | copy-start | bytes 9437188
  97.4 2.6 copy-start.5
  97.4 2.6 copy-start.7
  106.6 1.2 copy-start.9
  113.0 0.9 copy-start.12
  113.0 277.3 %all-reduce.8.cloned.1.call-start = ((), (), s32[]{:S(2)}) async-start(), calls=%async_computation.3 | async-start | bytes 1179648 | tf_op jit(solution)/shard_map/psum | solution.py:123
  116.8 3.1 copy-start.1
  174.2 97.7 %copy-start.10 = (bf16[4,128,1536]{2,1,0:T(8,128)(2,1)S(1)}, bf16[4,128,1536]{2,1,0:T(8,128)(2,1)}, u32[]{:S(2)}) copy-start(bf16[4,128,1536]{2,1,0:T(8,128)(2,1)} %copy-done.9) | copy-start | bytes 4718596
  176.7 1.7 copy-start.8
Sparse Core Ops, SparseCore 0:
  10.5 82.2 all-gather.1
  113.1 131.3 reduce-scatter.1
  272.0 118.2 all-reduce.7
where the time goes:
time: 403 us; the launch traced here: 399 us
  waiting for transfers between devices  182 us (45%)
  blocking collectives  84.7 us (21%)
  local copies, waits for them, and re-layouts  52.4 us (13%)
  other arithmetic  49 us (12%)
  matrix products  16.5 us (4%)
  between operations  14 us (3%)
    psum x1, waiting for transfers between devices, shards(): weight_sum = lax.psum(shard_sum, 'dp')  112 us
    psum x1, blocking collectives, shards(): kernel_sum, gain_sum = lax.psum((kernel_grad, gain_grad), ('dp', 'fsdp'))  84.7 us
    all_gather x1, waiting for transfers between devices, shards(): full_weight = lax.all_gather(out_weight, 'fsdp', axis=0, tiled=True)  69.4 us
    scatter-add x5, local copies, waits for them, and re-layouts, conv_back(): grad_ext = grad_ext.at[:, k:k + length].add(conv_kernel[k] * weighted)  38.2 us
    add x4, other arithmetic, conv_back(): grad_ext = grad_ext.at[:, k:k + length].add(conv_kernel[k] * weighted)  18.2 us
  transfers between devices with their start and end apart: 3, of which 2 were waited for; matrix products, arithmetic and copies ran while one was open for 23% of the time, Pallas kernels for 0%

commit v1 on v0

v1 whole, which is shorter than its diff:
```python
import math

import jax
import jax.numpy as jnp
from jax import lax
from jax.sharding import PartitionSpec as P


def tap_mask(lengths, frames, count):
    utt_ends = jnp.cumsum(lengths)
    position = jnp.arange(frames, dtype=jnp.int32)
    segment_id = jnp.sum((position[:, None] >= utt_ends[None, :]).astype(jnp.int32), axis=1)
    inside = position < utt_ends[-1]
    half_width = count // 2
    segment_pad = jnp.pad(segment_id, half_width, constant_values=-1)
    inside_pad = jnp.pad(inside, half_width, constant_values=False)
    rows_out = []
    for k in range(count):
        same = (segment_pad[k : k + frames] == segment_id) & inside_pad[k : k + frames] & inside
        rows_out.append(same.astype(jnp.float32))
    return jnp.stack(rows_out)


def shifted(x, half_width):
    frames = x.shape[0]
    padded = jnp.pad(x, ((half_width, half_width), (0, 0)))
    return [padded[k : k + frames] for k in range(2 * half_width + 1)]


def butterfly(x, axis):
    size = lax.axis_size(axis)
    step = 1
    while step < size:
        pairs = [(i, i ^ step) for i in range(size)]
        x = x + lax.ppermute(x, axis, pairs)
        step *= 2
    return x


def shards(hidden_in, grad_out, lengths, conv_kernel, norm_gain, out_weight):
    frames, chans = hidden_in.shape
    count = conv_kernel.shape[0]
    half_width = count // 2
    full_weight = lax.all_gather(out_weight, "fsdp", axis=0, tiled=True)
    taps = tap_mask(lengths[0], frames, count)
    live = taps[half_width][:, None]
    views = shifted(hidden_in, half_width)
    mixed = jnp.zeros((frames, chans), jnp.float32)
    for k in range(count):
        mixed = mixed + conv_kernel[k] * views[k].astype(jnp.float32) * taps[k][:, None]
    centred = mixed - jnp.mean(mixed, axis=-1, keepdims=True)
    inverse = lax.rsqrt(jnp.mean(centred * centred, axis=-1, keepdims=True) + 1e-05)
    normed = centred * inverse
    scaled = normed * norm_gain
    squash = jax.nn.sigmoid(scaled)
    activation = (scaled * squash * live).astype(jnp.bfloat16)
    weight_terms = lax.dot_general(
        activation, grad_out, (((0,), (0,)), ((), ())), preferred_element_type=jnp.float32
    )
    shard_sum = lax.psum_scatter(weight_terms, "fsdp", scatter_dimension=0, tiled=True)
    output = jnp.dot(activation, full_weight, preferred_element_type=jnp.float32)
    grad_act = lax.dot_general(
        grad_out, full_weight, (((1,), (1,)), ((), ())), preferred_element_type=jnp.float32
    )
    grad_scaled = grad_act * live * squash * (1.0 + scaled * (1.0 - squash))
    gain_grad = jnp.sum(grad_scaled * normed, axis=0)
    grad_normed = grad_scaled * norm_gain
    grad_mixed = inverse * (
        grad_normed
        - jnp.mean(grad_normed, axis=-1, keepdims=True)
        - normed * jnp.mean(grad_normed * normed, axis=-1, keepdims=True)
    )
    kernel_rows = []
    for k in range(count):
        weighted = grad_mixed * taps[k][:, None]
        kernel_rows.append(jnp.sum(weighted * views[k].astype(jnp.float32), axis=0))
    back_views = shifted(grad_mixed, half_width)
    grad_hidden = jnp.zeros((frames, chans), jnp.float32)
    for k in range(count):
        grad_hidden = grad_hidden + conv_kernel[k] * (
            back_views[count - 1 - k] * taps[count - 1 - k][:, None]
        )
    small = jnp.concatenate([jnp.stack(kernel_rows), gain_grad[None]], axis=0)
    small = butterfly(small, "fsdp")
    total = butterfly(jnp.concatenate([shard_sum, small], axis=0), "dp")
    rows = shard_sum.shape[0]
    dp_count = lax.axis_size("dp")
    fsdp_count = lax.axis_size("fsdp")
    factor = 1.0 / math.sqrt(frames * dp_count * fsdp_count)
    weight_sum = total[:rows] * factor
    kernel_sum = total[rows : rows + count] * factor
    gain_sum = total[rows + count] * factor
    return (output, grad_hidden, weight_sum, kernel_sum, gain_sum)


def solution(mesh):
    placed = (
        P(("dp", "fsdp"), None),
        P(("dp", "fsdp"), None),
        P(("dp", "fsdp"), None),
        P(),
        P(),
        P("fsdp", None),
    )
    return jax.shard_map(
        shards,
        mesh=mesh,
        in_specs=placed,
        out_specs=(P(("dp", "fsdp"), None), P(("dp", "fsdp"), None), P("fsdp", None), P(), P()),
        check_vma=False,
    )
```

time: 403 us -> 292 us (0.72)
  blocking collectives: 84.7 us -> 0 us
  local copies, waits for them, and re-layouts: 52.4 us -> 3 us
  waiting for transfers between devices: 182 us -> 207 us
  other arithmetic: 49 us -> 25.9 us
  starting transfers between devices: 0.3 us -> 20.3 us
    psum x1 -> x0, waiting for transfers between devices: 112 us -> none  [shards(): weight_sum = lax.psum(shard_sum, 'dp')]
    reduce_scatter x1, waiting for transfers between devices: 0.01 us -> 95.6 us  [shards(): lax.psum_scatter(weight_terms, 'fsdp', scatter_dimension=0, tiled=True)]
    psum x1 -> x0, blocking collectives: 84.7 us -> none  [shards(): kernel_sum, gain_sum = lax.psum((kernel_grad, gain_grad), ('dp', 'fsdp'))]
    ppermute x0 -> x8, waiting for transfers between devices: none -> 46.1 us  [butterfly(): x = x + lax.ppermute(x, axis, pairs)]
    scatter-add x6 -> x0, local copies, waits for them, and re-layouts: 41.2 us -> none  [the longest x5 38.2 us: conv_back(): grad_ext = grad_ext.at[:, k:k + length].add(conv_kernel[k] * weighted)]
    ppermute x0 -> x8, starting transfers between devices: none -> 20.2 us  [butterfly(): x = x + lax.ppermute(x, axis, pairs)]
    add x4 -> x9, other arithmetic: 18.2 us -> 5.46 us  [the longest x1 4.04 us: shards(): grad_hidden + conv_kernel[k] * (back_views[count - 1 - k] * taps[count -...]
    another operation x5 -> x1, other arithmetic: 5.16 us -> 0.83 us
  transfers between devices with their start and end apart: 3 -> 10, of which waited for: 2 -> 10; matrix products, arithmetic and copies ran while one was open for 23% -> 15% of each run, Pallas kernels for 0% -> 0%
where the time goes in v1:
time: 292 us; the launch traced here: 290 us
  waiting for transfers between devices  207 us (71%)
  other arithmetic  25.9 us (9%)
  starting transfers between devices  20.3 us (7%)
  matrix products  19.6 us (7%)
  between operations  14.2 us (5%)
  local copies, waits for them, and re-layouts  3 us (1%)
    reduce_scatter x1, waiting for transfers between devices, shards(): lax.psum_scatter(weight_terms, 'fsdp', scatter_dimension=0, tiled=True)  95.6 us
    all_gather x1, waiting for transfers between devices, shards(): full_weight = lax.all_gather(out_weight, 'fsdp', axis=0, tiled=True)  65 us
    ppermute x8, waiting for transfers between devices, butterfly(): x = x + lax.ppermute(x, axis, pairs)  46.1 us
    ppermute x8, starting transfers between devices, butterfly(): x = x + lax.ppermute(x, axis, pairs)  20.2 us
    reduce_sum x1, other arithmetic, shards(): centred = mixed - jnp.mean(mixed, axis=-1, keepdims=True)  8.57 us
    dot_general x1, matrix products, shards(): lax.dot_general(grad_out, full_weight, (((1,), (1,)), ((), ())), preferre...  7.12 us
    dot_general x1, matrix products, shards(): jnp.dot(activation, full_weight, preferred_element_type=jnp.float32)  7.04 us
  transfers between devices with their start and end apart: 10, of which 10 were waited for; matrix products, arithmetic and copies ran while one was open for 15% of the time, Pallas kernels for 0%

profile of v1, /device:TPU:1, one launch (start us, length us, event | category | flops | bytes accessed | tf_op | source)
XLA Modules:
  0.0 290.4 jit_solution(425887298165945984)
XLA Ops:
  7.2 0.7 all-gather.2.cloned.1.call-update
  8.0 0.8 reduce-window.4
  10.1 1.1 slice_reduce_fusion.4
  11.2 0.7 and_convert_fusion.4
  11.9 8.6 %fusion.28 = (f32[512]{0:T(512)S(1)}, f32[512,1536]{1,0:T(8,128)S(1)}) fusion(f32[512]{0:T(512)S(1)} %get-tuple-element.24, f32[1536]{0:T(1024)S(1)} %get-tuple-element.16, f32[512]{0:T(512)S(1)} %get-tuple-element.22, f32[1536]{0:T(1024)S(1)} %get-tuple-element.17, f32[512]{0:T(512)S(1)} %get-tuple-element.26, bf16[512,1536]{1,0:T(8,128)(2,1)} %param.6, ...), kind=kLoop, calls=%fused_computation.80 | loop fusion | flops 15728128 | bytes 4761600 | tf_op jit(solution)/shard_map/reduce_sum | solution.py:51
  21.0 1.2 copy-done.1
  22.2 5.4 %fusion.26 = f32[1536,1536]{1,0:T(8,128)} fusion(bf16[512,1536]{1,0:T(8,128)(2,1)S(1)} %copy-done, f32[512,1536]{1,0:T(8,128)S(1)} %get-tuple-element.20, f32[1536]{0:T(1024)S(1)} %copy-done.6, f32[512]{0:T(512)S(1)} %add_rsqrt_fusion, f32[512]{0:T(512)S(1)} %broadcast_multiply_fusion.2, f32[512]{0:T(512)S(1)} %get-tuple-element.26), kind=kOutput, calls=%fused_computation.78 | convolution fusion | flops 2422996992 | bytes 14168064 | tf_op jit(solution)/shard_map/dot_general | solution.py:57
  27.7 65.0 %all-gather.2.cloned.1.call-done = bf16[1536,1536]{1,0:T(8,128)(2,1)} async-done(((bf16[96,1536]{1,0:T(8,128)(2,1)}), bf16[1536,1536]{1,0:T(8,128)(2,1)}) %all-gather.2.cloned.1.call-update) | async-done | bytes 4718608 | tf_op jit(solution)/shard_map/all_gather | solution.py:44
  92.7 7.1 %multiply_reduce_fusion = (f32[1536]{0:T(1024)S(1)}, f32[512]{0:T(512)S(1)}, f32[512]{0:T(512)S(1)}, f32[512,1536]{1,0:T(8,128)S(1)}) fusion(f32[512,1536]{1,0:T(8,128)} %copy-done.1, f32[512]{0:T(512)S(1)} %add_rsqrt_fusion, f32[512]{0:T(512)S(1)} %broadcast_multiply_fusion.2, f32[1536]{0:T(1024)S(1)} %copy-done.6, f32[512]{0:T(512)S(1)} %get-tuple-element.26, ...), kind=kOutput, calls=%fused_computation.27 | convolution fusion | flops 2430072320 | bytes 12605440 | tf_op jit(solution)/shard_map/dot_general | solution.py:62
  99.9 5.8 %fusion.15 = (f32[1536]{0:T(1024)S(1)}, f32[1536]{0:T(1024)S(1)}, f32[1536]{0:T(1024)S(1)}, f32[1536]{0:T(1024)S(1)}, f32[1536]{0:T(1024)S(1)}, /*index=5*/f32[512,1536]{1,0:T(8,128)}) fusion(f32[512]{0:T(512)S(1)} %get-tuple-element.24, bf16[512,1536]{1,0:T(8,128)(2,1)S(1)} %copy-done.5, f32[512]{0:T(512)S(1)} %get-tuple-element.22, ...), kind=kLoop, calls=%fused_computation.26 | loop fusion | flops 21225984 | bytes 11065344 | tf_op jit(solution)/shard_map/reduce_sum | solution.py:76
  105.8 6.0 %collective-permute-start = (f32[6,1536]{1,0:T(8,128)S(1)}, f32[6,1536]{1,0:T(8,128)S(1)}, u32[]{:S(2)}, u32[]{:S(2)}) collective-permute-start(f32[6,1536]{1,0:T(8,128)S(1)} %concatenate.6), channel_id=1, source_target_pairs={{0,1},{1,0},{2,3},{3,2},{4,5},{5,4},{6,7},{7,6},{8,9},{9,8},{10,11... | collective-permute-start | bytes 110600 | tf_op jit(solution)/shard_map/ppermute | solution.py:35
  111.8 1.7 collective-permute-done
  113.6 2.4 collective-permute-start.1
  116.0 9.0 %collective-permute-done.1 = f32[6,1536]{1,0:T(8,128)S(1)} collective-permute-done((f32[6,1536]{1,0:T(8,128)S(1)}, f32[6,1536]{1,0:T(8,128)S(1)}, u32[]{:S(2)}, u32[]{:S(2)}) %collective-permute-start.1) | collective-permute-done | bytes 36896 | tf_op jit(solution)/shard_map/ppermute | solution.py:35
  125.0 1.7 collective-permute-start.2
  126.7 1.9 collective-permute-done.2
  128.6 3.5 %collective-permute-start.3 = (f32[6,1536]{1,0:T(8,128)S(1)}, f32[6,1536]{1,0:T(8,128)S(1)}, u32[]{:S(2)}, u32[]{:S(2)}) collective-permute-start(f32[6,1536]{1,0:T(8,128)S(1)} %add.87), channel_id=1, source_target_pairs={{0,8},{1,9},{2,10},{3,11},{4,12},{5,13},{6,14},{7,15},{8,0},{9,1},... | collective-permute-start | bytes 110600 | tf_op jit(solution)/shard_map/ppermute | solution.py:35
  132.1 2.3 collective-permute-done.3
  134.3 95.6 %reduce-scatter.2.cloned.1.call-done = f32[96,1536]{1,0:T(8,128)} async-done(((f32[1536,1536]{1,0:T(8,128)}), f32[96,1536]{1,0:T(8,128)}) %reduce-scatter.2.cloned.1.call-update) | async-done | bytes 589840 | tf_op jit(solution)/shard_map/reduce_scatter | solution.py:60
  229.9 1.3 pad_maximum_fusion
  231.2 1.3 collective-permute-start.4
  232.5 1.7 collective-permute-done.4
  234.2 1.2 fusion.25
  235.3 1.4 collective-permute-start.5
  236.7 14.3 %collective-permute-done.5 = f32[102,1536]{1,0:T(8,128)S(1)} collective-permute-done((f32[102,1536]{1,0:T(8,128)S(1)}, f32[102,1536]{1,0:T(8,128)S(1)}, u32[]{:S(2)}, u32[]{:S(2)}) %collective-permute-start.5) | collective-permute-done | bytes 626720 | tf_op jit(solution)/shard_map/ppermute | solution.py:35
  251.1 2.8 collective-permute-start.6
  253.9 7.0 %fusion.27 = f32[512,1536]{1,0:T(8,128)} fusion(bf16[1536,1536]{1,0:T(8,128)(2,1)} %all-gather.2.cloned.1.call-done, f32[512,1536]{1,0:T(8,128)S(1)} %copy-done.3, f32[1536]{0:T(1024)S(1)} %copy-done.6, f32[512]{0:T(512)S(1)} %add_rsqrt_fusion, f32[512]{0:T(512)S(1)} %broadcast_multiply_fusion.2, f32[512]{0:T(512)S(1)} %get-tuple-element.26), kind=kOutput, calls=%fused_computation.79 | convolution fusion | flops 2422996992 | bytes 11022336 | tf_op jit(solution)/shard_map/dot_general | solution.py:61
  260.9 6.5 %collective-permute-done.6 = f32[102,1536]{1,0:T(8,128)S(1)} collective-permute-done((f32[102,1536]{1,0:T(8,128)S(1)}, f32[102,1536]{1,0:T(8,128)S(1)}, u32[]{:S(2)}, u32[]{:S(2)}) %collective-permute-start.6) | collective-permute-done | bytes 626720 | tf_op jit(solution)/shard_map/ppermute | solution.py:35
  267.4 1.1 collective-permute-start.7
  268.6 4.0 %multiply_add_fusion = f32[512,1536]{1,0:T(8,128)} fusion(f32[512,1536]{1,0:T(8,128)S(1)} %copy-done.4, f32[512]{0:T(512)S(1)} %get-tuple-element.24, f32[1536]{0:T(1024)S(1)} %get-tuple-element.16, f32[512]{0:T(512)S(1)} %get-tuple-element.22, f32[1536]{0:T(1024)S(1)} %get-tuple-element.17, f32[512]{0:T(512)S(1)} %get-tuple-element.26, ...), kind=kLoop, calls=%fused_computation.28 | loop fusion | flops 11010048 | bytes 6332416 | tf_op jit(solution)/shard_map/add | solution.py:80
  272.6 8.8 %collective-permute-done.7 = f32[102,1536]{1,0:T(8,128)S(1)} collective-permute-done((f32[102,1536]{1,0:T(8,128)S(1)}, f32[102,1536]{1,0:T(8,128)S(1)}, u32[]{:S(2)}, u32[]{:S(2)}) %collective-permute-start.7) | collective-permute-done | bytes 626720 | tf_op jit(solution)/shard_map/ppermute | solution.py:35
  281.5 0.9 slice_multiply_fusion
  (40 shorter events, 3.5 us)
Async XLA Ops:
  7.2 15.0 %copy-start = (bf16[512,1536]{1,0:T(8,128)(2,1)S(1)}, bf16[512,1536]{1,0:T(8,128)(2,1)}, u32[]{:S(2)}) copy-start(bf16[512,1536]{1,0:T(8,128)(2,1)} %param.7) | copy-start | bytes 4718596
  7.2 85.5 %all-gather.2.cloned.1.call-start = ((), (), s32[]{:S(2)}) async-start(), calls=%async_computation.1 | async-start | bytes 5013504 | tf_op jit(solution)/shard_map/all_gather | solution.py:44
  7.9 222.0 %reduce-scatter.2.cloned.1.call-start = ((), (), s32[]{:S(2)}) async-start(), calls=%async_computation.2 | async-start | bytes 10027008 | tf_op jit(solution)/shard_map/reduce_scatter | solution.py:60
  11.9 10.3 %copy-start.6 = (f32[1536]{0:T(1024)S(1)}, f32[1536]{0:T(1024)}, u32[]{:S(2)}) copy-start(f32[1536]{0:T(1024)} %param.10) | copy-start | bytes 18436
  20.5 1.7 copy-start.1
  27.7 72.2 %copy-start.5 = (bf16[512,1536]{1,0:T(8,128)(2,1)S(1)}, bf16[512,1536]{1,0:T(8,128)(2,1)}, u32[]{:S(2)}) copy-start(bf16[512,1536]{1,0:T(8,128)(2,1)} %param.6) | copy-start | bytes 4718596
  92.7 7.2 %copy-start.2 = (f32[512,1536]{1,0:T(8,128)S(1)}, f32[512,1536]{1,0:T(8,128)}, u32[]{:S(2)}) copy-start(f32[512,1536]{1,0:T(8,128)} %copy-done.1) | copy-start | bytes 9437188
  105.8 7.8 %collective-permute-start = (f32[6,1536]{1,0:T(8,128)S(1)}, f32[6,1536]{1,0:T(8,128)S(1)}, u32[]{:S(2)}, u32[]{:S(2)}) collective-permute-start(f32[6,1536]{1,0:T(8,128)S(1)} %concatenate.6), channel_id=1, source_target_pairs={{0,1},{1,0},{2,3},{3,2},{4,5},{5,4},{6,7},{7,6},{8,9},{9,8},{10,11... | collective-permute-start | bytes 110600 | tf_op jit(solution)/shard_map/ppermute | solution.py:35
  113.6 11.4 %collective-permute-start.1 = (f32[6,1536]{1,0:T(8,128)S(1)}, f32[6,1536]{1,0:T(8,128)S(1)}, u32[]{:S(2)}, u32[]{:S(2)}) collective-permute-start(f32[6,1536]{1,0:T(8,128)S(1)} %add.85), channel_id=1, source_target_pairs={{0,2},{1,3},{2,0},{3,1},{4,6},{5,7},{6,4},{7,5},{8,10},{9,11},{10,... | collective-permute-start | bytes 110600 | tf_op jit(solution)/shard_map/ppermute | solution.py:35
  125.0 3.6 %collective-permute-start.2 = (f32[6,1536]{1,0:T(8,128)S(1)}, f32[6,1536]{1,0:T(8,128)S(1)}, u32[]{:S(2)}, u32[]{:S(2)}) collective-permute-start(f32[6,1536]{1,0:T(8,128)S(1)} %add.86), channel_id=1, source_target_pairs={{0,4},{1,5},{2,6},{3,7},{4,0},{5,1},{6,2},{7,3},{8,12},{9,13},{10,... | collective-permute-start | bytes 110600 | tf_op jit(solution)/shard_map/ppermute | solution.py:35
  128.6 5.8 %collective-permute-start.3 = (f32[6,1536]{1,0:T(8,128)S(1)}, f32[6,1536]{1,0:T(8,128)S(1)}, u32[]{:S(2)}, u32[]{:S(2)}) collective-permute-start(f32[6,1536]{1,0:T(8,128)S(1)} %add.87), channel_id=1, source_target_pairs={{0,8},{1,9},{2,10},{3,11},{4,12},{5,13},{6,14},{7,15},{8,0},{9,1},... | collective-permute-start | bytes 110600 | tf_op jit(solution)/shard_map/ppermute | solution.py:35
  229.9 23.9 %copy-start.3 = (f32[512,1536]{1,0:T(8,128)S(1)}, f32[512,1536]{1,0:T(8,128)}, u32[]{:S(2)}) copy-start(f32[512,1536]{1,0:T(8,128)} %copy-done.1) | copy-start | bytes 9437188
  231.2 3.0 %collective-permute-start.4 = (f32[102,1536]{1,0:T(8,128)S(1)}, f32[102,1536]{1,0:T(8,128)S(1)}, u32[]{:S(2)}, u32[]{:S(2)}) collective-permute-start(f32[102,1536]{1,0:T(8,128)S(1)} %pad_maximum_fusion), channel_id=1, source_target_pairs={{0,16},{16,0},{32,48},{48,32},{64,80},{80,64},{96,112},{112,96},{1... | collective-permute-start | bytes 1880072 | tf_op jit(solution)/shard_map/ppermute | solution.py:35
  235.3 15.7 %collective-permute-start.5 = (f32[102,1536]{1,0:T(8,128)S(1)}, f32[102,1536]{1,0:T(8,128)S(1)}, u32[]{:S(2)}, u32[]{:S(2)}) collective-permute-start(f32[102,1536]{1,0:T(8,128)S(1)} %fusion.25), channel_id=1, source_target_pairs={{0,32},{16,48},{32,0},{48,16},{64,96},{80,112},{96,64},{112,80},{1... | collective-permute-start | bytes 1880072 | tf_op jit(solution)/shard_map/ppermute | solution.py:35
  251.1 16.3 %collective-permute-start.6 = (f32[102,1536]{1,0:T(8,128)S(1)}, f32[102,1536]{1,0:T(8,128)S(1)}, u32[]{:S(2)}, u32[]{:S(2)}) collective-permute-start(f32[102,1536]{1,0:T(8,128)S(1)} %add.90), channel_id=1, source_target_pairs={{0,64},{16,80},{32,96},{48,112},{64,0},{80,16},{96,32},{112,48},{1... | collective-permute-start | bytes 1880072 | tf_op jit(solution)/shard_map/ppermute | solution.py:35
  253.9 14.7 %copy-start.4 = (f32[512,1536]{1,0:T(8,128)S(1)}, f32[512,1536]{1,0:T(8,128)}, u32[]{:S(2)}) copy-start(f32[512,1536]{1,0:T(8,128)} %get-tuple-element.18) | copy-start | bytes 9437188
  267.4 13.9 %collective-permute-start.7 = (f32[102,1536]{1,0:T(8,128)S(1)}, f32[102,1536]{1,0:T(8,128)S(1)}, u32[]{:S(2)}, u32[]{:S(2)}) collective-permute-start(f32[102,1536]{1,0:T(8,128)S(1)} %add.91), channel_id=1, source_target_pairs={{0,128},{16,144},{32,160},{48,176},{64,192},{80,208},{96,224},{112... | collective-permute-start | bytes 1880072 | tf_op jit(solution)/shard_map/ppermute | solution.py:35
Sparse Core Ops, SparseCore 0:
  10.5 82.1 all-gather.1
  96.5 133.3 reduce-scatter.1

commit v2 on v1

--- a/solution.py
+++ b/solution.py
@@ -27,21 +27,30 @@
     return [padded[k : k + frames] for k in range(2 * half_width + 1)]
 
 
-def butterfly(x, axis):
+def butterfly(x, axis, steps):
     size = lax.axis_size(axis)
-    step = 1
-    while step < size:
+    for step in steps:
         pairs = [(i, i ^ step) for i in range(size)]
         x = x + lax.ppermute(x, axis, pairs)
-        step *= 2
     return x
+
+
+def sibling(x):
+    size = lax.axis_size("dp")
+    return lax.ppermute(x, "dp", [(i, i ^ 1) for i in range(size)])
 
 
 def shards(hidden_in, grad_out, lengths, conv_kernel, norm_gain, out_weight):
     frames, chans = hidden_in.shape
+    width = grad_out.shape[1]
     count = conv_kernel.shape[0]
     half_width = count // 2
-    full_weight = lax.all_gather(out_weight, "fsdp", axis=0, tiled=True)
+    fsdp_count = lax.axis_size("fsdp")
+    dp_count = lax.axis_size("dp")
+    rows = out_weight.shape[0]
+    half_rows = rows // 2
+    core = lax.axis_index("dp") % 2
+    gathered = lax.all_gather(out_weight, "fsdp", axis=0, tiled=True)
     taps = tap_mask(lengths[0], frames, count)
     live = taps[half_width][:, None]
     views = shifted(hidden_in, half_width)
@@ -54,10 +63,16 @@
     scaled = normed * norm_gain
     squash = jax.nn.sigmoid(scaled)
     activation = (scaled * squash * live).astype(jnp.bfloat16)
-    weight_terms = lax.dot_general(
-        activation, grad_out, (((0,), (0,)), ((), ())), preferred_element_type=jnp.float32
-    )
-    shard_sum = lax.psum_scatter(weight_terms, "fsdp", scatter_dimension=0, tiled=True)
+    split_act = activation.reshape(frames, fsdp_count, 2, half_rows)
+    keep_act = lax.dynamic_index_in_dim(split_act, core, 2, keepdims=False).reshape(frames, -1)
+    send_act = lax.dynamic_index_in_dim(split_act, 1 - core, 2, keepdims=False).reshape(frames, -1)
+    contract = (((0,), (0,)), ((), ()))
+    keep_terms = lax.dot_general(keep_act, grad_out, contract, preferred_element_type=jnp.float32)
+    send_terms = lax.dot_general(send_act, grad_out, contract, preferred_element_type=jnp.float32)
+    chip_terms = keep_terms + sibling(send_terms)
+    gathered, chip_terms, activation = lax.optimization_barrier((gathered, chip_terms, activation))
+    shard_sum = lax.psum_scatter(chip_terms, "fsdp", scatter_dimension=0, tiled=True)
+    full_weight = gathered
     output = jnp.dot(activation, full_weight, preferred_element_type=jnp.float32)
     grad_act = lax.dot_general(
         grad_out, full_weight, (((1,), (1,)), ((), ())), preferred_element_type=jnp.float32
@@ -81,16 +96,24 @@
             back_views[count - 1 - k] * taps[count - 1 - k][:, None]
         )
     small = jnp.concatenate([jnp.stack(kernel_rows), gain_grad[None]], axis=0)
-    small = butterfly(small, "fsdp")
-    total = butterfly(jnp.concatenate([shard_sum, small], axis=0), "dp")
-    rows = shard_sum.shape[0]
-    dp_count = lax.axis_size("dp")
-    fsdp_count = lax.axis_size("fsdp")
+    small = butterfly(small, "fsdp", (1, 2, 4, 8))
+    small = butterfly(small, "dp", (1, 2, 4, 8))
+    shard_sum, small = lax.optimization_barrier((shard_sum, small))
+    half_sum = butterfly(shard_sum, "dp", (2, 4, 8))
+    other_sum = sibling(half_sum)
+    weight_sum = jnp.where(
+        core == 0,
+        jnp.concatenate([half_sum, other_sum], axis=0),
+        jnp.concatenate([other_sum, half_sum], axis=0),
+    )
     factor = 1.0 / math.sqrt(frames * dp_count * fsdp_count)
-    weight_sum = total[:rows] * factor
-    kernel_sum = total[rows : rows + count] * factor
-    gain_sum = total[rows + count] * factor
-    return (output, grad_hidden, weight_sum, kernel_sum, gain_sum)
+    return (
+        output,
+        grad_hidden,
+        weight_sum * factor,
+        small[:count] * factor,
+        small[count] * factor,
+    )
 
 
 def solution(mesh):

time: 292 us -> 238 us (0.82)
  waiting for transfers between devices: 207 us -> 145 us
  other arithmetic: 25.9 us -> 31.9 us
  matrix products: 19.6 us -> 16.4 us
  starting transfers between devices: 20.3 us -> 23.5 us
  local copies, waits for them, and re-layouts: 3 us -> 6.08 us
    reduce_scatter x1, waiting for transfers between devices: 95.6 us -> 44.7 us  [shards(): lax.psum_scatter(chip_terms, 'fsdp', scatter_dimension=0, tiled=True)]
    all_gather x1, waiting for transfers between devices: 65 us -> 50.4 us  [shards(): gathered = lax.all_gather(out_weight, 'fsdp', axis=0, tiled=True)]
    ppermute x0 -> x2, waiting for transfers between devices: none -> 8.12 us  [sibling(): return lax.ppermute(x, 'dp', [(i, i ^ 1) for i in range(size)])]
    ppermute x0 -> x2, starting transfers between devices: none -> 7.67 us  [sibling(): return lax.ppermute(x, 'dp', [(i, i ^ 1) for i in range(size)])]
    add x1, other arithmetic: 4.04 us -> 10.3 us  [shards(): grad_hidden + conv_kernel[k] * (back_views[count - 1 - k] * taps[count -...]
    ppermute x8 -> x11, waiting for transfers between devices: 46.1 us -> 41.4 us  [butterfly(): x = x + lax.ppermute(x, axis, pairs)]
    ppermute x8 -> x11, starting transfers between devices: 20.2 us -> 15.8 us  [butterfly(): x = x + lax.ppermute(x, axis, pairs)]
  transfers between devices with their start and end apart: 10 -> 15, of which waited for: 10 -> 14; matrix products, arithmetic and copies ran while one was open for 15% -> 22% of each run, Pallas kernels for 0% -> 0%
where the time goes in v2:
time: 238 us
  waiting for transfers between devices  145 us (61%)
  other arithmetic  31.9 us (13%)
  starting transfers between devices  23.5 us (10%)
  matrix products  16.4 us (7%)
  between operations  14.3 us (6%)
  local copies, waits for them, and re-layouts  6.08 us (3%)
    all_gather x1, waiting for transfers between devices, shards(): gathered = lax.all_gather(out_weight, 'fsdp', axis=0, tiled=True)  50.4 us
    reduce_scatter x1, waiting for transfers between devices, shards(): lax.psum_scatter(chip_terms, 'fsdp', scatter_dimension=0, tiled=True)  44.7 us
    ppermute x11, waiting for transfers between devices, butterfly(): x = x + lax.ppermute(x, axis, pairs)  41.4 us
    ppermute x11, starting transfers between devices, butterfly(): x = x + lax.ppermute(x, axis, pairs)  15.8 us
    add x1, other arithmetic, shards(): grad_hidden + conv_kernel[k] * (back_views[count - 1 - k] * taps[count -...  10.3 us
    reduce_sum x1, other arithmetic, shards(): centred = mixed - jnp.mean(mixed, axis=-1, keepdims=True)  8.56 us
    ppermute x2, waiting for transfers between devices, sibling(): return lax.ppermute(x, 'dp', [(i, i ^ 1) for i in range(size)])  8.12 us
    ppermute x2, starting transfers between devices, sibling(): return lax.ppermute(x, 'dp', [(i, i ^ 1) for i in range(size)])  7.67 us
  transfers between devices with their start and end apart: 15, of which 14 were waited for; matrix products, arithmetic and copies ran while one was open for 22% of the time, Pallas kernels for 0%

profile of v2, /device:TPU:1, one launch (start us, length us, event | category | flops | bytes accessed | tf_op | source)
XLA Modules:
  0.0 237.5 jit_solution(8009228557749847809)
XLA Ops:
  10.8 1.1 slice_reduce_fusion.4
  12.0 8.6 %fusion.26 = (f32[512]{0:T(512)S(1)}, f32[512,1536]{1,0:T(8,128)S(1)}) fusion(f32[512]{0:T(512)S(1)} %get-tuple-element.36, f32[1536]{0:T(1024)S(1)} %get-tuple-element.26, f32[512]{0:T(512)S(1)} %get-tuple-element.34, f32[1536]{0:T(1024)S(1)} %get-tuple-element.27, f32[512]{0:T(512)S(1)} %and_convert_fusion.2, bf16[512,1536]{1,0:T(8,128)(2,1)} %param.6, ...), kind=kLoop, calls=%fused_computation.80 | loop fusion | flops 15728128 | bytes 4761600 | tf_op jit(solution)/shard_map/reduce_sum | solution.py:60
  21.0 1.2 copy-done.1
  22.2 1.2 multiply_convert_fusion
  23.4 1.6 copy.12
  25.0 1.5 constant_dynamic-slice_fusion.1
  26.5 1.4 fusion.28
  27.9 3.3 %collective-permute-start = (f32[768,1536]{1,0:T(8,128)S(1)}, f32[768,1536]{1,0:T(8,128)S(1)}, u32[]{:S(2)}, u32[]{:S(2)}) collective-permute-start(f32[768,1536]{1,0:T(8,128)S(1)} %fusion.28), channel_id=1, source_target_pairs={{0,16},{16,0},{32,48},{48,32},{64,80},{80,64},{96,112},{112,96},{1... | collective-permute-start | bytes 14155784 | tf_op jit(solution)/shard_map/ppermute | solution.py:40
  31.3 7.5 %collective-permute-done = f32[768,1536]{1,0:T(8,128)S(1)} collective-permute-done((f32[768,1536]{1,0:T(8,128)S(1)}, f32[768,1536]{1,0:T(8,128)S(1)}, u32[]{:S(2)}, u32[]{:S(2)}) %collective-permute-start) | collective-permute-done | bytes 4718624 | tf_op jit(solution)/shard_map/ppermute | solution.py:40
  38.8 3.6 %convolution_add_fusion = f32[768,1536]{1,0:T(8,128)} fusion(f32[768,1536]{1,0:T(8,128)S(1)} %collective-permute-done, bf16[512,768]{0,1:T(8,128)(2,1)S(1)} %bitcast.21, bf16[512,1536]{1,0:T(8,128)(2,1)S(1)} %copy-done), kind=kOutput, calls=%fused_computation | convolution fusion | flops 1209139200 | bytes 11796480 | tf_op jit(solution)/shard_map/dot_general | solution.py:70
  42.3 50.4 %all-gather.2.cloned.1.call-done = bf16[1536,1536]{1,0:T(8,128)(2,1)} async-done(((bf16[96,1536]{1,0:T(8,128)(2,1)}), bf16[1536,1536]{1,0:T(8,128)(2,1)}) %all-gather.2.cloned.1.call-update) | async-done | bytes 4718608 | tf_op jit(solution)/shard_map/all_gather | solution.py:53
  92.8 7.2 %multiply_reduce_fusion = (f32[1536]{0:T(1024)S(1)}, f32[512]{0:T(512)S(1)}, f32[512]{0:T(512)S(1)}, f32[512,1536]{1,0:T(8,128)S(1)}) fusion(f32[512,1536]{1,0:T(8,128)} %copy-done.1, f32[512]{0:T(512)S(1)} %add_rsqrt_fusion, f32[512]{0:T(512)S(1)} %broadcast_multiply_fusion.2, f32[1536]{0:T(1024)S(1)} %copy-done.4, f32[512]{0:T(512)S(1)} %and_convert_fusion.2, ...), kind=kOutput, calls=%fused_computation.29 | convolution fusion | flops 2430072320 | bytes 12605440 | tf_op jit(solution)/shard_map/dot_general | solution.py:77
  100.0 5.8 %fusion.16 = (f32[1536]{0:T(1024)S(1)}, f32[1536]{0:T(1024)S(1)}, f32[1536]{0:T(1024)S(1)}, f32[1536]{0:T(1024)S(1)}, f32[1536]{0:T(1024)S(1)}, /*index=5*/f32[512,1536]{1,0:T(8,128)}) fusion(f32[512]{0:T(512)S(1)} %get-tuple-element.36, bf16[512,1536]{1,0:T(8,128)(2,1)S(1)} %copy-done.3, f32[512]{0:T(512)S(1)} %get-tuple-element.34, ...), kind=kLoop, calls=%fused_computation.28 | loop fusion | flops 21225984 | bytes 11065344 | tf_op jit(solution)/shard_map/reduce_sum | solution.py:91
  105.9 6.0 %collective-permute-start.1 = (f32[6,1536]{1,0:T(8,128)S(1)}, f32[6,1536]{1,0:T(8,128)S(1)}, u32[]{:S(2)}, u32[]{:S(2)}) collective-permute-start(f32[6,1536]{1,0:T(8,128)S(1)} %concatenate.9), channel_id=1, source_target_pairs={{0,1},{1,0},{2,3},{3,2},{4,5},{5,4},{6,7},{7,6},{8,9},{9,8},{10,11... | collective-permute-start | bytes 110600 | tf_op jit(solution)/shard_map/ppermute | solution.py:34
  111.9 5.1 %collective-permute-done.1 = f32[6,1536]{1,0:T(8,128)S(1)} collective-permute-done((f32[6,1536]{1,0:T(8,128)S(1)}, f32[6,1536]{1,0:T(8,128)S(1)}, u32[]{:S(2)}, u32[]{:S(2)}) %collective-permute-start.1) | collective-permute-done | bytes 36896 | tf_op jit(solution)/shard_map/ppermute | solution.py:34
  117.1 10.7 %collective-permute-done.2 = f32[6,1536]{1,0:T(8,128)S(1)} collective-permute-done((f32[6,1536]{1,0:T(8,128)S(1)}, f32[6,1536]{1,0:T(8,128)S(1)}, u32[]{:S(2)}, u32[]{:S(2)}) %collective-permute-start.2) | collective-permute-done | bytes 36896 | tf_op jit(solution)/shard_map/ppermute | solution.py:34
  128.1 4.1 %collective-permute-done.3 = f32[6,1536]{1,0:T(8,128)S(1)} collective-permute-done((f32[6,1536]{1,0:T(8,128)S(1)}, f32[6,1536]{1,0:T(8,128)S(1)}, u32[]{:S(2)}, u32[]{:S(2)}) %collective-permute-start.3) | collective-permute-done | bytes 36896 | tf_op jit(solution)/shard_map/ppermute | solution.py:34
  132.3 4.4 %collective-permute-done.4 = f32[6,1536]{1,0:T(8,128)S(1)} collective-permute-done((f32[6,1536]{1,0:T(8,128)S(1)}, f32[6,1536]{1,0:T(8,128)S(1)}, u32[]{:S(2)}, u32[]{:S(2)}) %collective-permute-start.4) | collective-permute-done | bytes 36896 | tf_op jit(solution)/shard_map/ppermute | solution.py:34
  136.8 3.4 %collective-permute-start.5 = (f32[6,1536]{1,0:T(8,128)S(1)}, f32[6,1536]{1,0:T(8,128)S(1)}, u32[]{:S(2)}, u32[]{:S(2)}) collective-permute-start(f32[6,1536]{1,0:T(8,128)S(1)} %add.116), channel_id=1, source_target_pairs={{0,16},{16,0},{32,48},{48,32},{64,80},{80,64},{96,112},{112,96},{1... | collective-permute-start | bytes 110600 | tf_op jit(solution)/shard_map/ppermute | solution.py:34
  140.2 0.9 collective-permute-done.5
  141.2 2.8 %collective-permute-done.6 = f32[6,1536]{1,0:T(8,128)S(1)} collective-permute-done((f32[6,1536]{1,0:T(8,128)S(1)}, f32[6,1536]{1,0:T(8,128)S(1)}, u32[]{:S(2)}, u32[]{:S(2)}) %collective-permute-start.6) | collective-permute-done | bytes 36896 | tf_op jit(solution)/shard_map/ppermute | solution.py:34
  144.0 2.2 collective-permute-start.7
  146.2 2.7 %collective-permute-done.7 = f32[6,1536]{1,0:T(8,128)S(1)} collective-permute-done((f32[6,1536]{1,0:T(8,128)S(1)}, f32[6,1536]{1,0:T(8,128)S(1)}, u32[]{:S(2)}, u32[]{:S(2)}) %collective-permute-start.7) | collective-permute-done | bytes 36896 | tf_op jit(solution)/shard_map/ppermute | solution.py:34
  149.0 4.1 %collective-permute-done.8 = f32[6,1536]{1,0:T(8,128)S(1)} collective-permute-done((f32[6,1536]{1,0:T(8,128)S(1)}, f32[6,1536]{1,0:T(8,128)S(1)}, u32[]{:S(2)}, u32[]{:S(2)}) %collective-permute-start.8) | collective-permute-done | bytes 36896 | tf_op jit(solution)/shard_map/ppermute | solution.py:34
  153.2 44.7 %reduce-scatter.2.cloned.1.call-done = f32[48,1536]{1,0:T(8,128)} async-done(((f32[768,1536]{1,0:T(8,128)}), f32[48,1536]{1,0:T(8,128)}) %reduce-scatter.2.cloned.1.call-update) | async-done | bytes 294928 | tf_op jit(solution)/shard_map/reduce_scatter | solution.py:74
  197.9 1.2 collective-permute-start.9
  199.2 5.9 %collective-permute-done.9 = f32[48,1536]{1,0:T(8,128)S(1)} collective-permute-done((f32[48,1536]{1,0:T(8,128)}, f32[48,1536]{1,0:T(8,128)S(1)}, u32[]{:S(2)}, u32[]{:S(2)}) %collective-permute-start.9) | collective-permute-done | bytes 294944 | tf_op jit(solution)/shard_map/ppermute | solution.py:34
  205.1 1.0 add.121
  206.1 2.1 collective-permute-start.10
  208.2 10.3 %multiply_add_fusion = f32[512,1536]{1,0:T(8,128)} fusion(f32[512,1536]{1,0:T(8,128)} %get-tuple-element.28, f32[512]{0:T(512)S(1)} %get-tuple-element.36, f32[1536]{0:T(1024)S(1)} %get-tuple-element.26, f32[512]{0:T(512)S(1)} %get-tuple-element.34, f32[1536]{0:T(1024)S(1)} %get-tuple-element.27, f32[512]{0:T(512)S(1)} %and_convert_fusion.2, ...), kind=kLoop, calls=%fused_computation.30 | loop fusion | flops 11010048 | bytes 6332416 | tf_op jit(solution)/shard_map/add | solution.py:95
  218.7 4.3 %fusion.29 = f32[512,1536]{1,0:T(8,128)} fusion(bf16[512,1536]{1,0:T(8,128)(2,1)S(1)} %multiply_convert_fusion, bf16[1536,1536]{1,0:T(8,128)(2,1)S(1)} %copy-done.5), kind=kOutput, calls=%fused_computation.82 | convolution fusion | flops 2415919104 | bytes 9437184 | tf_op jit(solution)/shard_map/dot_general | solution.py:76
  224.3 4.3 %collective-permute-start.12 = (f32[48,1536]{1,0:T(8,128)S(1)}, f32[48,1536]{1,0:T(8,128)S(1)}, u32[]{:S(2)}, u32[]{:S(2)}) collective-permute-start(f32[48,1536]{1,0:T(8,128)S(1)} %add.123), channel_id=1, source_target_pairs={{0,16},{16,0},{32,48},{48,32},{64,80},{80,64},{96,112},{112,96},{1... | collective-permute-start | bytes 884744 | tf_op jit(solution)/shard_map/ppermute | solution.py:40
  (54 shorter events, 8.5 us)
Async XLA Ops:
  7.2 19.4 %copy-start = (bf16[512,1536]{1,0:T(8,128)(2,1)S(1)}, bf16[512,1536]{1,0:T(8,128)(2,1)}, u32[]{:S(2)}) copy-start(bf16[512,1536]{1,0:T(8,128)(2,1)} %param.7) | copy-start | bytes 4718596
  7.2 85.5 %all-gather.2.cloned.1.call-start = ((), (), s32[]{:S(2)}) async-start(), calls=%async_computation.1 | async-start | bytes 5013504 | tf_op jit(solution)/shard_map/all_gather | solution.py:53
  7.9 190.0 %reduce-scatter.2.cloned.1.call-start = ((), (), s32[]{:S(2)}) async-start(), calls=%async_computation.2 | async-start | bytes 5013504 | tf_op jit(solution)/shard_map/reduce_scatter | solution.py:74
  12.0 10.2 %copy-start.4 = (f32[1536]{0:T(1024)S(1)}, f32[1536]{0:T(1024)}, u32[]{:S(2)}) copy-start(f32[1536]{0:T(1024)} %param.10) | copy-start | bytes 18436
  20.5 1.7 copy-start.1
  27.9 10.9 %collective-permute-start = (f32[768,1536]{1,0:T(8,128)S(1)}, f32[768,1536]{1,0:T(8,128)S(1)}, u32[]{:S(2)}, u32[]{:S(2)}) collective-permute-start(f32[768,1536]{1,0:T(8,128)S(1)} %fusion.28), channel_id=1, source_target_pairs={{0,16},{16,0},{32,48},{48,32},{64,80},{80,64},{96,112},{112,96},{1... | collective-permute-start | bytes 14155784 | tf_op jit(solution)/shard_map/ppermute | solution.py:40
  92.7 7.2 %copy-start.2 = (f32[512,1536]{1,0:T(8,128)S(1)}, f32[512,1536]{1,0:T(8,128)}, u32[]{:S(2)}) copy-start(f32[512,1536]{1,0:T(8,128)} %copy-done.1) | copy-start | bytes 9437188
  92.8 7.2 %copy-start.3 = (bf16[512,1536]{1,0:T(8,128)(2,1)S(1)}, bf16[512,1536]{1,0:T(8,128)(2,1)}, u32[]{:S(2)}) copy-start(bf16[512,1536]{1,0:T(8,128)(2,1)} %param.6) | copy-start | bytes 4718596
  105.9 11.1 %collective-permute-start.1 = (f32[6,1536]{1,0:T(8,128)S(1)}, f32[6,1536]{1,0:T(8,128)S(1)}, u32[]{:S(2)}, u32[]{:S(2)}) collective-permute-start(f32[6,1536]{1,0:T(8,128)S(1)} %concatenate.9), channel_id=1, source_target_pairs={{0,1},{1,0},{2,3},{3,2},{4,5},{5,4},{6,7},{7,6},{8,9},{9,8},{10,11... | collective-permute-start | bytes 110600 | tf_op jit(solution)/shard_map/ppermute | solution.py:34
  117.0 10.8 %collective-permute-start.2 = (f32[6,1536]{1,0:T(8,128)S(1)}, f32[6,1536]{1,0:T(8,128)S(1)}, u32[]{:S(2)}, u32[]{:S(2)}) collective-permute-start(f32[6,1536]{1,0:T(8,128)S(1)} %add.113), channel_id=1, source_target_pairs={{0,2},{1,3},{2,0},{3,1},{4,6},{5,7},{6,4},{7,5},{8,10},{9,11},{10,... | collective-permute-start | bytes 110600 | tf_op jit(solution)/shard_map/ppermute | solution.py:34
  127.8 4.4 %collective-permute-start.3 = (f32[6,1536]{1,0:T(8,128)S(1)}, f32[6,1536]{1,0:T(8,128)S(1)}, u32[]{:S(2)}, u32[]{:S(2)}) collective-permute-start(f32[6,1536]{1,0:T(8,128)S(1)} %add.114), channel_id=1, source_target_pairs={{0,4},{1,5},{2,6},{3,7},{4,0},{5,1},{6,2},{7,3},{8,12},{9,13},{10,... | collective-permute-start | bytes 110600 | tf_op jit(solution)/shard_map/ppermute | solution.py:34
  132.2 4.5 %collective-permute-start.4 = (f32[6,1536]{1,0:T(8,128)S(1)}, f32[6,1536]{1,0:T(8,128)S(1)}, u32[]{:S(2)}, u32[]{:S(2)}) collective-permute-start(f32[6,1536]{1,0:T(8,128)S(1)} %add.115), channel_id=1, source_target_pairs={{0,8},{1,9},{2,10},{3,11},{4,12},{5,13},{6,14},{7,15},{8,0},{9,1},... | collective-permute-start | bytes 110600 | tf_op jit(solution)/shard_map/ppermute | solution.py:34
  136.8 4.3 %collective-permute-start.5 = (f32[6,1536]{1,0:T(8,128)S(1)}, f32[6,1536]{1,0:T(8,128)S(1)}, u32[]{:S(2)}, u32[]{:S(2)}) collective-permute-start(f32[6,1536]{1,0:T(8,128)S(1)} %add.116), channel_id=1, source_target_pairs={{0,16},{16,0},{32,48},{48,32},{64,80},{80,64},{96,112},{112,96},{1... | collective-permute-start | bytes 110600 | tf_op jit(solution)/shard_map/ppermute | solution.py:34
  141.0 2.9 %collective-permute-start.6 = (f32[6,1536]{1,0:T(8,128)S(1)}, f32[6,1536]{1,0:T(8,128)S(1)}, u32[]{:S(2)}, u32[]{:S(2)}) collective-permute-start(f32[6,1536]{1,0:T(8,128)S(1)} %add.117), channel_id=1, source_target_pairs={{0,32},{16,48},{32,0},{48,16},{64,96},{80,112},{96,64},{112,80},{1... | collective-permute-start | bytes 110600 | tf_op jit(solution)/shard_map/ppermute | solution.py:34
  144.0 4.9 %collective-permute-start.7 = (f32[6,1536]{1,0:T(8,128)S(1)}, f32[6,1536]{1,0:T(8,128)S(1)}, u32[]{:S(2)}, u32[]{:S(2)}) collective-permute-start(f32[6,1536]{1,0:T(8,128)S(1)} %add.118), channel_id=1, source_target_pairs={{0,64},{16,80},{32,96},{48,112},{64,0},{80,16},{96,32},{112,48},{1... | collective-permute-start | bytes 110600 | tf_op jit(solution)/shard_map/ppermute | solution.py:34
  148.9 4.2 %collective-permute-start.8 = (f32[6,1536]{1,0:T(8,128)S(1)}, f32[6,1536]{1,0:T(8,128)S(1)}, u32[]{:S(2)}, u32[]{:S(2)}) collective-permute-start(f32[6,1536]{1,0:T(8,128)S(1)} %add.119), channel_id=1, source_target_pairs={{0,128},{16,144},{32,160},{48,176},{64,192},{80,208},{96,224},{112... | collective-permute-start | bytes 110600 | tf_op jit(solution)/shard_map/ppermute | solution.py:34
  197.9 7.2 %collective-permute-start.9 = (f32[48,1536]{1,0:T(8,128)}, f32[48,1536]{1,0:T(8,128)S(1)}, u32[]{:S(2)}, u32[]{:S(2)}) collective-permute-start(f32[48,1536]{1,0:T(8,128)} %reduce-scatter.2.cloned.1.call-done), channel_id=1, source_target_pairs={{0,32},{16,48},{32,0},{48,16},{64,96},{80,112},{96,64},{112,80},{1... | collective-permute-start | bytes 884744 | tf_op jit(solution)/shard_map/ppermute | solution.py:34
  206.1 12.4 %collective-permute-start.10 = (f32[48,1536]{1,0:T(8,128)S(1)}, f32[48,1536]{1,0:T(8,128)S(1)}, u32[]{:S(2)}, u32[]{:S(2)}) collective-permute-start(f32[48,1536]{1,0:T(8,128)S(1)} %add.121), channel_id=1, source_target_pairs={{0,64},{16,80},{32,96},{48,112},{64,0},{80,16},{96,32},{112,48},{1... | collective-permute-start | bytes 884744 | tf_op jit(solution)/shard_map/ppermute | solution.py:34
  208.2 10.5 %copy-start.5 = (bf16[1536,1536]{1,0:T(8,128)(2,1)S(1)}, bf16[1536,1536]{1,0:T(8,128)(2,1)}, u32[]{:S(2)}) copy-start(bf16[1536,1536]{1,0:T(8,128)(2,1)} %all-gather.2.cloned.1.call-done) | copy-start | bytes 14155780
  218.6 5.7 %collective-permute-start.11 = (f32[48,1536]{1,0:T(8,128)S(1)}, f32[48,1536]{1,0:T(8,128)S(1)}, u32[]{:S(2)}, u32[]{:S(2)}) collective-permute-start(f32[48,1536]{1,0:T(8,128)S(1)} %add.122), channel_id=1, source_target_pairs={{0,128},{16,144},{32,160},{48,176},{64,192},{80,208},{96,224},{112... | collective-permute-start | bytes 884744 | tf_op jit(solution)/shard_map/ppermute | solution.py:34
  224.3 5.5 %collective-permute-start.12 = (f32[48,1536]{1,0:T(8,128)S(1)}, f32[48,1536]{1,0:T(8,128)S(1)}, u32[]{:S(2)}, u32[]{:S(2)}) collective-permute-start(f32[48,1536]{1,0:T(8,128)S(1)} %add.123), channel_id=1, source_target_pairs={{0,16},{16,0},{32,48},{48,32},{64,80},{80,64},{96,112},{112,96},{1... | collective-permute-start | bytes 884744 | tf_op jit(solution)/shard_map/ppermute | solution.py:40
Sparse Core Ops, SparseCore 0:
  10.5 82.2 all-gather.1
  96.3 101.5 reduce-scatter.1

commit v3 on v2

--- a/solution.py
+++ b/solution.py
@@ -98,7 +98,9 @@
     small = jnp.concatenate([jnp.stack(kernel_rows), gain_grad[None]], axis=0)
     small = butterfly(small, "fsdp", (1, 2, 4, 8))
     small = butterfly(small, "dp", (1, 2, 4, 8))
-    shard_sum, small = lax.optimization_barrier((shard_sum, small))
+    shard_sum, small, output, grad_hidden = lax.optimization_barrier(
+        (shard_sum, small, output, grad_hidden)
+    )
     half_sum = butterfly(shard_sum, "dp", (2, 4, 8))
     other_sum = sibling(half_sum)
     weight_sum = jnp.where(

time: 238 us -> 235 us (0.987)
  waiting for transfers between devices: 145 us -> 128 us
  starting transfers between devices: 23.5 us -> 38 us
    ppermute x11, starting transfers between devices: 15.8 us -> 30.2 us  [butterfly(): x = x + lax.ppermute(x, axis, pairs)]
    ppermute x11, waiting for transfers between devices: 41.4 us -> 29.9 us  [butterfly(): x = x + lax.ppermute(x, axis, pairs)]
    reduce_scatter x1, waiting for transfers between devices: 44.7 us -> 38.9 us  [shards(): lax.psum_scatter(chip_terms, 'fsdp', scatter_dimension=0, tiled=True)]
  transfers between devices with their start and end apart: 15 -> 15, of which waited for: 14 -> 13; matrix products, arithmetic and copies ran while one was open for 22% -> 22% of each run, Pallas kernels for 0% -> 0%
where the time goes in v3:
time: 235 us; the launch traced here: 234 us
  waiting for transfers between devices  128 us (54%)
  starting transfers between devices  38 us (16%)
  other arithmetic  31.6 us (13%)
  matrix products  16.4 us (7%)
  between operations  14.3 us (6%)
  local copies, waits for them, and re-layouts  6.08 us (3%)
    all_gather x1, waiting for transfers between devices, shards(): gathered = lax.all_gather(out_weight, 'fsdp', axis=0, tiled=True)  50.4 us
    reduce_scatter x1, waiting for transfers between devices, shards(): lax.psum_scatter(chip_terms, 'fsdp', scatter_dimension=0, tiled=True)  38.9 us
    ppermute x11, starting transfers between devices, butterfly(): x = x + lax.ppermute(x, axis, pairs)  30.2 us
    ppermute x11, waiting for transfers between devices, butterfly(): x = x + lax.ppermute(x, axis, pairs)  29.9 us
    add x1, other arithmetic, shards(): grad_hidden + conv_kernel[k] * (back_views[count - 1 - k] * taps[count -...  10.3 us
    reduce_sum x1, other arithmetic, shards(): centred = mixed - jnp.mean(mixed, axis=-1, keepdims=True)  8.56 us
    ppermute x2, waiting for transfers between devices, sibling(): return lax.ppermute(x, 'dp', [(i, i ^ 1) for i in range(size)])  8.12 us
    ppermute x2, starting transfers between devices, sibling(): return lax.ppermute(x, 'dp', [(i, i ^ 1) for i in range(size)])  7.65 us
  transfers between devices with their start and end apart: 15, of which 13 were waited for; matrix products, arithmetic and copies ran while one was open for 22% of the time, Pallas kernels for 0%

profile of v3, /device:TPU:1, one launch (start us, length us, event | category | flops | bytes accessed | tf_op | source)
XLA Modules:
  0.0 234.3 jit_solution(16830589339130680729)
XLA Ops:
  12.0 8.6 %fusion.26 = (f32[512]{0:T(512)S(1)}, f32[512,1536]{1,0:T(8,128)S(1)}) fusion(f32[512]{0:T(512)S(1)} %get-tuple-element.40, f32[1536]{0:T(1024)S(1)} %get-tuple-element.30, f32[512]{0:T(512)S(1)} %get-tuple-element.38, f32[1536]{0:T(1024)S(1)} %get-tuple-element.31, f32[512]{0:T(512)S(1)} %and_convert_fusion.2, bf16[512,1536]{1,0:T(8,128)(2,1)} %param.6, ...), kind=kLoop, calls=%fused_computation.80 | loop fusion | flops 15728128 | bytes 4761600 | tf_op jit(solution)/shard_map/reduce_sum | solution.py:60
  21.0 1.2 copy-done.1
  22.2 1.2 multiply_convert_fusion
  23.4 1.6 copy.12
  25.0 1.5 constant_dynamic-slice_fusion.1
  26.5 1.4 fusion.28
  27.9 3.3 %collective-permute-start = (f32[768,1536]{1,0:T(8,128)S(1)}, f32[768,1536]{1,0:T(8,128)S(1)}, u32[]{:S(2)}, u32[]{:S(2)}) collective-permute-start(f32[768,1536]{1,0:T(8,128)S(1)} %fusion.28), channel_id=1, source_target_pairs={{0,16},{16,0},{32,48},{48,32},{64,80},{80,64},{96,112},{112,96},{1... | collective-permute-start | bytes 14155784 | tf_op jit(solution)/shard_map/ppermute | solution.py:40
  31.3 7.5 %collective-permute-done = f32[768,1536]{1,0:T(8,128)S(1)} collective-permute-done((f32[768,1536]{1,0:T(8,128)S(1)}, f32[768,1536]{1,0:T(8,128)S(1)}, u32[]{:S(2)}, u32[]{:S(2)}) %collective-permute-start) | collective-permute-done | bytes 4718624 | tf_op jit(solution)/shard_map/ppermute | solution.py:40
  38.8 3.6 %convolution_add_fusion = f32[768,1536]{1,0:T(8,128)} fusion(f32[768,1536]{1,0:T(8,128)S(1)} %collective-permute-done, bf16[512,768]{0,1:T(8,128)(2,1)S(1)} %bitcast.21, bf16[512,1536]{1,0:T(8,128)(2,1)S(1)} %copy-done), kind=kOutput, calls=%fused_computation | convolution fusion | flops 1209139200 | bytes 11796480 | tf_op jit(solution)/shard_map/dot_general | solution.py:70
  42.3 50.4 %all-gather.2.cloned.1.call-done = bf16[1536,1536]{1,0:T(8,128)(2,1)} async-done(((bf16[96,1536]{1,0:T(8,128)(2,1)}), bf16[1536,1536]{1,0:T(8,128)(2,1)}) %all-gather.2.cloned.1.call-update) | async-done | bytes 4718608 | tf_op jit(solution)/shard_map/all_gather | solution.py:53
  92.8 7.2 %multiply_reduce_fusion = (f32[1536]{0:T(1024)S(1)}, f32[512]{0:T(512)S(1)}, f32[512]{0:T(512)S(1)}, f32[512,1536]{1,0:T(8,128)S(1)}) fusion(f32[512,1536]{1,0:T(8,128)} %copy-done.1, f32[512]{0:T(512)S(1)} %add_rsqrt_fusion, f32[512]{0:T(512)S(1)} %broadcast_multiply_fusion.2, f32[1536]{0:T(1024)S(1)} %copy-done.4, f32[512]{0:T(512)S(1)} %and_convert_fusion.2, ...), kind=kOutput, calls=%fused_computation.30 | convolution fusion | flops 2430072320 | bytes 12605440 | tf_op jit(solution)/shard_map/dot_general | solution.py:77
  100.0 5.5 %fusion.16 = (f32[1536]{0:T(1024)S(1)}, f32[1536]{0:T(1024)S(1)}, f32[1536]{0:T(1024)S(1)}, f32[1536]{0:T(1024)S(1)}, f32[1536]{0:T(1024)S(1)}, /*index=5*/f32[512,1536]{1,0:T(8,128)}) fusion(f32[512]{0:T(512)S(1)} %get-tuple-element.40, bf16[512,1536]{1,0:T(8,128)(2,1)S(1)} %copy-done.3, f32[512]{0:T(512)S(1)} %get-tuple-element.38, ...), kind=kLoop, calls=%fused_computation.28 | loop fusion | flops 21225984 | bytes 11065344 | tf_op jit(solution)/shard_map/reduce_sum | solution.py:91
  105.6 6.0 %collective-permute-start.1 = (f32[6,1536]{1,0:T(8,128)S(1)}, f32[6,1536]{1,0:T(8,128)S(1)}, u32[]{:S(2)}, u32[]{:S(2)}) collective-permute-start(f32[6,1536]{1,0:T(8,128)S(1)} %concatenate.9), channel_id=1, source_target_pairs={{0,1},{1,0},{2,3},{3,2},{4,5},{5,4},{6,7},{7,6},{8,9},{9,8},{10,11... | collective-permute-start | bytes 110600 | tf_op jit(solution)/shard_map/ppermute | solution.py:34
  111.6 1.6 collective-permute-done.1
  113.2 2.5 %collective-permute-start.2 = (f32[6,1536]{1,0:T(8,128)S(1)}, f32[6,1536]{1,0:T(8,128)S(1)}, u32[]{:S(2)}, u32[]{:S(2)}) collective-permute-start(f32[6,1536]{1,0:T(8,128)S(1)} %add.109), channel_id=1, source_target_pairs={{0,2},{1,3},{2,0},{3,1},{4,6},{5,7},{6,4},{7,5},{8,10},{9,11},{10,... | collective-permute-start | bytes 110600 | tf_op jit(solution)/shard_map/ppermute | solution.py:34
  115.7 4.5 %collective-permute-done.2 = f32[6,1536]{1,0:T(8,128)S(1)} collective-permute-done((f32[6,1536]{1,0:T(8,128)S(1)}, f32[6,1536]{1,0:T(8,128)S(1)}, u32[]{:S(2)}, u32[]{:S(2)}) %collective-permute-start.2) | collective-permute-done | bytes 36896 | tf_op jit(solution)/shard_map/ppermute | solution.py:34
  120.3 2.1 collective-permute-start.3
  122.3 2.2 collective-permute-done.3
  124.5 2.9 %collective-permute-start.4 = (f32[6,1536]{1,0:T(8,128)S(1)}, f32[6,1536]{1,0:T(8,128)S(1)}, u32[]{:S(2)}, u32[]{:S(2)}) collective-permute-start(f32[6,1536]{1,0:T(8,128)S(1)} %add.111), channel_id=1, source_target_pairs={{0,8},{1,9},{2,10},{3,11},{4,12},{5,13},{6,14},{7,15},{8,0},{9,1},... | collective-permute-start | bytes 110600 | tf_op jit(solution)/shard_map/ppermute | solution.py:34
  127.5 2.0 collective-permute-done.4
  129.5 8.9 %collective-permute-start.5 = (f32[6,1536]{1,0:T(8,128)S(1)}, f32[6,1536]{1,0:T(8,128)S(1)}, u32[]{:S(2)}, u32[]{:S(2)}) collective-permute-start(f32[6,1536]{1,0:T(8,128)S(1)} %add.112), channel_id=1, source_target_pairs={{0,16},{16,0},{32,48},{48,32},{64,80},{80,64},{96,112},{112,96},{1... | collective-permute-start | bytes 110600 | tf_op jit(solution)/shard_map/ppermute | solution.py:34
  139.2 1.2 collective-permute-start.6
  140.4 2.2 collective-permute-done.6
  142.6 2.7 %collective-permute-start.7 = (f32[6,1536]{1,0:T(8,128)S(1)}, f32[6,1536]{1,0:T(8,128)S(1)}, u32[]{:S(2)}, u32[]{:S(2)}) collective-permute-start(f32[6,1536]{1,0:T(8,128)S(1)} %add.114), channel_id=1, source_target_pairs={{0,64},{16,80},{32,96},{48,112},{64,0},{80,16},{96,32},{112,48},{1... | collective-permute-start | bytes 110600 | tf_op jit(solution)/shard_map/ppermute | solution.py:34
  145.3 10.3 %multiply_add_fusion = f32[512,1536]{1,0:T(8,128)} fusion(f32[512,1536]{1,0:T(8,128)} %get-tuple-element.32, f32[512]{0:T(512)S(1)} %get-tuple-element.40, f32[1536]{0:T(1024)S(1)} %get-tuple-element.30, f32[512]{0:T(512)S(1)} %get-tuple-element.38, f32[1536]{0:T(1024)S(1)} %get-tuple-element.31, f32[512]{0:T(512)S(1)} %and_convert_fusion.2, ...), kind=kLoop, calls=%fused_computation.29 | loop fusion | flops 11010048 | bytes 6332416 | tf_op jit(solution)/shard_map/add | solution.py:95
  155.8 4.3 %fusion.29 = f32[512,1536]{1,0:T(8,128)} fusion(bf16[512,1536]{1,0:T(8,128)(2,1)S(1)} %multiply_convert_fusion, bf16[1536,1536]{1,0:T(8,128)(2,1)S(1)} %copy-done.5), kind=kOutput, calls=%fused_computation.82 | convolution fusion | flops 2415919104 | bytes 9437184 | tf_op jit(solution)/shard_map/dot_general | solution.py:76
  160.1 38.9 %reduce-scatter.2.cloned.1.call-done = f32[48,1536]{1,0:T(8,128)} async-done(((f32[768,1536]{1,0:T(8,128)}), f32[48,1536]{1,0:T(8,128)}) %reduce-scatter.2.cloned.1.call-update) | async-done | bytes 294928 | tf_op jit(solution)/shard_map/reduce_scatter | solution.py:74
  200.1 6.3 %collective-permute-done.9 = f32[48,1536]{1,0:T(8,128)S(1)} collective-permute-done((f32[48,1536]{1,0:T(8,128)}, f32[48,1536]{1,0:T(8,128)S(1)}, u32[]{:S(2)}, u32[]{:S(2)}) %collective-permute-start.9) | collective-permute-done | bytes 294944 | tf_op jit(solution)/shard_map/ppermute | solution.py:34
  207.4 2.6 %collective-permute-start.10 = (f32[48,1536]{1,0:T(8,128)S(1)}, f32[48,1536]{1,0:T(8,128)S(1)}, u32[]{:S(2)}, u32[]{:S(2)}) collective-permute-start(f32[48,1536]{1,0:T(8,128)S(1)} %add.121), channel_id=1, source_target_pairs={{0,64},{16,80},{32,96},{48,112},{64,0},{80,16},{96,32},{112,48},{1... | collective-permute-start | bytes 884744 | tf_op jit(solution)/shard_map/ppermute | solution.py:34
  210.0 5.3 %collective-permute-done.10 = f32[48,1536]{1,0:T(8,128)S(1)} collective-permute-done((f32[48,1536]{1,0:T(8,128)S(1)}, f32[48,1536]{1,0:T(8,128)S(1)}, u32[]{:S(2)}, u32[]{:S(2)}) %collective-permute-start.10) | collective-permute-done | bytes 294944 | tf_op jit(solution)/shard_map/ppermute | solution.py:34
  216.1 4.9 %collective-permute-done.11 = f32[48,1536]{1,0:T(8,128)S(1)} collective-permute-done((f32[48,1536]{1,0:T(8,128)S(1)}, f32[48,1536]{1,0:T(8,128)S(1)}, u32[]{:S(2)}, u32[]{:S(2)}) %collective-permute-start.11) | collective-permute-done | bytes 294944 | tf_op jit(solution)/shard_map/ppermute | solution.py:34
  221.1 4.3 %collective-permute-start.12 = (f32[48,1536]{1,0:T(8,128)S(1)}, f32[48,1536]{1,0:T(8,128)S(1)}, u32[]{:S(2)}, u32[]{:S(2)}) collective-permute-start(f32[48,1536]{1,0:T(8,128)S(1)} %add.123), channel_id=1, source_target_pairs={{0,16},{16,0},{32,48},{48,32},{64,80},{80,64},{96,112},{112,96},{1... | collective-permute-start | bytes 884744 | tf_op jit(solution)/shard_map/ppermute | solution.py:40
  (54 shorter events, 11.3 us)
Async XLA Ops:
  7.2 19.4 %copy-start = (bf16[512,1536]{1,0:T(8,128)(2,1)S(1)}, bf16[512,1536]{1,0:T(8,128)(2,1)}, u32[]{:S(2)}) copy-start(bf16[512,1536]{1,0:T(8,128)(2,1)} %param.7) | copy-start | bytes 4718596
  7.2 85.5 %all-gather.2.cloned.1.call-start = ((), (), s32[]{:S(2)}) async-start(), calls=%async_computation.1 | async-start | bytes 5013504 | tf_op jit(solution)/shard_map/all_gather | solution.py:53
  7.9 191.1 %reduce-scatter.2.cloned.1.call-start = ((), (), s32[]{:S(2)}) async-start(), calls=%async_computation.2 | async-start | bytes 5013504 | tf_op jit(solution)/shard_map/reduce_scatter | solution.py:74
  12.0 10.2 %copy-start.4 = (f32[1536]{0:T(1024)S(1)}, f32[1536]{0:T(1024)}, u32[]{:S(2)}) copy-start(f32[1536]{0:T(1024)} %param.10) | copy-start | bytes 18436
  20.5 1.7 copy-start.1
  27.9 10.9 %collective-permute-start = (f32[768,1536]{1,0:T(8,128)S(1)}, f32[768,1536]{1,0:T(8,128)S(1)}, u32[]{:S(2)}, u32[]{:S(2)}) collective-permute-start(f32[768,1536]{1,0:T(8,128)S(1)} %fusion.28), channel_id=1, source_target_pairs={{0,16},{16,0},{32,48},{48,32},{64,80},{80,64},{96,112},{112,96},{1... | collective-permute-start | bytes 14155784 | tf_op jit(solution)/shard_map/ppermute | solution.py:40
  92.7 7.2 %copy-start.2 = (f32[512,1536]{1,0:T(8,128)S(1)}, f32[512,1536]{1,0:T(8,128)}, u32[]{:S(2)}) copy-start(f32[512,1536]{1,0:T(8,128)} %copy-done.1) | copy-start | bytes 9437188
  92.7 7.2 %copy-start.3 = (bf16[512,1536]{1,0:T(8,128)(2,1)S(1)}, bf16[512,1536]{1,0:T(8,128)(2,1)}, u32[]{:S(2)}) copy-start(bf16[512,1536]{1,0:T(8,128)(2,1)} %param.6) | copy-start | bytes 4718596
  105.6 7.6 %collective-permute-start.1 = (f32[6,1536]{1,0:T(8,128)S(1)}, f32[6,1536]{1,0:T(8,128)S(1)}, u32[]{:S(2)}, u32[]{:S(2)}) collective-permute-start(f32[6,1536]{1,0:T(8,128)S(1)} %concatenate.9), channel_id=1, source_target_pairs={{0,1},{1,0},{2,3},{3,2},{4,5},{5,4},{6,7},{7,6},{8,9},{9,8},{10,11... | collective-permute-start | bytes 110600 | tf_op jit(solution)/shard_map/ppermute | solution.py:34
  113.2 7.0 %collective-permute-start.2 = (f32[6,1536]{1,0:T(8,128)S(1)}, f32[6,1536]{1,0:T(8,128)S(1)}, u32[]{:S(2)}, u32[]{:S(2)}) collective-permute-start(f32[6,1536]{1,0:T(8,128)S(1)} %add.109), channel_id=1, source_target_pairs={{0,2},{1,3},{2,0},{3,1},{4,6},{5,7},{6,4},{7,5},{8,10},{9,11},{10,... | collective-permute-start | bytes 110600 | tf_op jit(solution)/shard_map/ppermute | solution.py:34
  120.3 4.3 %collective-permute-start.3 = (f32[6,1536]{1,0:T(8,128)S(1)}, f32[6,1536]{1,0:T(8,128)S(1)}, u32[]{:S(2)}, u32[]{:S(2)}) collective-permute-start(f32[6,1536]{1,0:T(8,128)S(1)} %add.110), channel_id=1, source_target_pairs={{0,4},{1,5},{2,6},{3,7},{4,0},{5,1},{6,2},{7,3},{8,12},{9,13},{10,... | collective-permute-start | bytes 110600 | tf_op jit(solution)/shard_map/ppermute | solution.py:34
  124.5 4.9 %collective-permute-start.4 = (f32[6,1536]{1,0:T(8,128)S(1)}, f32[6,1536]{1,0:T(8,128)S(1)}, u32[]{:S(2)}, u32[]{:S(2)}) collective-permute-start(f32[6,1536]{1,0:T(8,128)S(1)} %add.111), channel_id=1, source_target_pairs={{0,8},{1,9},{2,10},{3,11},{4,12},{5,13},{6,14},{7,15},{8,0},{9,1},... | collective-permute-start | bytes 110600 | tf_op jit(solution)/shard_map/ppermute | solution.py:34
  129.5 9.8 %collective-permute-start.5 = (f32[6,1536]{1,0:T(8,128)S(1)}, f32[6,1536]{1,0:T(8,128)S(1)}, u32[]{:S(2)}, u32[]{:S(2)}) collective-permute-start(f32[6,1536]{1,0:T(8,128)S(1)} %add.112), channel_id=1, source_target_pairs={{0,16},{16,0},{32,48},{48,32},{64,80},{80,64},{96,112},{112,96},{1... | collective-permute-start | bytes 110600 | tf_op jit(solution)/shard_map/ppermute | solution.py:34
  139.2 3.3 %collective-permute-start.6 = (f32[6,1536]{1,0:T(8,128)S(1)}, f32[6,1536]{1,0:T(8,128)S(1)}, u32[]{:S(2)}, u32[]{:S(2)}) collective-permute-start(f32[6,1536]{1,0:T(8,128)S(1)} %add.113), channel_id=1, source_target_pairs={{0,32},{16,48},{32,0},{48,16},{64,96},{80,112},{96,64},{112,80},{1... | collective-permute-start | bytes 110600 | tf_op jit(solution)/shard_map/ppermute | solution.py:34
  142.6 13.0 %collective-permute-start.7 = (f32[6,1536]{1,0:T(8,128)S(1)}, f32[6,1536]{1,0:T(8,128)S(1)}, u32[]{:S(2)}, u32[]{:S(2)}) collective-permute-start(f32[6,1536]{1,0:T(8,128)S(1)} %add.114), channel_id=1, source_target_pairs={{0,64},{16,80},{32,96},{48,112},{64,0},{80,16},{96,32},{112,48},{1... | collective-permute-start | bytes 110600 | tf_op jit(solution)/shard_map/ppermute | solution.py:34
  145.3 10.4 %copy-start.5 = (bf16[1536,1536]{1,0:T(8,128)(2,1)S(1)}, bf16[1536,1536]{1,0:T(8,128)(2,1)}, u32[]{:S(2)}) copy-start(bf16[1536,1536]{1,0:T(8,128)(2,1)} %all-gather.2.cloned.1.call-done) | copy-start | bytes 14155780
  155.7 4.4 %collective-permute-start.8 = (f32[6,1536]{1,0:T(8,128)S(1)}, f32[6,1536]{1,0:T(8,128)S(1)}, u32[]{:S(2)}, u32[]{:S(2)}) collective-permute-start(f32[6,1536]{1,0:T(8,128)S(1)} %add.115), channel_id=1, source_target_pairs={{0,128},{16,144},{32,160},{48,176},{64,192},{80,208},{96,224},{112... | collective-permute-start | bytes 110600 | tf_op jit(solution)/shard_map/ppermute | solution.py:34
  199.0 7.4 %collective-permute-start.9 = (f32[48,1536]{1,0:T(8,128)}, f32[48,1536]{1,0:T(8,128)S(1)}, u32[]{:S(2)}, u32[]{:S(2)}) collective-permute-start(f32[48,1536]{1,0:T(8,128)} %reduce-scatter.2.cloned.1.call-done), channel_id=1, source_target_pairs={{0,32},{16,48},{32,0},{48,16},{64,96},{80,112},{96,64},{112,80},{1... | collective-permute-start | bytes 884744 | tf_op jit(solution)/shard_map/ppermute | solution.py:34
  207.4 7.9 %collective-permute-start.10 = (f32[48,1536]{1,0:T(8,128)S(1)}, f32[48,1536]{1,0:T(8,128)S(1)}, u32[]{:S(2)}, u32[]{:S(2)}) collective-permute-start(f32[48,1536]{1,0:T(8,128)S(1)} %add.121), channel_id=1, source_target_pairs={{0,64},{16,80},{32,96},{48,112},{64,0},{80,16},{96,32},{112,48},{1... | collective-permute-start | bytes 884744 | tf_op jit(solution)/shard_map/ppermute | solution.py:34
  215.4 5.7 %collective-permute-start.11 = (f32[48,1536]{1,0:T(8,128)S(1)}, f32[48,1536]{1,0:T(8,128)S(1)}, u32[]{:S(2)}, u32[]{:S(2)}) collective-permute-start(f32[48,1536]{1,0:T(8,128)S(1)} %add.122), channel_id=1, source_target_pairs={{0,128},{16,144},{32,160},{48,176},{64,192},{80,208},{96,224},{112... | collective-permute-start | bytes 884744 | tf_op jit(solution)/shard_map/ppermute | solution.py:34
  221.1 5.5 %collective-permute-start.12 = (f32[48,1536]{1,0:T(8,128)S(1)}, f32[48,1536]{1,0:T(8,128)S(1)}, u32[]{:S(2)}, u32[]{:S(2)}) collective-permute-start(f32[48,1536]{1,0:T(8,128)S(1)} %add.123), channel_id=1, source_target_pairs={{0,16},{16,0},{32,48},{48,32},{64,80},{80,64},{96,112},{112,96},{1... | collective-permute-start | bytes 884744 | tf_op jit(solution)/shard_map/ppermute | solution.py:40
Sparse Core Ops, SparseCore 0:
  10.5 82.1 all-gather.1
  96.3 102.6 reduce-scatter.1

commit v4 on v3

--- a/solution.py
+++ b/solution.py
@@ -40,6 +40,27 @@
     return lax.ppermute(x, "dp", [(i, i ^ 1) for i in range(size)])
 
 
+def doubling_step(held, axis, mask):
+    size = lax.axis_size(axis)
+    upper = (lax.axis_index(axis) & mask) != 0
+    received = lax.ppermute(held, axis, [(i, i ^ mask) for i in range(size)])
+    return jnp.where(
+        upper,
+        jnp.concatenate([received, held], axis=0),
+        jnp.concatenate([held, received], axis=0),
+    )
+
+
+def doubling_order(held, masks):
+    count = len(masks)
+    bits = [int(math.log2(mask)) for mask in reversed(masks)]
+    rest = held.shape[1:]
+    held = held.reshape((2,) * count + rest)
+    order = sorted(range(count), key=lambda axis_at: -bits[axis_at])
+    held = jnp.transpose(held, order + [count + d for d in range(len(rest))])
+    return held.reshape((-1,) + rest[1:])
+
+
 def shards(hidden_in, grad_out, lengths, conv_kernel, norm_gain, out_weight):
     frames, chans = hidden_in.shape
     width = grad_out.shape[1]
@@ -50,13 +71,19 @@
     rows = out_weight.shape[0]
     half_rows = rows // 2
     core = lax.axis_index("dp") % 2
-    gathered = lax.all_gather(out_weight, "fsdp", axis=0, tiled=True)
+    masks = (2, 8, 1, 4)
+    own_half = lax.dynamic_slice_in_dim(out_weight, core * half_rows, half_rows, 0)
+    held = doubling_step(own_half[None], "fsdp", masks[0])
     taps = tap_mask(lengths[0], frames, count)
+    held, taps = lax.optimization_barrier((held, taps))
+    held = doubling_step(held, "fsdp", masks[1])
     live = taps[half_width][:, None]
     views = shifted(hidden_in, half_width)
     mixed = jnp.zeros((frames, chans), jnp.float32)
     for k in range(count):
         mixed = mixed + conv_kernel[k] * views[k].astype(jnp.float32) * taps[k][:, None]
+    held, mixed = lax.optimization_barrier((held, mixed))
+    held = doubling_step(held, "fsdp", masks[2])
     centred = mixed - jnp.mean(mixed, axis=-1, keepdims=True)
     inverse = lax.rsqrt(jnp.mean(centred * centred, axis=-1, keepdims=True) + 1e-05)
     normed = centred * inverse
@@ -69,10 +96,18 @@
     contract = (((0,), (0,)), ((), ()))
     keep_terms = lax.dot_general(keep_act, grad_out, contract, preferred_element_type=jnp.float32)
     send_terms = lax.dot_general(send_act, grad_out, contract, preferred_element_type=jnp.float32)
+    held, keep_terms, send_terms, activation = lax.optimization_barrier(
+        (held, keep_terms, send_terms, activation)
+    )
+    held = doubling_step(held, "fsdp", masks[3])
     chip_terms = keep_terms + sibling(send_terms)
-    gathered, chip_terms, activation = lax.optimization_barrier((gathered, chip_terms, activation))
     shard_sum = lax.psum_scatter(chip_terms, "fsdp", scatter_dimension=0, tiled=True)
-    full_weight = gathered
+    held, chip_terms = lax.optimization_barrier((held, chip_terms))
+    gathered = doubling_order(held, masks)
+    other = sibling(gathered)
+    first = jnp.where(core == 0, gathered, other).reshape(fsdp_count, 1, half_rows, width)
+    second = jnp.where(core == 0, other, gathered).reshape(fsdp_count, 1, half_rows, width)
+    full_weight = jnp.concatenate([first, second], axis=1).reshape(chans, width)
     output = jnp.dot(activation, full_weight, preferred_element_type=jnp.float32)
     grad_act = lax.dot_general(
         grad_out, full_weight, (((1,), (1,)), ((), ())), preferred_element_type=jnp.float32

time: 235 us -> 222 us (0.945)
  waiting for transfers between devices: 128 us -> 97.1 us
  other arithmetic: 31.6 us -> 48.5 us
  matrix products: 16.4 us -> 10.9 us
  local copies, waits for them, and re-layouts: 6.08 us -> 10.5 us
    all_gather x1 -> x0, waiting for transfers between devices: 50.4 us -> none  [shards(): gathered = lax.all_gather(out_weight, 'fsdp', axis=0, tiled=True)]
    ppermute x0 -> x4, waiting for transfers between devices: none -> 48.5 us  [doubling_step(): received = lax.ppermute(held, axis, [(i, i ^ mask) for i in range(size)])]
    reduce_scatter x1, waiting for transfers between devices: 38.9 us -> 0.02 us  [shards(): lax.psum_scatter(chip_terms, 'fsdp', scatter_dimension=0, tiled=True)]
    ppermute x0 -> x4, starting transfers between devices: none -> 15.4 us  [doubling_step(): received = lax.ppermute(held, axis, [(i, i ^ mask) for i in range(size)])]
    ppermute x11, starting transfers between devices: 30.2 us -> 16.8 us  [butterfly(): x = x + lax.ppermute(x, axis, pairs)]
    add x0 -> x2, other arithmetic: none -> 11.7 us  [the longest x1 8.63 us: shards(): mixed + conv_kernel[k] * views[k].astype(jnp.float32) * taps[k][:, None]]
    select_n x0 -> x5, other arithmetic: none -> 9.08 us  [the longest x4 6.35 us: doubling_step(): jnp.where(upper, jnp.concatenate([received, held], axis=0), jnp.concatena...]
    reduce_sum x1, other arithmetic: 8.56 us -> 2.11 us  [shards(): centred = mixed - jnp.mean(mixed, axis=-1, keepdims=True)]
  transfers between devices with their start and end apart: 15 -> 19, of which waited for: 13 -> 14; matrix products, arithmetic and copies ran while one was open for 22% -> 26% of each run, Pallas kernels for 0% -> 0%
where the time goes in v4:
time: 222 us
  waiting for transfers between devices  97.1 us (44%)
  other arithmetic  48.5 us (22%)
  starting transfers between devices  40.3 us (18%)
  between operations  14.3 us (6%)
  matrix products  10.9 us (5%)
  local copies, waits for them, and re-layouts  10.5 us (5%)
    ppermute x4, waiting for transfers between devices, doubling_step(): received = lax.ppermute(held, axis, [(i, i ^ mask) for i in range(size)])  48.5 us
    ppermute x11, waiting for transfers between devices, butterfly(): x = x + lax.ppermute(x, axis, pairs)  36 us
    ppermute x11, starting transfers between devices, butterfly(): x = x + lax.ppermute(x, axis, pairs)  16.8 us
    ppermute x4, starting transfers between devices, doubling_step(): received = lax.ppermute(held, axis, [(i, i ^ mask) for i in range(size)])  15.4 us
    ppermute x3, waiting for transfers between devices, sibling(): return lax.ppermute(x, 'dp', [(i, i ^ 1) for i in range(size)])  12.6 us
    add x1, other arithmetic, shards(): grad_hidden + conv_kernel[k] * (back_views[count - 1 - k] * taps[count -...  10.3 us
    add x1, other arithmetic, shards(): mixed + conv_kernel[k] * views[k].astype(jnp.float32) * taps[k][:, None]  8.63 us
    ppermute x3, starting transfers between devices, sibling(): return lax.ppermute(x, 'dp', [(i, i ^ 1) for i in range(size)])  8.01 us
  transfers between devices with their start and end apart: 19, of which 14 were waited for; matrix products, arithmetic and copies ran while one was open for 26% of the time, Pallas kernels for 0%

profile of v4, /device:TPU:1, one launch (start us, length us, event | category | flops | bytes accessed | tf_op | source)
XLA Modules:
  0.0 221.7 jit_solution(13216445042963701929)
XLA Ops:
  8.3 7.8 %collective-permute-start = (bf16[1,48,1536]{2,1,0:T(8,128)(2,1)S(1)}, bf16[1,48,1536]{2,1,0:T(8,128)(2,1)S(1)}, u32[]{:S(2)}, u32[]{:S(2)}) collective-permute-start(bf16[1,48,1536]{2,1,0:T(8,128)(2,1)S(1)} %dynamic-slice_bitcast_fusion), channel_id=1, source_target_pairs={{0,2},{1,3},{2,0},{3,1},{4,6},{5,7},{6,4},{7,5},{8,10},{9,11},{10,... | collective-permute-start | bytes 442376 | tf_op jit(solution)/shard_map/ppermute | solution.py:46
  20.3 3.0 %collective-permute-start.1 = (bf16[2,48,1536]{2,1,0:T(8,128)(2,1)S(1)}, bf16[2,48,1536]{2,1,0:T(8,128)(2,1)S(1)}, u32[]{:S(2)}, u32[]{:S(2)}) collective-permute-start(bf16[2,48,1536]{2,1,0:T(8,128)(2,1)S(1)} %maximum_select_fusion.4), channel_id=1, source_target_pairs={{0,8},{1,9},{2,10},{3,11},{4,12},{5,13},{6,14},{7,15},{8,0},{9,1},... | collective-permute-start | bytes 884744 | tf_op jit(solution)/shard_map/ppermute | solution.py:46
  23.3 8.6 %fusion.7 = f32[512,1536]{1,0:T(8,128)} fusion(bf16[512,1536]{1,0:T(8,128)(2,1)} %param.6, f32[512]{0:T(512)S(1)} %bitcast.56, f32[1536]{0:T(1024)S(1)} %get-tuple-element.42, f32[512]{0:T(512)S(1)} %bitcast.59, f32[1536]{0:T(1024)S(1)} %get-tuple-element.43, f32[512]{0:T(512)S(1)} %bitcast.48, f32[1536]{0:T(1024)S(1)} %get-tuple-element.40, ...), kind=kLoop, calls=%fused_computation.19 | loop fusion | flops 14942208 | bytes 4759552 | tf_op jit(solution)/shard_map/add | solution.py:84
  32.8 4.1 %collective-permute-start.2 = (bf16[4,48,1536]{2,1,0:T(8,128)(2,1)}, bf16[4,48,1536]{2,1,0:T(8,128)(2,1)}, u32[]{:S(2)}, u32[]{:S(2)}) collective-permute-start(bf16[4,48,1536]{2,1,0:T(8,128)(2,1)} %maximum_select_fusion.2), channel_id=1, source_target_pairs={{0,1},{1,0},{2,3},{3,2},{4,5},{5,4},{6,7},{7,6},{8,9},{9,8},{10,11... | collective-permute-start | bytes 1769480 | tf_op jit(solution)/shard_map/ppermute | solution.py:46
  37.0 2.1 reduce_sum.100
  39.1 2.5 %multiply_reduce_fusion.2 = f32[512]{0:T(512)S(1)} fusion(f32[512,1536]{1,0:T(8,128)} %fusion.7, f32[512]{0:T(512)S(1)} %broadcast_multiply_fusion.2), kind=kLoop, calls=%fused_computation.35 | loop fusion | flops 2358784 | bytes 3149824 | tf_op jit(solution)/shard_map/reduce_sum | solution.py:88
  49.0 13.5 %collective-permute-done.2 = bf16[4,48,1536]{2,1,0:T(8,128)(2,1)} collective-permute-done((bf16[4,48,1536]{2,1,0:T(8,128)(2,1)}, bf16[4,48,1536]{2,1,0:T(8,128)(2,1)}, u32[]{:S(2)}, u32[]{:S(2)}) %collective-permute-start.2) | collective-permute-done | bytes 589856 | tf_op jit(solution)/shard_map/ppermute | solution.py:46
  62.5 2.8 %maximum_select_fusion.1 = bf16[8,48,1536]{2,1,0:T(8,128)(2,1)} fusion(bf16[4,48,1536]{2,1,0:T(8,128)(2,1)} %maximum_select_fusion.2, bf16[4,48,1536]{2,1,0:T(8,128)(2,1)} %collective-permute-done.2, pred[]{:T(512)S(6)} %ne.18), kind=kLoop, calls=%fused_computation.44 | loop fusion | flops 1769472 | bytes 2359297 | tf_op jit(solution)/shard_map/jit(_where)/select_n | solution.py:47
  65.3 1.7 collective-permute-start.3
  67.1 7.5 %collective-permute-done.3 = f32[768,1536]{1,0:T(8,128)S(1)} collective-permute-done((f32[768,1536]{1,0:T(8,128)S(1)}, f32[768,1536]{1,0:T(8,128)S(1)}, u32[]{:S(2)}, u32[]{:S(2)}) %collective-permute-start.3) | collective-permute-done | bytes 4718624 | tf_op jit(solution)/shard_map/ppermute | solution.py:40
  74.6 3.1 %add.111 = f32[768,1536]{1,0:T(8,128)} add(f32[768,1536]{1,0:T(8,128)S(1)} %fusion.31, f32[768,1536]{1,0:T(8,128)S(1)} %collective-permute-done.3) | non-fusion elementwise | flops 1179648 | bytes 14155776 | tf_op jit(solution)/shard_map/add | solution.py:103
  78.2 35.0 %collective-permute-done.4 = bf16[8,48,1536]{2,1,0:T(8,128)(2,1)} collective-permute-done((bf16[8,48,1536]{2,1,0:T(8,128)(2,1)}, bf16[8,48,1536]{2,1,0:T(8,128)(2,1)}, u32[]{:S(2)}, u32[]{:S(2)}) %collective-permute-start.4) | collective-permute-done | bytes 1179680 | tf_op jit(solution)/shard_map/ppermute | solution.py:46
  113.2 2.6 %maximum_select_fusion = bf16[16,48,1536]{2,1,0:T(8,128)(2,1)S(1)} fusion(bf16[8,48,1536]{2,1,0:T(8,128)(2,1)} %maximum_select_fusion.1, bf16[8,48,1536]{2,1,0:T(8,128)(2,1)} %collective-permute-done.4, pred[]{:T(512)S(6)} %ne.22), kind=kLoop, calls=%fused_computation.38 | loop fusion | flops 3538944 | bytes 4718593 | tf_op jit(solution)/shard_map/jit(_where)/select_n | solution.py:47
  117.3 1.6 collective-permute-start.5
  118.9 4.5 %collective-permute-done.5 = bf16[768,1536]{1,0:T(8,128)(2,1)} collective-permute-done((bf16[768,1536]{1,0:T(8,128)(2,1)}, bf16[768,1536]{1,0:T(8,128)(2,1)}, u32[]{:S(2)}, u32[]{:S(2)}) %collective-permute-start.5) | collective-permute-done | bytes 2359328 | tf_op jit(solution)/shard_map/ppermute | solution.py:40
  123.4 2.7 %broadcast_select_fusion.1 = (bf16[768,1536]{1,0:T(8,128)(2,1)S(1)}, bf16[768,1536]{1,0:T(8,128)(2,1)S(1)}) fusion(bf16[768,1536]{1,0:T(8,128)(2,1)} %collective-permute-done.5, pred[]{:T(512)S(6)} %eq.24, bf16[2,2,2,2,48,1536]{5,4,3,2,1,0:T(8,128)(2,1)} %copy.19), kind=kLoop, calls=%fused_computation.40 | loop fusion | flops 2359296 | bytes 9437185 | tf_op jit(solution)/shard_map/jit(_where)/select_n | solution.py:108
  126.6 2.7 %copy-done.3 = f32[512,1536]{1,0:T(8,128)S(1)} copy-done((f32[512,1536]{1,0:T(8,128)S(1)}, f32[512,1536]{1,0:T(8,128)}, u32[]{:S(2)}) %copy-start.3) | copy-done | bytes 3145752
  129.3 3.8 %multiply_reduce_fusion = (f32[1536]{0:T(1024)S(1)}, f32[512]{0:T(512)S(1)}, f32[512]{0:T(512)S(1)}, f32[512,1536]{1,0:T(8,128)S(1)}) fusion(f32[512,1536]{1,0:T(8,128)S(1)} %copy-done.3, f32[512]{0:T(512)S(1)} %add_rsqrt_fusion, f32[512]{0:T(512)S(1)} %broadcast_multiply_fusion.2, f32[1536]{0:T(1024)S(1)} %copy-done.7, f32[512]{0:T(512)S(1)} %bitcast.50, ...), kind=kOutput, calls=%fused_computation.30 | convolution fusion | flops 2430072320 | bytes 12605440 | tf_op jit(solution)/shard_map/dot_general | solution.py:112
  133.2 5.5 %fusion.16 = (f32[1536]{0:T(1024)S(1)}, f32[1536]{0:T(1024)S(1)}, f32[1536]{0:T(1024)S(1)}, f32[1536]{0:T(1024)S(1)}, f32[1536]{0:T(1024)S(1)}, /*index=5*/f32[512,1536]{1,0:T(8,128)}) fusion(f32[512]{0:T(512)S(1)} %bitcast.57, bf16[512,1536]{1,0:T(8,128)(2,1)S(1)} %copy-done.4, f32[512]{0:T(512)S(1)} %bitcast.60, f32[512]{0:T(512)S(1)} %bitcast.51, ...), kind=kLoop, calls=%fused_computation.28 | loop fusion | flops 21225984 | bytes 11065344 | tf_op jit(solution)/shard_map/reduce_sum | solution.py:126
  138.9 6.5 %collective-permute-done.6 = f32[6,1536]{1,0:T(8,128)S(1)} collective-permute-done((f32[6,1536]{1,0:T(8,128)S(1)}, f32[6,1536]{1,0:T(8,128)S(1)}, u32[]{:S(2)}, u32[]{:S(2)}) %collective-permute-start.6) | collective-permute-done | bytes 36896 | tf_op jit(solution)/shard_map/ppermute | solution.py:34
  145.4 5.6 %collective-permute-start.7 = (f32[6,1536]{1,0:T(8,128)S(1)}, f32[6,1536]{1,0:T(8,128)S(1)}, u32[]{:S(2)}, u32[]{:S(2)}) collective-permute-start(f32[6,1536]{1,0:T(8,128)S(1)} %add.113), channel_id=1, source_target_pairs={{0,2},{1,3},{2,0},{3,1},{4,6},{5,7},{6,4},{7,5},{8,10},{9,11},{10,... | collective-permute-start | bytes 110600 | tf_op jit(solution)/shard_map/ppermute | solution.py:34
  152.8 2.7 %collective-permute-done.8 = f32[6,1536]{1,0:T(8,128)S(1)} collective-permute-done((f32[6,1536]{1,0:T(8,128)S(1)}, f32[6,1536]{1,0:T(8,128)S(1)}, u32[]{:S(2)}, u32[]{:S(2)}) %collective-permute-start.8) | collective-permute-done | bytes 36896 | tf_op jit(solution)/shard_map/ppermute | solution.py:34
  156.4 3.7 %collective-permute-done.9 = f32[6,1536]{1,0:T(8,128)S(1)} collective-permute-done((f32[6,1536]{1,0:T(8,128)S(1)}, f32[6,1536]{1,0:T(8,128)S(1)}, u32[]{:S(2)}, u32[]{:S(2)}) %collective-permute-start.9) | collective-permute-done | bytes 36896 | tf_op jit(solution)/shard_map/ppermute | solution.py:34
  160.1 4.0 %collective-permute-start.10 = (f32[6,1536]{1,0:T(8,128)S(1)}, f32[6,1536]{1,0:T(8,128)S(1)}, u32[]{:S(2)}, u32[]{:S(2)}) collective-permute-start(f32[6,1536]{1,0:T(8,128)S(1)} %add.116), channel_id=1, source_target_pairs={{0,16},{16,0},{32,48},{48,32},{64,80},{80,64},{96,112},{112,96},{1... | collective-permute-start | bytes 110600 | tf_op jit(solution)/shard_map/ppermute | solution.py:34
  166.0 2.3 %collective-permute-done.11 = f32[6,1536]{1,0:T(8,128)S(1)} collective-permute-done((f32[6,1536]{1,0:T(8,128)S(1)}, f32[6,1536]{1,0:T(8,128)S(1)}, u32[]{:S(2)}, u32[]{:S(2)}) %collective-permute-start.11) | collective-permute-done | bytes 36896 | tf_op jit(solution)/shard_map/ppermute | solution.py:34
  168.3 2.5 %collective-permute-start.12 = (f32[6,1536]{1,0:T(8,128)S(1)}, f32[6,1536]{1,0:T(8,128)S(1)}, u32[]{:S(2)}, u32[]{:S(2)}) collective-permute-start(f32[6,1536]{1,0:T(8,128)S(1)} %add.118), channel_id=1, source_target_pairs={{0,64},{16,80},{32,96},{48,112},{64,0},{80,16},{96,32},{112,48},{1... | collective-permute-start | bytes 110600 | tf_op jit(solution)/shard_map/ppermute | solution.py:34
  170.9 10.3 %multiply_add_fusion = f32[512,1536]{1,0:T(8,128)} fusion(f32[512,1536]{1,0:T(8,128)} %get-tuple-element.44, f32[512]{0:T(512)S(1)} %bitcast.58, f32[1536]{0:T(1024)S(1)} %get-tuple-element.42, f32[512]{0:T(512)S(1)} %bitcast.61, f32[1536]{0:T(1024)S(1)} %get-tuple-element.43, f32[512]{0:T(512)S(1)} %bitcast.52, f32[1536]{0:T(1024)S(1)} %get-tuple-element.40, ...), kind=kLoop, calls=%fused_computation.29 | loop fusion | flops 11010048 | bytes 6332416 | tf_op jit(solution)/shard_map/add | solution.py:130
  182.3 4.3 %fusion.33 = f32[512,1536]{1,0:T(8,128)} fusion(bf16[512,1536]{1,0:T(8,128)(2,1)S(1)} %multiply_convert_fusion, bf16[1536,1536]{1,0:T(8,128)(2,1)S(1)} %bitcast.45), kind=kOutput, calls=%fused_computation.90 | convolution fusion | flops 2415919104 | bytes 9437184 | tf_op jit(solution)/shard_map/dot_general | solution.py:111
  186.7 7.0 %collective-permute-done.14 = f32[48,1536]{1,0:T(8,128)S(1)} collective-permute-done((f32[48,1536]{1,0:T(8,128)}, f32[48,1536]{1,0:T(8,128)S(1)}, u32[]{:S(2)}, u32[]{:S(2)}) %collective-permute-start.14) | collective-permute-done | bytes 294944 | tf_op jit(solution)/shard_map/ppermute | solution.py:34
  195.1 7.2 %collective-permute-done.15 = f32[48,1536]{1,0:T(8,128)S(1)} collective-permute-done((f32[48,1536]{1,0:T(8,128)S(1)}, f32[48,1536]{1,0:T(8,128)S(1)}, u32[]{:S(2)}, u32[]{:S(2)}) %collective-permute-start.15) | collective-permute-done | bytes 294944 | tf_op jit(solution)/shard_map/ppermute | solution.py:34
  203.8 4.2 %collective-permute-done.16 = f32[48,1536]{1,0:T(8,128)S(1)} collective-permute-done((f32[48,1536]{1,0:T(8,128)S(1)}, f32[48,1536]{1,0:T(8,128)S(1)}, u32[]{:S(2)}, u32[]{:S(2)}) %collective-permute-start.16) | collective-permute-done | bytes 294944 | tf_op jit(solution)/shard_map/ppermute | solution.py:34
  208.0 4.7 %collective-permute-start.17 = (f32[48,1536]{1,0:T(8,128)S(1)}, f32[48,1536]{1,0:T(8,128)S(1)}, u32[]{:S(2)}, u32[]{:S(2)}) collective-permute-start(f32[48,1536]{1,0:T(8,128)S(1)} %add.127), channel_id=1, source_target_pairs={{0,16},{16,0},{32,48},{48,32},{64,80},{80,64},{96,112},{112,96},{1... | collective-permute-start | bytes 884744 | tf_op jit(solution)/shard_map/ppermute | solution.py:40
  (82 shorter events, 27.0 us)
Async XLA Ops:
  7.2 39.0 %copy-start = (bf16[512,1536]{1,0:T(8,128)(2,1)S(1)}, bf16[512,1536]{1,0:T(8,128)(2,1)}, u32[]{:S(2)}) copy-start(bf16[512,1536]{1,0:T(8,128)(2,1)} %param.7) | copy-start | bytes 4718596
  7.2 179.4 %reduce-scatter.2.cloned.1.call-start = ((), (), s32[]{:S(2)}) async-start(), calls=%async_computation.1 | async-start | bytes 5013504 | tf_op jit(solution)/shard_map/reduce_scatter | solution.py:104
  8.3 11.9 %collective-permute-start = (bf16[1,48,1536]{2,1,0:T(8,128)(2,1)S(1)}, bf16[1,48,1536]{2,1,0:T(8,128)(2,1)S(1)}, u32[]{:S(2)}, u32[]{:S(2)}) collective-permute-start(bf16[1,48,1536]{2,1,0:T(8,128)(2,1)S(1)} %dynamic-slice_bitcast_fusion), channel_id=1, source_target_pairs={{0,2},{1,3},{2,0},{3,1},{4,6},{5,7},{6,4},{7,5},{8,10},{9,11},{10,... | collective-permute-start | bytes 442376 | tf_op jit(solution)/shard_map/ppermute | solution.py:46
  20.3 11.7 %collective-permute-start.1 = (bf16[2,48,1536]{2,1,0:T(8,128)(2,1)S(1)}, bf16[2,48,1536]{2,1,0:T(8,128)(2,1)S(1)}, u32[]{:S(2)}, u32[]{:S(2)}) collective-permute-start(bf16[2,48,1536]{2,1,0:T(8,128)(2,1)S(1)} %maximum_select_fusion.4), channel_id=1, source_target_pairs={{0,8},{1,9},{2,10},{3,11},{4,12},{5,13},{6,14},{7,15},{8,0},{9,1},... | collective-permute-start | bytes 884744 | tf_op jit(solution)/shard_map/ppermute | solution.py:46
  32.8 8.8 %copy-start.7 = (f32[1536]{0:T(1024)S(1)}, f32[1536]{0:T(1024)}, u32[]{:S(2)}) copy-start(f32[1536]{0:T(1024)} %param.10) | copy-start | bytes 18436
  32.8 29.7 %collective-permute-start.2 = (bf16[4,48,1536]{2,1,0:T(8,128)(2,1)}, bf16[4,48,1536]{2,1,0:T(8,128)(2,1)}, u32[]{:S(2)}, u32[]{:S(2)}) collective-permute-start(bf16[4,48,1536]{2,1,0:T(8,128)(2,1)} %maximum_select_fusion.2), channel_id=1, source_target_pairs={{0,1},{1,0},{2,3},{3,2},{4,5},{5,4},{6,7},{7,6},{8,9},{9,8},{10,11... | collective-permute-start | bytes 1769480 | tf_op jit(solution)/shard_map/ppermute | solution.py:46
  39.1 2.8 %copy-start.2 = (f32[512,1536]{1,0:T(8,128)S(1)}, f32[512,1536]{1,0:T(8,128)}, u32[]{:S(2)}) copy-start(f32[512,1536]{1,0:T(8,128)} %fusion.7) | copy-start | bytes 9437188
  65.3 9.2 %collective-permute-start.3 = (f32[768,1536]{1,0:T(8,128)S(1)}, f32[768,1536]{1,0:T(8,128)S(1)}, u32[]{:S(2)}, u32[]{:S(2)}) collective-permute-start(f32[768,1536]{1,0:T(8,128)S(1)} %fusion.32), channel_id=1, source_target_pairs={{0,16},{16,0},{32,48},{48,32},{64,80},{80,64},{96,112},{112,96},{1... | collective-permute-start | bytes 14155784 | tf_op jit(solution)/shard_map/ppermute | solution.py:40
  77.7 35.5 %collective-permute-start.4 = (bf16[8,48,1536]{2,1,0:T(8,128)(2,1)}, bf16[8,48,1536]{2,1,0:T(8,128)(2,1)}, u32[]{:S(2)}, u32[]{:S(2)}) collective-permute-start(bf16[8,48,1536]{2,1,0:T(8,128)(2,1)} %maximum_select_fusion.1), channel_id=1, source_target_pairs={{0,4},{1,5},{2,6},{3,7},{4,0},{5,1},{6,2},{7,3},{8,12},{9,13},{10,... | collective-permute-start | bytes 3538952 | tf_op jit(solution)/shard_map/ppermute | solution.py:46
  117.3 6.1 %collective-permute-start.5 = (bf16[768,1536]{1,0:T(8,128)(2,1)}, bf16[768,1536]{1,0:T(8,128)(2,1)}, u32[]{:S(2)}, u32[]{:S(2)}) collective-permute-start(bf16[768,1536]{1,0:T(8,128)(2,1)} %bitcast.14), channel_id=1, source_target_pairs={{0,16},{16,0},{32,48},{48,32},{64,80},{80,64},{96,112},{112,96},{1... | collective-permute-start | bytes 7077896 | tf_op jit(solution)/shard_map/ppermute | solution.py:40
  126.2 3.1 %copy-start.3 = (f32[512,1536]{1,0:T(8,128)S(1)}, f32[512,1536]{1,0:T(8,128)}, u32[]{:S(2)}) copy-start(f32[512,1536]{1,0:T(8,128)} %fusion.7) | copy-start | bytes 9437188
  126.6 6.5 %copy-start.5 = (bf16[16,2,48,1536]{3,2,1,0:T(8,128)(2,1)}, bf16[16,2,48,1536]{3,2,1,0:T(8,128)(2,1)S(1)}, u32[]{:S(2)}) copy-start(bf16[16,2,48,1536]{3,2,1,0:T(8,128)(2,1)S(1)} %pad_maximum_fusion) | copy-start | bytes 14155780
  129.3 3.9 %copy-start.4 = (bf16[512,1536]{1,0:T(8,128)(2,1)S(1)}, bf16[512,1536]{1,0:T(8,128)(2,1)}, u32[]{:S(2)}) copy-start(bf16[512,1536]{1,0:T(8,128)(2,1)} %param.6) | copy-start | bytes 4718596
  138.8 6.6 %collective-permute-start.6 = (f32[6,1536]{1,0:T(8,128)S(1)}, f32[6,1536]{1,0:T(8,128)S(1)}, u32[]{:S(2)}, u32[]{:S(2)}) collective-permute-start(f32[6,1536]{1,0:T(8,128)S(1)} %concatenate.45), channel_id=1, source_target_pairs={{0,1},{1,0},{2,3},{3,2},{4,5},{5,4},{6,7},{7,6},{8,9},{9,8},{10,11... | collective-permute-start | bytes 110600 | tf_op jit(solution)/shard_map/ppermute | solution.py:34
  145.4 7.1 %collective-permute-start.7 = (f32[6,1536]{1,0:T(8,128)S(1)}, f32[6,1536]{1,0:T(8,128)S(1)}, u32[]{:S(2)}, u32[]{:S(2)}) collective-permute-start(f32[6,1536]{1,0:T(8,128)S(1)} %add.113), channel_id=1, source_target_pairs={{0,2},{1,3},{2,0},{3,1},{4,6},{5,7},{6,4},{7,5},{8,10},{9,11},{10,... | collective-permute-start | bytes 110600 | tf_op jit(solution)/shard_map/ppermute | solution.py:34
  152.5 3.0 %collective-permute-start.8 = (f32[6,1536]{1,0:T(8,128)S(1)}, f32[6,1536]{1,0:T(8,128)S(1)}, u32[]{:S(2)}, u32[]{:S(2)}) collective-permute-start(f32[6,1536]{1,0:T(8,128)S(1)} %add.114), channel_id=1, source_target_pairs={{0,4},{1,5},{2,6},{3,7},{4,0},{5,1},{6,2},{7,3},{8,12},{9,13},{10,... | collective-permute-start | bytes 110600 | tf_op jit(solution)/shard_map/ppermute | solution.py:34
  155.5 4.5 %collective-permute-start.9 = (f32[6,1536]{1,0:T(8,128)S(1)}, f32[6,1536]{1,0:T(8,128)S(1)}, u32[]{:S(2)}, u32[]{:S(2)}) collective-permute-start(f32[6,1536]{1,0:T(8,128)S(1)} %add.115), channel_id=1, source_target_pairs={{0,8},{1,9},{2,10},{3,11},{4,12},{5,13},{6,14},{7,15},{8,0},{9,1},... | collective-permute-start | bytes 110600 | tf_op jit(solution)/shard_map/ppermute | solution.py:34
  160.1 4.9 %collective-permute-start.10 = (f32[6,1536]{1,0:T(8,128)S(1)}, f32[6,1536]{1,0:T(8,128)S(1)}, u32[]{:S(2)}, u32[]{:S(2)}) collective-permute-start(f32[6,1536]{1,0:T(8,128)S(1)} %add.116), channel_id=1, source_target_pairs={{0,16},{16,0},{32,48},{48,32},{64,80},{80,64},{96,112},{112,96},{1... | collective-permute-start | bytes 110600 | tf_op jit(solution)/shard_map/ppermute | solution.py:34
  165.0 3.3 %collective-permute-start.11 = (f32[6,1536]{1,0:T(8,128)S(1)}, f32[6,1536]{1,0:T(8,128)S(1)}, u32[]{:S(2)}, u32[]{:S(2)}) collective-permute-start(f32[6,1536]{1,0:T(8,128)S(1)} %add.117), channel_id=1, source_target_pairs={{0,32},{16,48},{32,0},{48,16},{64,96},{80,112},{96,64},{112,80},{1... | collective-permute-start | bytes 110600 | tf_op jit(solution)/shard_map/ppermute | solution.py:34
  168.3 12.9 %collective-permute-start.12 = (f32[6,1536]{1,0:T(8,128)S(1)}, f32[6,1536]{1,0:T(8,128)S(1)}, u32[]{:S(2)}, u32[]{:S(2)}) collective-permute-start(f32[6,1536]{1,0:T(8,128)S(1)} %add.118), channel_id=1, source_target_pairs={{0,64},{16,80},{32,96},{48,112},{64,0},{80,16},{96,32},{112,48},{1... | collective-permute-start | bytes 110600 | tf_op jit(solution)/shard_map/ppermute | solution.py:34
  170.9 11.4 %copy-start.6 = (bf16[16,2,48,1536]{3,2,1,0:T(8,128)(2,1)S(1)}, bf16[16,2,48,1536]{3,2,1,0:T(8,128)(2,1)}, u32[]{:S(2)}) copy-start(bf16[16,2,48,1536]{3,2,1,0:T(8,128)(2,1)} %copy-done.5) | copy-start | bytes 14155780
  181.2 5.3 %collective-permute-start.13 = (f32[6,1536]{1,0:T(8,128)S(1)}, f32[6,1536]{1,0:T(8,128)S(1)}, u32[]{:S(2)}, u32[]{:S(2)}) collective-permute-start(f32[6,1536]{1,0:T(8,128)S(1)} %add.119), channel_id=1, source_target_pairs={{0,128},{16,144},{32,160},{48,176},{64,192},{80,208},{96,224},{112... | collective-permute-start | bytes 110600 | tf_op jit(solution)/shard_map/ppermute | solution.py:34
  182.3 32.5 %copy-start.1 = (bf16[512,1536]{1,0:T(8,128)(2,1)S(1)}, bf16[512,1536]{1,0:T(8,128)(2,1)}, u32[]{:S(2)}) copy-start(bf16[512,1536]{1,0:T(8,128)(2,1)} %param.7) | copy-start | bytes 4718596
  186.6 7.1 %collective-permute-start.14 = (f32[48,1536]{1,0:T(8,128)}, f32[48,1536]{1,0:T(8,128)S(1)}, u32[]{:S(2)}, u32[]{:S(2)}) collective-permute-start(f32[48,1536]{1,0:T(8,128)} %reduce-scatter.2.cloned.1.call-done), channel_id=1, source_target_pairs={{0,32},{16,48},{32,0},{48,16},{64,96},{80,112},{96,64},{112,80},{1... | collective-permute-start | bytes 884744 | tf_op jit(solution)/shard_map/ppermute | solution.py:34
  194.7 7.6 %collective-permute-start.15 = (f32[48,1536]{1,0:T(8,128)S(1)}, f32[48,1536]{1,0:T(8,128)S(1)}, u32[]{:S(2)}, u32[]{:S(2)}) collective-permute-start(f32[48,1536]{1,0:T(8,128)S(1)} %add.125), channel_id=1, source_target_pairs={{0,64},{16,80},{32,96},{48,112},{64,0},{80,16},{96,32},{112,48},{1... | collective-permute-start | bytes 884744 | tf_op jit(solution)/shard_map/ppermute | solution.py:34
  202.3 5.7 %collective-permute-start.16 = (f32[48,1536]{1,0:T(8,128)S(1)}, f32[48,1536]{1,0:T(8,128)S(1)}, u32[]{:S(2)}, u32[]{:S(2)}) collective-permute-start(f32[48,1536]{1,0:T(8,128)S(1)} %add.126), channel_id=1, source_target_pairs={{0,128},{16,144},{32,160},{48,176},{64,192},{80,208},{96,224},{112... | collective-permute-start | bytes 884744 | tf_op jit(solution)/shard_map/ppermute | solution.py:34
  208.0 5.9 %collective-permute-start.17 = (f32[48,1536]{1,0:T(8,128)S(1)}, f32[48,1536]{1,0:T(8,128)S(1)}, u32[]{:S(2)}, u32[]{:S(2)}) collective-permute-start(f32[48,1536]{1,0:T(8,128)S(1)} %add.127), channel_id=1, source_target_pairs={{0,16},{16,0},{32,48},{48,32},{64,80},{80,64},{96,112},{112,96},{1... | collective-permute-start | bytes 884744 | tf_op jit(solution)/shard_map/ppermute | solution.py:40
Sparse Core Ops, SparseCore 0:
  77.8 96.7 reduce-scatter.1

commit v5 on v4

--- a/solution.py
+++ b/solution.py
@@ -96,12 +96,10 @@
     contract = (((0,), (0,)), ((), ()))
     keep_terms = lax.dot_general(keep_act, grad_out, contract, preferred_element_type=jnp.float32)
     send_terms = lax.dot_general(send_act, grad_out, contract, preferred_element_type=jnp.float32)
-    held, keep_terms, send_terms, activation = lax.optimization_barrier(
-        (held, keep_terms, send_terms, activation)
-    )
+    chip_terms = keep_terms + sibling(send_terms)
+    held, chip_terms, activation = lax.optimization_barrier((held, chip_terms, activation))
+    shard_sum = lax.psum_scatter(chip_terms, "fsdp", scatter_dimension=0, tiled=True)
     held = doubling_step(held, "fsdp", masks[3])
-    chip_terms = keep_terms + sibling(send_terms)
-    shard_sum = lax.psum_scatter(chip_terms, "fsdp", scatter_dimension=0, tiled=True)
     held, chip_terms = lax.optimization_barrier((held, chip_terms))
     gathered = doubling_order(held, masks)
     other = sibling(gathered)
@@ -132,6 +130,7 @@
         )
     small = jnp.concatenate([jnp.stack(kernel_rows), gain_grad[None]], axis=0)
     small = butterfly(small, "fsdp", (1, 2, 4, 8))
+    small, output, grad_hidden = lax.optimization_barrier((small, output, grad_hidden))
     small = butterfly(small, "dp", (1, 2, 4, 8))
     shard_sum, small, output, grad_hidden = lax.optimization_barrier(
         (shard_sum, small, output, grad_hidden)

time: 222 us -> 230 us (1.036)
  matrix products: 10.9 us -> 17.5 us
  starting transfers between devices: 40.3 us -> 45.8 us
  other arithmetic: 48.5 us -> 45.6 us
    ppermute x4, waiting for transfers between devices: 48.5 us -> 60.7 us  [doubling_step(): received = lax.ppermute(held, axis, [(i, i ^ mask) for i in range(size)])]
    ppermute x3, waiting for transfers between devices: 12.6 us -> 5.09 us  [sibling(): return lax.ppermute(x, 'dp', [(i, i ^ 1) for i in range(size)])]
    ppermute x11, waiting for transfers between devices: 36 us -> 29.4 us  [butterfly(): x = x + lax.ppermute(x, axis, pairs)]
    dot_general x1, matrix products: 1.39 us -> 5.84 us  [shards(): lax.dot_general(keep_act, grad_out, contract, preferred_element_type=jnp....]
    ppermute x11, starting transfers between devices: 16.8 us -> 20.8 us  [butterfly(): x = x + lax.ppermute(x, axis, pairs)]
    add x1 -> x0, other arithmetic: 3.1 us -> none  [shards(): chip_terms = keep_terms + sibling(send_terms)]
  transfers between devices with their start and end apart: 19 -> 19, of which waited for: 14 -> 13; matrix products, arithmetic and copies ran while one was open for 26% -> 21% of each run, Pallas kernels for 0% -> 0%
where the time goes in v5:
time: 230 us
  waiting for transfers between devices  95.3 us (41%)
  starting transfers between devices  45.8 us (20%)
  other arithmetic  45.6 us (20%)
  matrix products  17.5 us (8%)
  between operations  14.4 us (6%)
  local copies, waits for them, and re-layouts  11.4 us (5%)
    ppermute x4, waiting for transfers between devices, doubling_step(): received = lax.ppermute(held, axis, [(i, i ^ mask) for i in range(size)])  60.7 us
    ppermute x11, waiting for transfers between devices, butterfly(): x = x + lax.ppermute(x, axis, pairs)  29.4 us
    ppermute x11, starting transfers between devices, butterfly(): x = x + lax.ppermute(x, axis, pairs)  20.8 us
    ppermute x4, starting transfers between devices, doubling_step(): received = lax.ppermute(held, axis, [(i, i ^ mask) for i in range(size)])  15.8 us
    add x1, other arithmetic, shards(): grad_hidden + conv_kernel[k] * (back_views[count - 1 - k] * taps[count -...  10.3 us
    ppermute x3, starting transfers between devices, sibling(): return lax.ppermute(x, 'dp', [(i, i ^ 1) for i in range(size)])  9.14 us
    add x1, other arithmetic, shards(): mixed + conv_kernel[k] * views[k].astype(jnp.float32) * taps[k][:, None]  8.85 us
    select_n x4, other arithmetic, doubling_step(): jnp.where(upper, jnp.concatenate([received, held], axis=0), jnp.concatena...  6.34 us
  transfers between devices with their start and end apart: 19, of which 13 were waited for; matrix products, arithmetic and copies ran while one was open for 21% of the time, Pallas kernels for 0%

profile of v5, /device:TPU:1, one launch (start us, length us, event | category | flops | bytes accessed | tf_op | source)
XLA Modules:
  0.0 229.9 jit_solution(14615552904780816947)
XLA Ops:
  8.3 7.8 %collective-permute-start = (bf16[1,48,1536]{2,1,0:T(8,128)(2,1)S(1)}, bf16[1,48,1536]{2,1,0:T(8,128)(2,1)S(1)}, u32[]{:S(2)}, u32[]{:S(2)}) collective-permute-start(bf16[1,48,1536]{2,1,0:T(8,128)(2,1)S(1)} %dynamic-slice_bitcast_fusion), channel_id=1, source_target_pairs={{0,2},{1,3},{2,0},{3,1},{4,6},{5,7},{6,4},{7,5},{8,10},{9,11},{10,... | collective-permute-start | bytes 442376 | tf_op jit(solution)/shard_map/ppermute | solution.py:46
  20.3 3.0 %collective-permute-start.1 = (bf16[2,48,1536]{2,1,0:T(8,128)(2,1)S(1)}, bf16[2,48,1536]{2,1,0:T(8,128)(2,1)S(1)}, u32[]{:S(2)}, u32[]{:S(2)}) collective-permute-start(bf16[2,48,1536]{2,1,0:T(8,128)(2,1)S(1)} %maximum_select_fusion.4), channel_id=1, source_target_pairs={{0,8},{1,9},{2,10},{3,11},{4,12},{5,13},{6,14},{7,15},{8,0},{9,1},... | collective-permute-start | bytes 884744 | tf_op jit(solution)/shard_map/ppermute | solution.py:46
  23.3 8.9 %fusion.7 = f32[512,1536]{1,0:T(8,128)} fusion(bf16[512,1536]{1,0:T(8,128)(2,1)} %param.6, f32[512]{0:T(512)S(1)} %bitcast.56, f32[1536]{0:T(1024)S(1)} %get-tuple-element.46, f32[512]{0:T(512)S(1)} %bitcast.59, f32[1536]{0:T(1024)S(1)} %get-tuple-element.47, f32[512]{0:T(512)S(1)} %bitcast.48, f32[1536]{0:T(1024)S(1)} %get-tuple-element.44, ...), kind=kLoop, calls=%fused_computation.20 | loop fusion | flops 14942208 | bytes 4759552 | tf_op jit(solution)/shard_map/add | solution.py:84
  33.0 2.1 reduce_sum.100
  35.2 2.5 %multiply_reduce_fusion.2 = f32[512]{0:T(512)S(1)} fusion(f32[512,1536]{1,0:T(8,128)} %fusion.7, f32[512]{0:T(512)S(1)} %broadcast_multiply_fusion.2), kind=kLoop, calls=%fused_computation.36 | loop fusion | flops 2358784 | bytes 3149824 | tf_op jit(solution)/shard_map/reduce_sum | solution.py:88
  40.8 2.4 %constant_dynamic-slice_fusion.1 = (bf16[512,16,1,48]{0,3,2,1:T(8,128)(2,1)}, bf16[512,16,1,48]{0,3,2,1:T(8,128)(2,1)S(1)}) fusion(bf16[512,16,2,48]{0,3,2,1:T(8,128)(2,1)} %bitcast.43, s32[]{:T(128)S(6)} %select_n.77, s32[]{:T(128)S(6)} %select_n.78), kind=kLoop, calls=%fused_computation.87 | loop fusion | bytes 3145736 | tf_op jit(solution)/shard_map/jit(dynamic_index_in_dim)/dynamic_slice | solution.py:94
  43.2 3.5 %fusion.31 = f32[768,1536]{1,0:T(8,128)} fusion(bf16[512,768]{0,1:T(8,128)(2,1)S(1)} %bitcast.47, bf16[512,1536]{1,0:T(8,128)(2,1)S(1)} %copy-done), kind=kOutput, calls=%fused_computation.89 | convolution fusion | flops 1207959552 | bytes 7077888 | tf_op jit(solution)/shard_map/dot_general | solution.py:98
  47.9 4.5 %collective-permute-start.2 = (bf16[4,48,1536]{2,1,0:T(8,128)(2,1)}, bf16[4,48,1536]{2,1,0:T(8,128)(2,1)}, u32[]{:S(2)}, u32[]{:S(2)}) collective-permute-start(bf16[4,48,1536]{2,1,0:T(8,128)(2,1)} %maximum_select_fusion.2), channel_id=1, source_target_pairs={{0,1},{1,0},{2,3},{3,2},{4,5},{5,4},{6,7},{7,6},{8,9},{9,8},{10,11... | collective-permute-start | bytes 1769480 | tf_op jit(solution)/shard_map/ppermute | solution.py:46
  52.4 26.7 %collective-permute-done.2 = bf16[4,48,1536]{2,1,0:T(8,128)(2,1)} collective-permute-done((bf16[4,48,1536]{2,1,0:T(8,128)(2,1)}, bf16[4,48,1536]{2,1,0:T(8,128)(2,1)}, u32[]{:S(2)}, u32[]{:S(2)}) %collective-permute-start.2) | collective-permute-done | bytes 589856 | tf_op jit(solution)/shard_map/ppermute | solution.py:46
  79.1 2.8 %maximum_select_fusion.1 = bf16[8,48,1536]{2,1,0:T(8,128)(2,1)} fusion(bf16[4,48,1536]{2,1,0:T(8,128)(2,1)} %maximum_select_fusion.2, bf16[4,48,1536]{2,1,0:T(8,128)(2,1)} %collective-permute-done.2, pred[]{:T(512)S(6)} %ne.18), kind=kLoop, calls=%fused_computation.45 | loop fusion | flops 1769472 | bytes 2359297 | tf_op jit(solution)/shard_map/jit(_where)/select_n | solution.py:47
  81.9 5.8 %convolution_add_fusion = f32[768,1536]{1,0:T(8,128)} fusion(f32[768,1536]{1,0:T(8,128)} %collective-permute-done.3, bf16[512,768]{0,1:T(8,128)(2,1)S(1)} %bitcast.44, bf16[512,1536]{1,0:T(8,128)(2,1)S(1)} %copy-done), kind=kOutput, calls=%fused_computation.1 | convolution fusion | flops 1209139200 | bytes 11796480 | tf_op jit(solution)/shard_map/dot_general | solution.py:97
  88.2 34.1 %collective-permute-done.4 = bf16[8,48,1536]{2,1,0:T(8,128)(2,1)} collective-permute-done((bf16[8,48,1536]{2,1,0:T(8,128)(2,1)}, bf16[8,48,1536]{2,1,0:T(8,128)(2,1)}, u32[]{:S(2)}, u32[]{:S(2)}) %collective-permute-start.4) | collective-permute-done | bytes 1179680 | tf_op jit(solution)/shard_map/ppermute | solution.py:46
  122.3 2.6 %maximum_select_fusion = bf16[16,48,1536]{2,1,0:T(8,128)(2,1)S(1)} fusion(bf16[8,48,1536]{2,1,0:T(8,128)(2,1)} %maximum_select_fusion.1, bf16[8,48,1536]{2,1,0:T(8,128)(2,1)} %collective-permute-done.4, pred[]{:T(512)S(6)} %ne.22), kind=kLoop, calls=%fused_computation.39 | loop fusion | flops 3538944 | bytes 4718593 | tf_op jit(solution)/shard_map/jit(_where)/select_n | solution.py:47
  128.2 4.5 %collective-permute-done.5 = bf16[768,1536]{1,0:T(8,128)(2,1)} collective-permute-done((bf16[768,1536]{1,0:T(8,128)(2,1)}, bf16[768,1536]{1,0:T(8,128)(2,1)}, u32[]{:S(2)}, u32[]{:S(2)}) %collective-permute-start.5) | collective-permute-done | bytes 2359328 | tf_op jit(solution)/shard_map/ppermute | solution.py:40
  132.7 2.7 %broadcast_select_fusion.1 = (bf16[768,1536]{1,0:T(8,128)(2,1)S(1)}, bf16[768,1536]{1,0:T(8,128)(2,1)S(1)}) fusion(bf16[768,1536]{1,0:T(8,128)(2,1)} %collective-permute-done.5, pred[]{:T(512)S(6)} %eq.24, bf16[2,2,2,2,48,1536]{5,4,3,2,1,0:T(8,128)(2,1)} %copy.19), kind=kLoop, calls=%fused_computation.41 | loop fusion | flops 2359296 | bytes 9437185 | tf_op jit(solution)/shard_map/jit(_where)/select_n | solution.py:106
  135.9 2.7 %copy-done.2 = f32[512,1536]{1,0:T(8,128)S(1)} copy-done((f32[512,1536]{1,0:T(8,128)S(1)}, f32[512,1536]{1,0:T(8,128)}, u32[]{:S(2)}) %copy-start.2) | copy-done | bytes 3145752
  138.5 3.8 %multiply_reduce_fusion = (f32[1536]{0:T(1024)S(1)}, f32[512]{0:T(512)S(1)}, f32[512]{0:T(512)S(1)}, f32[512,1536]{1,0:T(8,128)S(1)}) fusion(f32[512,1536]{1,0:T(8,128)S(1)} %copy-done.2, f32[512]{0:T(512)S(1)} %add_rsqrt_fusion, f32[512]{0:T(512)S(1)} %broadcast_multiply_fusion.2, f32[1536]{0:T(1024)S(1)} %copy-done.7, f32[512]{0:T(512)S(1)} %bitcast.50, ...), kind=kOutput, calls=%fused_computation.31 | convolution fusion | flops 2430072320 | bytes 12605440 | tf_op jit(solution)/shard_map/dot_general | solution.py:110
  142.4 5.5 %fusion.16 = (f32[1536]{0:T(1024)S(1)}, f32[1536]{0:T(1024)S(1)}, f32[1536]{0:T(1024)S(1)}, f32[1536]{0:T(1024)S(1)}, f32[1536]{0:T(1024)S(1)}, /*index=5*/f32[512,1536]{1,0:T(8,128)}) fusion(f32[512]{0:T(512)S(1)} %bitcast.57, bf16[512,1536]{1,0:T(8,128)(2,1)S(1)} %copy-done.3, f32[512]{0:T(512)S(1)} %bitcast.60, f32[512]{0:T(512)S(1)} %bitcast.51, ...), kind=kLoop, calls=%fused_computation.29 | loop fusion | flops 21225984 | bytes 11065344 | tf_op jit(solution)/shard_map/reduce_sum | solution.py:124
  148.1 5.6 %collective-permute-done.6 = f32[6,1536]{1,0:T(8,128)S(1)} collective-permute-done((f32[6,1536]{1,0:T(8,128)S(1)}, f32[6,1536]{1,0:T(8,128)S(1)}, u32[]{:S(2)}, u32[]{:S(2)}) %collective-permute-start.6) | collective-permute-done | bytes 36896 | tf_op jit(solution)/shard_map/ppermute | solution.py:34
  153.8 7.7 %collective-permute-start.7 = (f32[6,1536]{1,0:T(8,128)S(1)}, f32[6,1536]{1,0:T(8,128)S(1)}, u32[]{:S(2)}, u32[]{:S(2)}) collective-permute-start(f32[6,1536]{1,0:T(8,128)S(1)} %add.113), channel_id=1, source_target_pairs={{0,2},{1,3},{2,0},{3,1},{4,6},{5,7},{6,4},{7,5},{8,10},{9,11},{10,... | collective-permute-start | bytes 110600 | tf_op jit(solution)/shard_map/ppermute | solution.py:34
  163.0 10.3 %multiply_add_fusion = f32[512,1536]{1,0:T(8,128)} fusion(f32[512,1536]{1,0:T(8,128)} %get-tuple-element.48, f32[512]{0:T(512)S(1)} %bitcast.58, f32[1536]{0:T(1024)S(1)} %get-tuple-element.46, f32[512]{0:T(512)S(1)} %bitcast.61, f32[1536]{0:T(1024)S(1)} %get-tuple-element.47, f32[512]{0:T(512)S(1)} %bitcast.52, f32[1536]{0:T(1024)S(1)} %get-tuple-element.44, ...), kind=kLoop, calls=%fused_computation.30 | loop fusion | flops 11010048 | bytes 6332416 | tf_op jit(solution)/shard_map/add | solution.py:128
  173.3 2.1 collective-permute-start.9
  175.5 4.3 %fusion.32 = f32[512,1536]{1,0:T(8,128)} fusion(bf16[512,1536]{1,0:T(8,128)(2,1)S(1)} %multiply_convert_fusion, bf16[1536,1536]{1,0:T(8,128)(2,1)S(1)} %bitcast.46), kind=kOutput, calls=%fused_computation.90 | convolution fusion | flops 2415919104 | bytes 9437184 | tf_op jit(solution)/shard_map/dot_general | solution.py:109
  179.8 2.3 %collective-permute-start.10 = (f32[6,1536]{1,0:T(8,128)S(1)}, f32[6,1536]{1,0:T(8,128)S(1)}, u32[]{:S(2)}, u32[]{:S(2)}) collective-permute-start(f32[6,1536]{1,0:T(8,128)S(1)} %add.116), channel_id=1, source_target_pairs={{0,16},{16,0},{32,48},{48,32},{64,80},{80,64},{96,112},{112,96},{1... | collective-permute-start | bytes 110600 | tf_op jit(solution)/shard_map/ppermute | solution.py:34
  184.1 2.2 collective-permute-done.11
  186.2 2.9 %collective-permute-start.12 = (f32[6,1536]{1,0:T(8,128)S(1)}, f32[6,1536]{1,0:T(8,128)S(1)}, u32[]{:S(2)}, u32[]{:S(2)}) collective-permute-start(f32[6,1536]{1,0:T(8,128)S(1)} %add.122), channel_id=1, source_target_pairs={{0,64},{16,80},{32,96},{48,112},{64,0},{80,16},{96,32},{112,48},{1... | collective-permute-start | bytes 110600 | tf_op jit(solution)/shard_map/ppermute | solution.py:34
  191.1 2.9 %collective-permute-done.13 = f32[6,1536]{1,0:T(8,128)S(1)} collective-permute-done((f32[6,1536]{1,0:T(8,128)S(1)}, f32[6,1536]{1,0:T(8,128)S(1)}, u32[]{:S(2)}, u32[]{:S(2)}) %collective-permute-start.13) | collective-permute-done | bytes 36896 | tf_op jit(solution)/shard_map/ppermute | solution.py:34
  195.3 4.6 %collective-permute-done.14 = f32[48,1536]{1,0:T(8,128)S(1)} collective-permute-done((f32[48,1536]{1,0:T(8,128)}, f32[48,1536]{1,0:T(8,128)S(1)}, u32[]{:S(2)}, u32[]{:S(2)}) %collective-permute-start.14) | collective-permute-done | bytes 294944 | tf_op jit(solution)/shard_map/ppermute | solution.py:34
  200.9 2.9 %collective-permute-start.15 = (f32[48,1536]{1,0:T(8,128)S(1)}, f32[48,1536]{1,0:T(8,128)S(1)}, u32[]{:S(2)}, u32[]{:S(2)}) collective-permute-start(f32[48,1536]{1,0:T(8,128)S(1)} %add.125), channel_id=1, source_target_pairs={{0,64},{16,80},{32,96},{48,112},{64,0},{80,16},{96,32},{112,48},{1... | collective-permute-start | bytes 884744 | tf_op jit(solution)/shard_map/ppermute | solution.py:34
  203.8 5.2 %collective-permute-done.15 = f32[48,1536]{1,0:T(8,128)S(1)} collective-permute-done((f32[48,1536]{1,0:T(8,128)S(1)}, f32[48,1536]{1,0:T(8,128)S(1)}, u32[]{:S(2)}, u32[]{:S(2)}) %collective-permute-start.15) | collective-permute-done | bytes 294944 | tf_op jit(solution)/shard_map/ppermute | solution.py:34
  209.8 4.9 %collective-permute-done.16 = f32[48,1536]{1,0:T(8,128)S(1)} collective-permute-done((f32[48,1536]{1,0:T(8,128)S(1)}, f32[48,1536]{1,0:T(8,128)S(1)}, u32[]{:S(2)}, u32[]{:S(2)}) %collective-permute-start.16) | collective-permute-done | bytes 294944 | tf_op jit(solution)/shard_map/ppermute | solution.py:34
  214.8 6.2 %collective-permute-start.17 = (f32[48,1536]{1,0:T(8,128)S(1)}, f32[48,1536]{1,0:T(8,128)S(1)}, u32[]{:S(2)}, u32[]{:S(2)}) collective-permute-start(f32[48,1536]{1,0:T(8,128)S(1)} %add.127), channel_id=1, source_target_pairs={{0,16},{16,0},{32,48},{48,32},{64,80},{80,64},{96,112},{112,96},{1... | collective-permute-start | bytes 884744 | tf_op jit(solution)/shard_map/ppermute | solution.py:40
  (81 shorter events, 25.6 us)
Async XLA Ops:
  7.2 36.0 %copy-start = (bf16[512,1536]{1,0:T(8,128)(2,1)S(1)}, bf16[512,1536]{1,0:T(8,128)(2,1)}, u32[]{:S(2)}) copy-start(bf16[512,1536]{1,0:T(8,128)(2,1)} %param.7) | copy-start | bytes 4718596
  7.2 186.9 %reduce-scatter.2.cloned.1.call-start = ((), (), s32[]{:S(2)}) async-start(), calls=%async_computation.1 | async-start | bytes 5013504 | tf_op jit(solution)/shard_map/reduce_scatter | solution.py:101
  8.3 11.9 %collective-permute-start = (bf16[1,48,1536]{2,1,0:T(8,128)(2,1)S(1)}, bf16[1,48,1536]{2,1,0:T(8,128)(2,1)S(1)}, u32[]{:S(2)}, u32[]{:S(2)}) collective-permute-start(bf16[1,48,1536]{2,1,0:T(8,128)(2,1)S(1)} %dynamic-slice_bitcast_fusion), channel_id=1, source_target_pairs={{0,2},{1,3},{2,0},{3,1},{4,6},{5,7},{6,4},{7,5},{8,10},{9,11},{10,... | collective-permute-start | bytes 442376 | tf_op jit(solution)/shard_map/ppermute | solution.py:46
  20.3 11.9 %collective-permute-start.1 = (bf16[2,48,1536]{2,1,0:T(8,128)(2,1)S(1)}, bf16[2,48,1536]{2,1,0:T(8,128)(2,1)S(1)}, u32[]{:S(2)}, u32[]{:S(2)}) collective-permute-start(bf16[2,48,1536]{2,1,0:T(8,128)(2,1)S(1)} %maximum_select_fusion.4), channel_id=1, source_target_pairs={{0,8},{1,9},{2,10},{3,11},{4,12},{5,13},{6,14},{7,15},{8,0},{9,1},... | collective-permute-start | bytes 884744 | tf_op jit(solution)/shard_map/ppermute | solution.py:46
  33.0 4.6 %copy-start.7 = (f32[1536]{0:T(1024)S(1)}, f32[1536]{0:T(1024)}, u32[]{:S(2)}) copy-start(f32[1536]{0:T(1024)} %param.10) | copy-start | bytes 18436
  35.2 2.8 %copy-start.1 = (f32[512,1536]{1,0:T(8,128)S(1)}, f32[512,1536]{1,0:T(8,128)}, u32[]{:S(2)}) copy-start(f32[512,1536]{1,0:T(8,128)} %fusion.7) | copy-start | bytes 9437188
  46.7 35.2 %collective-permute-start.3 = (f32[768,1536]{1,0:T(8,128)}, f32[768,1536]{1,0:T(8,128)}, u32[]{:S(2)}, u32[]{:S(2)}) collective-permute-start(f32[768,1536]{1,0:T(8,128)} %fusion.31), channel_id=1, source_target_pairs={{0,16},{16,0},{32,48},{48,32},{64,80},{80,64},{96,112},{112,96},{1... | collective-permute-start | bytes 14155784 | tf_op jit(solution)/shard_map/ppermute | solution.py:40
  47.9 31.1 %collective-permute-start.2 = (bf16[4,48,1536]{2,1,0:T(8,128)(2,1)}, bf16[4,48,1536]{2,1,0:T(8,128)(2,1)}, u32[]{:S(2)}, u32[]{:S(2)}) collective-permute-start(bf16[4,48,1536]{2,1,0:T(8,128)(2,1)} %maximum_select_fusion.2), channel_id=1, source_target_pairs={{0,1},{1,0},{2,3},{3,2},{4,5},{5,4},{6,7},{7,6},{8,9},{9,8},{10,11... | collective-permute-start | bytes 1769480 | tf_op jit(solution)/shard_map/ppermute | solution.py:46
  52.4 29.5 %copy-start.4 = (bf16[512,16,1,48]{0,3,2,1:T(8,128)(2,1)S(1)}, bf16[512,16,1,48]{0,3,2,1:T(8,128)(2,1)}, u32[]{:S(2)}) copy-start(bf16[512,16,1,48]{0,3,2,1:T(8,128)(2,1)} %get-tuple-element.51) | copy-start | bytes 2359300
  87.7 34.6 %collective-permute-start.4 = (bf16[8,48,1536]{2,1,0:T(8,128)(2,1)}, bf16[8,48,1536]{2,1,0:T(8,128)(2,1)}, u32[]{:S(2)}, u32[]{:S(2)}) collective-permute-start(bf16[8,48,1536]{2,1,0:T(8,128)(2,1)} %maximum_select_fusion.1), channel_id=1, source_target_pairs={{0,4},{1,5},{2,6},{3,7},{4,0},{5,1},{6,2},{7,3},{8,12},{9,13},{10,... | collective-permute-start | bytes 3538952 | tf_op jit(solution)/shard_map/ppermute | solution.py:46
  126.4 6.2 %collective-permute-start.5 = (bf16[768,1536]{1,0:T(8,128)(2,1)}, bf16[768,1536]{1,0:T(8,128)(2,1)}, u32[]{:S(2)}, u32[]{:S(2)}) collective-permute-start(bf16[768,1536]{1,0:T(8,128)(2,1)} %bitcast.14), channel_id=1, source_target_pairs={{0,16},{16,0},{32,48},{48,32},{64,80},{80,64},{96,112},{112,96},{1... | collective-permute-start | bytes 7077896 | tf_op jit(solution)/shard_map/ppermute | solution.py:40
  135.4 3.1 %copy-start.2 = (f32[512,1536]{1,0:T(8,128)S(1)}, f32[512,1536]{1,0:T(8,128)}, u32[]{:S(2)}) copy-start(f32[512,1536]{1,0:T(8,128)} %fusion.7) | copy-start | bytes 9437188
  135.9 6.5 %copy-start.5 = (bf16[16,2,48,1536]{3,2,1,0:T(8,128)(2,1)}, bf16[16,2,48,1536]{3,2,1,0:T(8,128)(2,1)S(1)}, u32[]{:S(2)}) copy-start(bf16[16,2,48,1536]{3,2,1,0:T(8,128)(2,1)S(1)} %pad_maximum_fusion) | copy-start | bytes 14155780
  138.5 3.9 %copy-start.3 = (bf16[512,1536]{1,0:T(8,128)(2,1)S(1)}, bf16[512,1536]{1,0:T(8,128)(2,1)}, u32[]{:S(2)}) copy-start(bf16[512,1536]{1,0:T(8,128)(2,1)} %param.6) | copy-start | bytes 4718596
  148.0 5.7 %collective-permute-start.6 = (f32[6,1536]{1,0:T(8,128)S(1)}, f32[6,1536]{1,0:T(8,128)S(1)}, u32[]{:S(2)}, u32[]{:S(2)}) collective-permute-start(f32[6,1536]{1,0:T(8,128)S(1)} %concatenate.45), channel_id=1, source_target_pairs={{0,1},{1,0},{2,3},{3,2},{4,5},{5,4},{6,7},{7,6},{8,9},{9,8},{10,11... | collective-permute-start | bytes 110600 | tf_op jit(solution)/shard_map/ppermute | solution.py:34
  153.8 9.1 %collective-permute-start.7 = (f32[6,1536]{1,0:T(8,128)S(1)}, f32[6,1536]{1,0:T(8,128)S(1)}, u32[]{:S(2)}, u32[]{:S(2)}) collective-permute-start(f32[6,1536]{1,0:T(8,128)S(1)} %add.113), channel_id=1, source_target_pairs={{0,2},{1,3},{2,0},{3,1},{4,6},{5,7},{6,4},{7,5},{8,10},{9,11},{10,... | collective-permute-start | bytes 110600 | tf_op jit(solution)/shard_map/ppermute | solution.py:34
  162.9 10.4 %collective-permute-start.8 = (f32[6,1536]{1,0:T(8,128)S(1)}, f32[6,1536]{1,0:T(8,128)S(1)}, u32[]{:S(2)}, u32[]{:S(2)}) collective-permute-start(f32[6,1536]{1,0:T(8,128)S(1)} %add.114), channel_id=1, source_target_pairs={{0,4},{1,5},{2,6},{3,7},{4,0},{5,1},{6,2},{7,3},{8,12},{9,13},{10,... | collective-permute-start | bytes 110600 | tf_op jit(solution)/shard_map/ppermute | solution.py:34
  163.0 12.5 %copy-start.6 = (bf16[16,2,48,1536]{3,2,1,0:T(8,128)(2,1)S(1)}, bf16[16,2,48,1536]{3,2,1,0:T(8,128)(2,1)}, u32[]{:S(2)}) copy-start(bf16[16,2,48,1536]{3,2,1,0:T(8,128)(2,1)} %copy-done.5) | copy-start | bytes 14155780
  173.3 6.4 %collective-permute-start.9 = (f32[6,1536]{1,0:T(8,128)S(1)}, f32[6,1536]{1,0:T(8,128)S(1)}, u32[]{:S(2)}, u32[]{:S(2)}) collective-permute-start(f32[6,1536]{1,0:T(8,128)S(1)} %add.115), channel_id=1, source_target_pairs={{0,8},{1,9},{2,10},{3,11},{4,12},{5,13},{6,14},{7,15},{8,0},{9,1},... | collective-permute-start | bytes 110600 | tf_op jit(solution)/shard_map/ppermute | solution.py:34
  179.8 3.2 %collective-permute-start.10 = (f32[6,1536]{1,0:T(8,128)S(1)}, f32[6,1536]{1,0:T(8,128)S(1)}, u32[]{:S(2)}, u32[]{:S(2)}) collective-permute-start(f32[6,1536]{1,0:T(8,128)S(1)} %add.116), channel_id=1, source_target_pairs={{0,16},{16,0},{32,48},{48,32},{64,80},{80,64},{96,112},{112,96},{1... | collective-permute-start | bytes 110600 | tf_op jit(solution)/shard_map/ppermute | solution.py:34
  183.0 3.2 %collective-permute-start.11 = (f32[6,1536]{1,0:T(8,128)S(1)}, f32[6,1536]{1,0:T(8,128)S(1)}, u32[]{:S(2)}, u32[]{:S(2)}) collective-permute-start(f32[6,1536]{1,0:T(8,128)S(1)} %add.121), channel_id=1, source_target_pairs={{0,32},{16,48},{32,0},{48,16},{64,96},{80,112},{96,64},{112,80},{1... | collective-permute-start | bytes 110600 | tf_op jit(solution)/shard_map/ppermute | solution.py:34
  186.2 4.5 %collective-permute-start.12 = (f32[6,1536]{1,0:T(8,128)S(1)}, f32[6,1536]{1,0:T(8,128)S(1)}, u32[]{:S(2)}, u32[]{:S(2)}) collective-permute-start(f32[6,1536]{1,0:T(8,128)S(1)} %add.122), channel_id=1, source_target_pairs={{0,64},{16,80},{32,96},{48,112},{64,0},{80,16},{96,32},{112,48},{1... | collective-permute-start | bytes 110600 | tf_op jit(solution)/shard_map/ppermute | solution.py:34
  190.8 3.2 %collective-permute-start.13 = (f32[6,1536]{1,0:T(8,128)S(1)}, f32[6,1536]{1,0:T(8,128)S(1)}, u32[]{:S(2)}, u32[]{:S(2)}) collective-permute-start(f32[6,1536]{1,0:T(8,128)S(1)} %add.123), channel_id=1, source_target_pairs={{0,128},{16,144},{32,160},{48,176},{64,192},{80,208},{96,224},{112... | collective-permute-start | bytes 110600 | tf_op jit(solution)/shard_map/ppermute | solution.py:34
  194.0 5.9 %collective-permute-start.14 = (f32[48,1536]{1,0:T(8,128)}, f32[48,1536]{1,0:T(8,128)S(1)}, u32[]{:S(2)}, u32[]{:S(2)}) collective-permute-start(f32[48,1536]{1,0:T(8,128)} %reduce-scatter.2.cloned.1.call-done), channel_id=1, source_target_pairs={{0,32},{16,48},{32,0},{48,16},{64,96},{80,112},{96,64},{112,80},{1... | collective-permute-start | bytes 884744 | tf_op jit(solution)/shard_map/ppermute | solution.py:34
  200.9 8.1 %collective-permute-start.15 = (f32[48,1536]{1,0:T(8,128)S(1)}, f32[48,1536]{1,0:T(8,128)S(1)}, u32[]{:S(2)}, u32[]{:S(2)}) collective-permute-start(f32[48,1536]{1,0:T(8,128)S(1)} %add.125), channel_id=1, source_target_pairs={{0,64},{16,80},{32,96},{48,112},{64,0},{80,16},{96,32},{112,48},{1... | collective-permute-start | bytes 884744 | tf_op jit(solution)/shard_map/ppermute | solution.py:34
  209.1 5.7 %collective-permute-start.16 = (f32[48,1536]{1,0:T(8,128)S(1)}, f32[48,1536]{1,0:T(8,128)S(1)}, u32[]{:S(2)}, u32[]{:S(2)}) collective-permute-start(f32[48,1536]{1,0:T(8,128)S(1)} %add.126), channel_id=1, source_target_pairs={{0,128},{16,144},{32,160},{48,176},{64,192},{80,208},{96,224},{112... | collective-permute-start | bytes 884744 | tf_op jit(solution)/shard_map/ppermute | solution.py:34
  214.8 7.4 %collective-permute-start.17 = (f32[48,1536]{1,0:T(8,128)S(1)}, f32[48,1536]{1,0:T(8,128)S(1)}, u32[]{:S(2)}, u32[]{:S(2)}) collective-permute-start(f32[48,1536]{1,0:T(8,128)S(1)} %add.127), channel_id=1, source_target_pairs={{0,16},{16,0},{32,48},{48,32},{64,80},{80,64},{96,112},{112,96},{1... | collective-permute-start | bytes 884744 | tf_op jit(solution)/shard_map/ppermute | solution.py:40
Sparse Core Ops, SparseCore 0:
  87.9 98.1 reduce-scatter.1

commit v6 on v4

--- a/solution.py
+++ b/solution.py
@@ -132,11 +132,13 @@
         )
     small = jnp.concatenate([jnp.stack(kernel_rows), gain_grad[None]], axis=0)
     small = butterfly(small, "fsdp", (1, 2, 4, 8))
-    small = butterfly(small, "dp", (1, 2, 4, 8))
+    small = butterfly(small, "dp", (1,))
     shard_sum, small, output, grad_hidden = lax.optimization_barrier(
         (shard_sum, small, output, grad_hidden)
     )
-    half_sum = butterfly(shard_sum, "dp", (2, 4, 8))
+    joined = butterfly(jnp.concatenate([shard_sum, small], axis=0), "dp", (2, 4, 8))
+    half_sum = joined[: shard_sum.shape[0]]
+    small = joined[shard_sum.shape[0] :]
     other_sum = sibling(half_sum)
     weight_sum = jnp.where(
         core == 0,

time: 222 us -> 214 us (0.964)
  waiting for transfers between devices: 97.1 us -> 91.4 us
  starting transfers between devices: 40.3 us -> 37.3 us
    ppermute x11 -> x8, waiting for transfers between devices: 36 us -> 29.2 us  [butterfly(): x = x + lax.ppermute(x, axis, pairs)]
    ppermute x11 -> x8, starting transfers between devices: 16.8 us -> 14 us  [butterfly(): x = x + lax.ppermute(x, axis, pairs)]
  transfers between devices with their start and end apart: 19 -> 16, of which waited for: 14 -> 12; matrix products, arithmetic and copies ran while one was open for 26% -> 26% of each run, Pallas kernels for 0% -> 0%
where the time goes in v6:
time: 214 us; the launch traced here: 213 us
  waiting for transfers between devices  91.4 us (43%)
  other arithmetic  47.5 us (22%)
  starting transfers between devices  37.3 us (17%)
  between operations  14.4 us (7%)
  local copies, waits for them, and re-layouts  11.5 us (5%)
  matrix products  10.9 us (5%)
    ppermute x4, waiting for transfers between devices, doubling_step(): received = lax.ppermute(held, axis, [(i, i ^ mask) for i in range(size)])  48.5 us
    ppermute x8, waiting for transfers between devices, butterfly(): x = x + lax.ppermute(x, axis, pairs)  29.2 us
    ppermute x4, starting transfers between devices, doubling_step(): received = lax.ppermute(held, axis, [(i, i ^ mask) for i in range(size)])  15.4 us
    ppermute x8, starting transfers between devices, butterfly(): x = x + lax.ppermute(x, axis, pairs)  14 us
    ppermute x3, waiting for transfers between devices, sibling(): return lax.ppermute(x, 'dp', [(i, i ^ 1) for i in range(size)])  12.6 us
    add x1, other arithmetic, shards(): grad_hidden + conv_kernel[k] * (back_views[count - 1 - k] * taps[count -...  10.3 us
    add x1, other arithmetic, shards(): mixed + conv_kernel[k] * views[k].astype(jnp.float32) * taps[k][:, None]  8.63 us
    ppermute x3, starting transfers between devices, sibling(): return lax.ppermute(x, 'dp', [(i, i ^ 1) for i in range(size)])  7.76 us
  transfers between devices with their start and end apart: 16, of which 12 were waited for; matrix products, arithmetic and copies ran while one was open for 26% of the time, Pallas kernels for 0%

profile of v6, /device:TPU:1, one launch (start us, length us, event | category | flops | bytes accessed | tf_op | source)
XLA Modules:
  0.0 212.9 jit_solution(670868751096777315)
XLA Ops:
  8.3 7.8 %collective-permute-start = (bf16[1,48,1536]{2,1,0:T(8,128)(2,1)S(1)}, bf16[1,48,1536]{2,1,0:T(8,128)(2,1)S(1)}, u32[]{:S(2)}, u32[]{:S(2)}) collective-permute-start(bf16[1,48,1536]{2,1,0:T(8,128)(2,1)S(1)} %dynamic-slice_bitcast_fusion), channel_id=1, source_target_pairs={{0,2},{1,3},{2,0},{3,1},{4,6},{5,7},{6,4},{7,5},{8,10},{9,11},{10,... | collective-permute-start | bytes 442376 | tf_op jit(solution)/shard_map/ppermute | solution.py:46
  20.3 3.0 %collective-permute-start.1 = (bf16[2,48,1536]{2,1,0:T(8,128)(2,1)S(1)}, bf16[2,48,1536]{2,1,0:T(8,128)(2,1)S(1)}, u32[]{:S(2)}, u32[]{:S(2)}) collective-permute-start(bf16[2,48,1536]{2,1,0:T(8,128)(2,1)S(1)} %maximum_select_fusion.4), channel_id=1, source_target_pairs={{0,8},{1,9},{2,10},{3,11},{4,12},{5,13},{6,14},{7,15},{8,0},{9,1},... | collective-permute-start | bytes 884744 | tf_op jit(solution)/shard_map/ppermute | solution.py:46
  23.3 8.6 %fusion.7 = f32[512,1536]{1,0:T(8,128)} fusion(bf16[512,1536]{1,0:T(8,128)(2,1)} %param.6, f32[512]{0:T(512)S(1)} %bitcast.56, f32[1536]{0:T(1024)S(1)} %get-tuple-element.42, f32[512]{0:T(512)S(1)} %bitcast.59, f32[1536]{0:T(1024)S(1)} %get-tuple-element.43, f32[512]{0:T(512)S(1)} %bitcast.48, f32[1536]{0:T(1024)S(1)} %get-tuple-element.40, ...), kind=kLoop, calls=%fused_computation.19 | loop fusion | flops 14942208 | bytes 4759552 | tf_op jit(solution)/shard_map/add | solution.py:84
  32.8 4.1 %collective-permute-start.2 = (bf16[4,48,1536]{2,1,0:T(8,128)(2,1)}, bf16[4,48,1536]{2,1,0:T(8,128)(2,1)}, u32[]{:S(2)}, u32[]{:S(2)}) collective-permute-start(bf16[4,48,1536]{2,1,0:T(8,128)(2,1)} %maximum_select_fusion.2), channel_id=1, source_target_pairs={{0,1},{1,0},{2,3},{3,2},{4,5},{5,4},{6,7},{7,6},{8,9},{9,8},{10,11... | collective-permute-start | bytes 1769480 | tf_op jit(solution)/shard_map/ppermute | solution.py:46
  37.0 2.1 reduce_sum.100
  39.1 2.5 %multiply_reduce_fusion.2 = f32[512]{0:T(512)S(1)} fusion(f32[512,1536]{1,0:T(8,128)} %fusion.7, f32[512]{0:T(512)S(1)} %broadcast_multiply_fusion.2), kind=kLoop, calls=%fused_computation.35 | loop fusion | flops 2358784 | bytes 3149824 | tf_op jit(solution)/shard_map/reduce_sum | solution.py:88
  43.1 1.6 copy.18
  49.0 13.5 %collective-permute-done.2 = bf16[4,48,1536]{2,1,0:T(8,128)(2,1)} collective-permute-done((bf16[4,48,1536]{2,1,0:T(8,128)(2,1)}, bf16[4,48,1536]{2,1,0:T(8,128)(2,1)}, u32[]{:S(2)}, u32[]{:S(2)}) %collective-permute-start.2) | collective-permute-done | bytes 589856 | tf_op jit(solution)/shard_map/ppermute | solution.py:46
  62.5 2.8 %maximum_select_fusion.1 = bf16[8,48,1536]{2,1,0:T(8,128)(2,1)} fusion(bf16[4,48,1536]{2,1,0:T(8,128)(2,1)} %maximum_select_fusion.2, bf16[4,48,1536]{2,1,0:T(8,128)(2,1)} %collective-permute-done.2, pred[]{:T(512)S(6)} %ne.18), kind=kLoop, calls=%fused_computation.44 | loop fusion | flops 1769472 | bytes 2359297 | tf_op jit(solution)/shard_map/jit(_where)/select_n | solution.py:47
  65.3 1.7 collective-permute-start.3
  67.1 7.5 %collective-permute-done.3 = f32[768,1536]{1,0:T(8,128)S(1)} collective-permute-done((f32[768,1536]{1,0:T(8,128)S(1)}, f32[768,1536]{1,0:T(8,128)S(1)}, u32[]{:S(2)}, u32[]{:S(2)}) %collective-permute-start.3) | collective-permute-done | bytes 4718624 | tf_op jit(solution)/shard_map/ppermute | solution.py:40
  74.6 3.1 %add.102 = f32[768,1536]{1,0:T(8,128)} add(f32[768,1536]{1,0:T(8,128)S(1)} %fusion.32, f32[768,1536]{1,0:T(8,128)S(1)} %collective-permute-done.3) | non-fusion elementwise | flops 1179648 | bytes 14155776 | tf_op jit(solution)/shard_map/add | solution.py:103
  78.2 35.0 %collective-permute-done.4 = bf16[8,48,1536]{2,1,0:T(8,128)(2,1)} collective-permute-done((bf16[8,48,1536]{2,1,0:T(8,128)(2,1)}, bf16[8,48,1536]{2,1,0:T(8,128)(2,1)}, u32[]{:S(2)}, u32[]{:S(2)}) %collective-permute-start.4) | collective-permute-done | bytes 1179680 | tf_op jit(solution)/shard_map/ppermute | solution.py:46
  113.2 2.6 %maximum_select_fusion = bf16[16,48,1536]{2,1,0:T(8,128)(2,1)S(1)} fusion(bf16[8,48,1536]{2,1,0:T(8,128)(2,1)} %maximum_select_fusion.1, bf16[8,48,1536]{2,1,0:T(8,128)(2,1)} %collective-permute-done.4, pred[]{:T(512)S(6)} %ne.22), kind=kLoop, calls=%fused_computation.38 | loop fusion | flops 3538944 | bytes 4718593 | tf_op jit(solution)/shard_map/jit(_where)/select_n | solution.py:47
  115.7 1.6 copy.19
  117.3 1.6 collective-permute-start.5
  118.9 4.5 %collective-permute-done.5 = bf16[768,1536]{1,0:T(8,128)(2,1)} collective-permute-done((bf16[768,1536]{1,0:T(8,128)(2,1)}, bf16[768,1536]{1,0:T(8,128)(2,1)}, u32[]{:S(2)}, u32[]{:S(2)}) %collective-permute-start.5) | collective-permute-done | bytes 2359328 | tf_op jit(solution)/shard_map/ppermute | solution.py:40
  123.4 2.7 %broadcast_select_fusion.1 = (bf16[768,1536]{1,0:T(8,128)(2,1)S(1)}, bf16[768,1536]{1,0:T(8,128)(2,1)S(1)}) fusion(bf16[768,1536]{1,0:T(8,128)(2,1)} %collective-permute-done.5, pred[]{:T(512)S(6)} %eq.24, bf16[2,2,2,2,48,1536]{5,4,3,2,1,0:T(8,128)(2,1)} %copy.19), kind=kLoop, calls=%fused_computation.40 | loop fusion | flops 2359296 | bytes 9437185 | tf_op jit(solution)/shard_map/jit(_where)/select_n | solution.py:108
  126.6 2.7 %copy-done.3 = f32[512,1536]{1,0:T(8,128)S(1)} copy-done((f32[512,1536]{1,0:T(8,128)S(1)}, f32[512,1536]{1,0:T(8,128)}, u32[]{:S(2)}) %copy-start.3) | copy-done | bytes 3145752
  129.3 3.8 %multiply_reduce_fusion = (f32[1536]{0:T(1024)S(1)}, f32[512]{0:T(512)S(1)}, f32[512]{0:T(512)S(1)}, f32[512,1536]{1,0:T(8,128)S(1)}) fusion(f32[512,1536]{1,0:T(8,128)S(1)} %copy-done.3, f32[512]{0:T(512)S(1)} %add_rsqrt_fusion, f32[512]{0:T(512)S(1)} %broadcast_multiply_fusion.2, f32[1536]{0:T(1024)S(1)} %copy-done.7, f32[512]{0:T(512)S(1)} %bitcast.50, ...), kind=kOutput, calls=%fused_computation.30 | convolution fusion | flops 2430072320 | bytes 12605440 | tf_op jit(solution)/shard_map/dot_general | solution.py:112
  133.2 5.5 %fusion.16 = (f32[1536]{0:T(1024)S(1)}, f32[1536]{0:T(1024)S(1)}, f32[1536]{0:T(1024)S(1)}, f32[1536]{0:T(1024)S(1)}, f32[1536]{0:T(1024)S(1)}, /*index=5*/f32[512,1536]{1,0:T(8,128)}) fusion(f32[512]{0:T(512)S(1)} %bitcast.57, bf16[512,1536]{1,0:T(8,128)(2,1)S(1)} %copy-done.4, f32[512]{0:T(512)S(1)} %bitcast.60, f32[512]{0:T(512)S(1)} %bitcast.51, ...), kind=kLoop, calls=%fused_computation.28 | loop fusion | flops 21225984 | bytes 11065344 | tf_op jit(solution)/shard_map/reduce_sum | solution.py:126
  138.9 6.5 %collective-permute-done.6 = f32[6,1536]{1,0:T(8,128)S(1)} collective-permute-done((f32[6,1536]{1,0:T(8,128)S(1)}, f32[6,1536]{1,0:T(8,128)S(1)}, u32[]{:S(2)}, u32[]{:S(2)}) %collective-permute-start.6) | collective-permute-done | bytes 36896 | tf_op jit(solution)/shard_map/ppermute | solution.py:34
  145.4 5.6 %collective-permute-start.7 = (f32[6,1536]{1,0:T(8,128)S(1)}, f32[6,1536]{1,0:T(8,128)S(1)}, u32[]{:S(2)}, u32[]{:S(2)}) collective-permute-start(f32[6,1536]{1,0:T(8,128)S(1)} %add.104), channel_id=1, source_target_pairs={{0,2},{1,3},{2,0},{3,1},{4,6},{5,7},{6,4},{7,5},{8,10},{9,11},{10,... | collective-permute-start | bytes 110600 | tf_op jit(solution)/shard_map/ppermute | solution.py:34
  152.8 2.7 %collective-permute-done.8 = f32[6,1536]{1,0:T(8,128)S(1)} collective-permute-done((f32[6,1536]{1,0:T(8,128)S(1)}, f32[6,1536]{1,0:T(8,128)S(1)}, u32[]{:S(2)}, u32[]{:S(2)}) %collective-permute-start.8) | collective-permute-done | bytes 36896 | tf_op jit(solution)/shard_map/ppermute | solution.py:34
  156.4 10.3 %multiply_add_fusion = f32[512,1536]{1,0:T(8,128)} fusion(f32[512,1536]{1,0:T(8,128)} %get-tuple-element.44, f32[512]{0:T(512)S(1)} %bitcast.58, f32[1536]{0:T(1024)S(1)} %get-tuple-element.42, f32[512]{0:T(512)S(1)} %bitcast.61, f32[1536]{0:T(1024)S(1)} %get-tuple-element.43, f32[512]{0:T(512)S(1)} %bitcast.52, f32[1536]{0:T(1024)S(1)} %get-tuple-element.40, ...), kind=kLoop, calls=%fused_computation.29 | loop fusion | flops 11010048 | bytes 6332416 | tf_op jit(solution)/shard_map/add | solution.py:130
  166.7 2.6 %collective-permute-start.10 = (f32[6,1536]{1,0:T(8,128)S(1)}, f32[6,1536]{1,0:T(8,128)S(1)}, u32[]{:S(2)}, u32[]{:S(2)}) collective-permute-start(f32[6,1536]{1,0:T(8,128)S(1)} %add.107), channel_id=1, source_target_pairs={{0,16},{16,0},{32,48},{48,32},{64,80},{80,64},{96,112},{112,96},{1... | collective-permute-start | bytes 110600 | tf_op jit(solution)/shard_map/ppermute | solution.py:34
  169.3 4.3 %fusion.34 = f32[512,1536]{1,0:T(8,128)} fusion(bf16[512,1536]{1,0:T(8,128)(2,1)S(1)} %multiply_convert_fusion, bf16[1536,1536]{1,0:T(8,128)(2,1)S(1)} %bitcast.45), kind=kOutput, calls=%fused_computation.93 | convolution fusion | flops 2415919104 | bytes 9437184 | tf_op jit(solution)/shard_map/dot_general | solution.py:111
  177.2 6.4 %collective-permute-done.11 = f32[54,1536]{1,0:T(8,128)S(1)} collective-permute-done((f32[54,1536]{1,0:T(8,128)S(1)}, f32[54,1536]{1,0:T(8,128)S(1)}, u32[]{:S(2)}, u32[]{:S(2)}) %collective-permute-start.11) | collective-permute-done | bytes 331808 | tf_op jit(solution)/shard_map/ppermute | solution.py:34
  183.6 3.0 %collective-permute-start.12 = (f32[54,1536]{1,0:T(8,128)S(1)}, f32[54,1536]{1,0:T(8,128)S(1)}, u32[]{:S(2)}, u32[]{:S(2)}) collective-permute-start(f32[54,1536]{1,0:T(8,128)S(1)} %add.113), channel_id=1, source_target_pairs={{0,64},{16,80},{32,96},{48,112},{64,0},{80,16},{96,32},{112,48},{1... | collective-permute-start | bytes 995336 | tf_op jit(solution)/shard_map/ppermute | solution.py:34
  186.6 6.0 %collective-permute-done.12 = f32[54,1536]{1,0:T(8,128)S(1)} collective-permute-done((f32[54,1536]{1,0:T(8,128)S(1)}, f32[54,1536]{1,0:T(8,128)S(1)}, u32[]{:S(2)}, u32[]{:S(2)}) %collective-permute-start.12) | collective-permute-done | bytes 331808 | tf_op jit(solution)/shard_map/ppermute | solution.py:34
  192.8 6.1 %collective-permute-done.13 = f32[54,1536]{1,0:T(8,128)S(1)} collective-permute-done((f32[54,1536]{1,0:T(8,128)S(1)}, f32[54,1536]{1,0:T(8,128)S(1)}, u32[]{:S(2)}, u32[]{:S(2)}) %collective-permute-start.13) | collective-permute-done | bytes 331808 | tf_op jit(solution)/shard_map/ppermute | solution.py:34
  199.6 4.4 %collective-permute-start.14 = (f32[48,1536]{1,0:T(8,128)S(1)}, f32[48,1536]{1,0:T(8,128)S(1)}, u32[]{:S(2)}, u32[]{:S(2)}) collective-permute-start(f32[48,1536]{1,0:T(8,128)S(1)} %slice.144), channel_id=1, source_target_pairs={{0,16},{16,0},{32,48},{48,32},{64,80},{80,64},{96,112},{112,96},{1... | collective-permute-start | bytes 884744 | tf_op jit(solution)/shard_map/ppermute | solution.py:40
  (76 shorter events, 22.3 us)
Async XLA Ops:
  7.2 39.0 %copy-start = (bf16[512,1536]{1,0:T(8,128)(2,1)S(1)}, bf16[512,1536]{1,0:T(8,128)(2,1)}, u32[]{:S(2)}) copy-start(bf16[512,1536]{1,0:T(8,128)(2,1)} %param.7) | copy-start | bytes 4718596
  7.2 167.5 %reduce-scatter.2.cloned.1.call-start = ((), (), s32[]{:S(2)}) async-start(), calls=%async_computation.1 | async-start | bytes 5013504 | tf_op jit(solution)/shard_map/reduce_scatter | solution.py:104
  8.3 11.9 %collective-permute-start = (bf16[1,48,1536]{2,1,0:T(8,128)(2,1)S(1)}, bf16[1,48,1536]{2,1,0:T(8,128)(2,1)S(1)}, u32[]{:S(2)}, u32[]{:S(2)}) collective-permute-start(bf16[1,48,1536]{2,1,0:T(8,128)(2,1)S(1)} %dynamic-slice_bitcast_fusion), channel_id=1, source_target_pairs={{0,2},{1,3},{2,0},{3,1},{4,6},{5,7},{6,4},{7,5},{8,10},{9,11},{10,... | collective-permute-start | bytes 442376 | tf_op jit(solution)/shard_map/ppermute | solution.py:46
  20.3 11.7 %collective-permute-start.1 = (bf16[2,48,1536]{2,1,0:T(8,128)(2,1)S(1)}, bf16[2,48,1536]{2,1,0:T(8,128)(2,1)S(1)}, u32[]{:S(2)}, u32[]{:S(2)}) collective-permute-start(bf16[2,48,1536]{2,1,0:T(8,128)(2,1)S(1)} %maximum_select_fusion.4), channel_id=1, source_target_pairs={{0,8},{1,9},{2,10},{3,11},{4,12},{5,13},{6,14},{7,15},{8,0},{9,1},... | collective-permute-start | bytes 884744 | tf_op jit(solution)/shard_map/ppermute | solution.py:46
  32.8 8.8 %copy-start.7 = (f32[1536]{0:T(1024)S(1)}, f32[1536]{0:T(1024)}, u32[]{:S(2)}) copy-start(f32[1536]{0:T(1024)} %param.10) | copy-start | bytes 18436
  32.8 29.7 %collective-permute-start.2 = (bf16[4,48,1536]{2,1,0:T(8,128)(2,1)}, bf16[4,48,1536]{2,1,0:T(8,128)(2,1)}, u32[]{:S(2)}, u32[]{:S(2)}) collective-permute-start(bf16[4,48,1536]{2,1,0:T(8,128)(2,1)} %maximum_select_fusion.2), channel_id=1, source_target_pairs={{0,1},{1,0},{2,3},{3,2},{4,5},{5,4},{6,7},{7,6},{8,9},{9,8},{10,11... | collective-permute-start | bytes 1769480 | tf_op jit(solution)/shard_map/ppermute | solution.py:46
  39.1 2.8 %copy-start.2 = (f32[512,1536]{1,0:T(8,128)S(1)}, f32[512,1536]{1,0:T(8,128)}, u32[]{:S(2)}) copy-start(f32[512,1536]{1,0:T(8,128)} %fusion.7) | copy-start | bytes 9437188
  65.3 9.2 %collective-permute-start.3 = (f32[768,1536]{1,0:T(8,128)S(1)}, f32[768,1536]{1,0:T(8,128)S(1)}, u32[]{:S(2)}, u32[]{:S(2)}) collective-permute-start(f32[768,1536]{1,0:T(8,128)S(1)} %fusion.33), channel_id=1, source_target_pairs={{0,16},{16,0},{32,48},{48,32},{64,80},{80,64},{96,112},{112,96},{1... | collective-permute-start | bytes 14155784 | tf_op jit(solution)/shard_map/ppermute | solution.py:40
  77.7 35.5 %collective-permute-start.4 = (bf16[8,48,1536]{2,1,0:T(8,128)(2,1)}, bf16[8,48,1536]{2,1,0:T(8,128)(2,1)}, u32[]{:S(2)}, u32[]{:S(2)}) collective-permute-start(bf16[8,48,1536]{2,1,0:T(8,128)(2,1)} %maximum_select_fusion.1), channel_id=1, source_target_pairs={{0,4},{1,5},{2,6},{3,7},{4,0},{5,1},{6,2},{7,3},{8,12},{9,13},{10,... | collective-permute-start | bytes 3538952 | tf_op jit(solution)/shard_map/ppermute | solution.py:46
  117.3 6.1 %collective-permute-start.5 = (bf16[768,1536]{1,0:T(8,128)(2,1)}, bf16[768,1536]{1,0:T(8,128)(2,1)}, u32[]{:S(2)}, u32[]{:S(2)}) collective-permute-start(bf16[768,1536]{1,0:T(8,128)(2,1)} %bitcast.14), channel_id=1, source_target_pairs={{0,16},{16,0},{32,48},{48,32},{64,80},{80,64},{96,112},{112,96},{1... | collective-permute-start | bytes 7077896 | tf_op jit(solution)/shard_map/ppermute | solution.py:40
  126.2 3.1 %copy-start.3 = (f32[512,1536]{1,0:T(8,128)S(1)}, f32[512,1536]{1,0:T(8,128)}, u32[]{:S(2)}) copy-start(f32[512,1536]{1,0:T(8,128)} %fusion.7) | copy-start | bytes 9437188
  126.6 6.5 %copy-start.5 = (bf16[16,2,48,1536]{3,2,1,0:T(8,128)(2,1)}, bf16[16,2,48,1536]{3,2,1,0:T(8,128)(2,1)S(1)}, u32[]{:S(2)}) copy-start(bf16[16,2,48,1536]{3,2,1,0:T(8,128)(2,1)S(1)} %pad_maximum_fusion) | copy-start | bytes 14155780
  129.3 3.9 %copy-start.4 = (bf16[512,1536]{1,0:T(8,128)(2,1)S(1)}, bf16[512,1536]{1,0:T(8,128)(2,1)}, u32[]{:S(2)}) copy-start(bf16[512,1536]{1,0:T(8,128)(2,1)} %param.6) | copy-start | bytes 4718596
  138.8 6.6 %collective-permute-start.6 = (f32[6,1536]{1,0:T(8,128)S(1)}, f32[6,1536]{1,0:T(8,128)S(1)}, u32[]{:S(2)}, u32[]{:S(2)}) collective-permute-start(f32[6,1536]{1,0:T(8,128)S(1)} %concatenate.48), channel_id=1, source_target_pairs={{0,1},{1,0},{2,3},{3,2},{4,5},{5,4},{6,7},{7,6},{8,9},{9,8},{10,11... | collective-permute-start | bytes 110600 | tf_op jit(solution)/shard_map/ppermute | solution.py:34
  145.4 7.1 %collective-permute-start.7 = (f32[6,1536]{1,0:T(8,128)S(1)}, f32[6,1536]{1,0:T(8,128)S(1)}, u32[]{:S(2)}, u32[]{:S(2)}) collective-permute-start(f32[6,1536]{1,0:T(8,128)S(1)} %add.104), channel_id=1, source_target_pairs={{0,2},{1,3},{2,0},{3,1},{4,6},{5,7},{6,4},{7,5},{8,10},{9,11},{10,... | collective-permute-start | bytes 110600 | tf_op jit(solution)/shard_map/ppermute | solution.py:34
  152.5 3.0 %collective-permute-start.8 = (f32[6,1536]{1,0:T(8,128)S(1)}, f32[6,1536]{1,0:T(8,128)S(1)}, u32[]{:S(2)}, u32[]{:S(2)}) collective-permute-start(f32[6,1536]{1,0:T(8,128)S(1)} %add.105), channel_id=1, source_target_pairs={{0,4},{1,5},{2,6},{3,7},{4,0},{5,1},{6,2},{7,3},{8,12},{9,13},{10,... | collective-permute-start | bytes 110600 | tf_op jit(solution)/shard_map/ppermute | solution.py:34
  155.5 11.2 %collective-permute-start.9 = (f32[6,1536]{1,0:T(8,128)S(1)}, f32[6,1536]{1,0:T(8,128)S(1)}, u32[]{:S(2)}, u32[]{:S(2)}) collective-permute-start(f32[6,1536]{1,0:T(8,128)S(1)} %add.106), channel_id=1, source_target_pairs={{0,8},{1,9},{2,10},{3,11},{4,12},{5,13},{6,14},{7,15},{8,0},{9,1},... | collective-permute-start | bytes 110600 | tf_op jit(solution)/shard_map/ppermute | solution.py:34
  156.4 12.9 %copy-start.6 = (bf16[16,2,48,1536]{3,2,1,0:T(8,128)(2,1)S(1)}, bf16[16,2,48,1536]{3,2,1,0:T(8,128)(2,1)}, u32[]{:S(2)}) copy-start(bf16[16,2,48,1536]{3,2,1,0:T(8,128)(2,1)} %copy-done.5) | copy-start | bytes 14155780
  166.7 6.8 %collective-permute-start.10 = (f32[6,1536]{1,0:T(8,128)S(1)}, f32[6,1536]{1,0:T(8,128)S(1)}, u32[]{:S(2)}, u32[]{:S(2)}) collective-permute-start(f32[6,1536]{1,0:T(8,128)S(1)} %add.107), channel_id=1, source_target_pairs={{0,16},{16,0},{32,48},{48,32},{64,80},{80,64},{96,112},{112,96},{1... | collective-permute-start | bytes 110600 | tf_op jit(solution)/shard_map/ppermute | solution.py:34
  169.3 36.8 %copy-start.1 = (bf16[512,1536]{1,0:T(8,128)(2,1)S(1)}, bf16[512,1536]{1,0:T(8,128)(2,1)}, u32[]{:S(2)}) copy-start(bf16[512,1536]{1,0:T(8,128)(2,1)} %param.7) | copy-start | bytes 4718596
  175.7 7.8 %collective-permute-start.11 = (f32[54,1536]{1,0:T(8,128)S(1)}, f32[54,1536]{1,0:T(8,128)S(1)}, u32[]{:S(2)}, u32[]{:S(2)}) collective-permute-start(f32[54,1536]{1,0:T(8,128)S(1)} %constant_dynamic-update-slice_fusion), channel_id=1, source_target_pairs={{0,32},{16,48},{32,0},{48,16},{64,96},{80,112},{96,64},{112,80},{1... | collective-permute-start | bytes 995336 | tf_op jit(solution)/shard_map/ppermute | solution.py:34
  183.6 9.1 %collective-permute-start.12 = (f32[54,1536]{1,0:T(8,128)S(1)}, f32[54,1536]{1,0:T(8,128)S(1)}, u32[]{:S(2)}, u32[]{:S(2)}) collective-permute-start(f32[54,1536]{1,0:T(8,128)S(1)} %add.113), channel_id=1, source_target_pairs={{0,64},{16,80},{32,96},{48,112},{64,0},{80,16},{96,32},{112,48},{1... | collective-permute-start | bytes 995336 | tf_op jit(solution)/shard_map/ppermute | solution.py:34
  192.7 6.2 %collective-permute-start.13 = (f32[54,1536]{1,0:T(8,128)S(1)}, f32[54,1536]{1,0:T(8,128)S(1)}, u32[]{:S(2)}, u32[]{:S(2)}) collective-permute-start(f32[54,1536]{1,0:T(8,128)S(1)} %add.114), channel_id=1, source_target_pairs={{0,128},{16,144},{32,160},{48,176},{64,192},{80,208},{96,224},{112... | collective-permute-start | bytes 995336 | tf_op jit(solution)/shard_map/ppermute | solution.py:34
  199.6 5.6 %collective-permute-start.14 = (f32[48,1536]{1,0:T(8,128)S(1)}, f32[48,1536]{1,0:T(8,128)S(1)}, u32[]{:S(2)}, u32[]{:S(2)}) collective-permute-start(f32[48,1536]{1,0:T(8,128)S(1)} %slice.144), channel_id=1, source_target_pairs={{0,16},{16,0},{32,48},{48,32},{64,80},{80,64},{96,112},{112,96},{1... | collective-permute-start | bytes 884744 | tf_op jit(solution)/shard_map/ppermute | solution.py:40
Sparse Core Ops, SparseCore 0:
  77.8 96.7 reduce-scatter.1

commit v7 on v5

--- a/solution.py
+++ b/solution.py
@@ -83,7 +83,6 @@
     for k in range(count):
         mixed = mixed + conv_kernel[k] * views[k].astype(jnp.float32) * taps[k][:, None]
     held, mixed = lax.optimization_barrier((held, mixed))
-    held = doubling_step(held, "fsdp", masks[2])
     centred = mixed - jnp.mean(mixed, axis=-1, keepdims=True)
     inverse = lax.rsqrt(jnp.mean(centred * centred, axis=-1, keepdims=True) + 1e-05)
     normed = centred * inverse
@@ -99,6 +98,7 @@
     chip_terms = keep_terms + sibling(send_terms)
     held, chip_terms, activation = lax.optimization_barrier((held, chip_terms, activation))
     shard_sum = lax.psum_scatter(chip_terms, "fsdp", scatter_dimension=0, tiled=True)
+    held = doubling_step(held, "fsdp", masks[2])
     held = doubling_step(held, "fsdp", masks[3])
     held, chip_terms = lax.optimization_barrier((held, chip_terms))
     gathered = doubling_order(held, masks)
@@ -130,12 +130,13 @@
         )
     small = jnp.concatenate([jnp.stack(kernel_rows), gain_grad[None]], axis=0)
     small = butterfly(small, "fsdp", (1, 2, 4, 8))
-    small, output, grad_hidden = lax.optimization_barrier((small, output, grad_hidden))
-    small = butterfly(small, "dp", (1, 2, 4, 8))
+    small = butterfly(small, "dp", (1,))
     shard_sum, small, output, grad_hidden = lax.optimization_barrier(
         (shard_sum, small, output, grad_hidden)
     )
-    half_sum = butterfly(shard_sum, "dp", (2, 4, 8))
+    joined = butterfly(jnp.concatenate([shard_sum, small], axis=0), "dp", (2, 4, 8))
+    half_sum = joined[: shard_sum.shape[0]]
+    small = joined[shard_sum.shape[0] :]
     other_sum = sibling(half_sum)
     weight_sum = jnp.where(
         core == 0,

time: 230 us -> 243 us (1.057)
  waiting for transfers between devices: 95.3 us -> 120 us
  starting transfers between devices: 45.8 us -> 39.3 us
  matrix products: 17.5 us -> 13 us
    ppermute x4, waiting for transfers between devices: 60.7 us -> 75.4 us  [doubling_step(): received = lax.ppermute(held, axis, [(i, i ^ mask) for i in range(size)])]
    ppermute x3, waiting for transfers between devices: 5.09 us -> 12.6 us  [sibling(): return lax.ppermute(x, 'dp', [(i, i ^ 1) for i in range(size)])]
    ppermute x11 -> x8, starting transfers between devices: 20.8 us -> 15.7 us  [butterfly(): x = x + lax.ppermute(x, axis, pairs)]
    ppermute x3, starting transfers between devices: 9.14 us -> 6.52 us  [sibling(): return lax.ppermute(x, 'dp', [(i, i ^ 1) for i in range(size)])]
    ppermute x11 -> x8, waiting for transfers between devices: 29.4 us -> 32 us  [butterfly(): x = x + lax.ppermute(x, axis, pairs)]
  transfers between devices with their start and end apart: 19 -> 16, of which waited for: 13 -> 11; matrix products, arithmetic and copies ran while one was open for 21% -> 20% of each run, Pallas kernels for 0% -> 0%
where the time goes in v7:
time: 243 us
  waiting for transfers between devices  120 us (49%)
  other arithmetic  44.4 us (18%)
  starting transfers between devices  39.3 us (16%)
  between operations  14.4 us (6%)
  matrix products  13 us (5%)
  local copies, waits for them, and re-layouts  11.5 us (5%)
    ppermute x4, waiting for transfers between devices, doubling_step(): received = lax.ppermute(held, axis, [(i, i ^ mask) for i in range(size)])  75.4 us
    ppermute x8, waiting for transfers between devices, butterfly(): x = x + lax.ppermute(x, axis, pairs)  32 us
    ppermute x4, starting transfers between devices, doubling_step(): received = lax.ppermute(held, axis, [(i, i ^ mask) for i in range(size)])  17.1 us
    ppermute x8, starting transfers between devices, butterfly(): x = x + lax.ppermute(x, axis, pairs)  15.7 us
    ppermute x3, waiting for transfers between devices, sibling(): return lax.ppermute(x, 'dp', [(i, i ^ 1) for i in range(size)])  12.6 us
    add x1, other arithmetic, shards(): grad_hidden + conv_kernel[k] * (back_views[count - 1 - k] * taps[count -...  10.3 us
    add x1, other arithmetic, shards(): mixed + conv_kernel[k] * views[k].astype(jnp.float32) * taps[k][:, None]  8.6 us
    ppermute x3, starting transfers between devices, sibling(): return lax.ppermute(x, 'dp', [(i, i ^ 1) for i in range(size)])  6.52 us
  transfers between devices with their start and end apart: 16, of which 11 were waited for; matrix products, arithmetic and copies ran while one was open for 20% of the time, Pallas kernels for 0%

profile of v7, /device:TPU:1, one launch (start us, length us, event | category | flops | bytes accessed | tf_op | source)
XLA Modules:
  0.0 242.7 jit_solution(9262240830278860280)
XLA Ops:
  8.3 7.8 %collective-permute-start = (bf16[1,48,1536]{2,1,0:T(8,128)(2,1)S(1)}, bf16[1,48,1536]{2,1,0:T(8,128)(2,1)S(1)}, u32[]{:S(2)}, u32[]{:S(2)}) collective-permute-start(bf16[1,48,1536]{2,1,0:T(8,128)(2,1)S(1)} %dynamic-slice_bitcast_fusion), channel_id=1, source_target_pairs={{0,2},{1,3},{2,0},{3,1},{4,6},{5,7},{6,4},{7,5},{8,10},{9,11},{10,... | collective-permute-start | bytes 442376 | tf_op jit(solution)/shard_map/ppermute | solution.py:46
  20.3 3.0 %collective-permute-start.1 = (bf16[2,48,1536]{2,1,0:T(8,128)(2,1)S(1)}, bf16[2,48,1536]{2,1,0:T(8,128)(2,1)S(1)}, u32[]{:S(2)}, u32[]{:S(2)}) collective-permute-start(bf16[2,48,1536]{2,1,0:T(8,128)(2,1)S(1)} %maximum_select_fusion.4), channel_id=1, source_target_pairs={{0,8},{1,9},{2,10},{3,11},{4,12},{5,13},{6,14},{7,15},{8,0},{9,1},... | collective-permute-start | bytes 884744 | tf_op jit(solution)/shard_map/ppermute | solution.py:46
  23.3 8.6 %fusion.7 = f32[512,1536]{1,0:T(8,128)} fusion(bf16[512,1536]{1,0:T(8,128)(2,1)} %param.6, f32[512]{0:T(512)S(1)} %bitcast.56, f32[1536]{0:T(1024)S(1)} %get-tuple-element.40, f32[512]{0:T(512)S(1)} %bitcast.59, f32[1536]{0:T(1024)S(1)} %get-tuple-element.41, f32[512]{0:T(512)S(1)} %bitcast.48, f32[1536]{0:T(1024)S(1)} %get-tuple-element.38, ...), kind=kLoop, calls=%fused_computation.20 | loop fusion | flops 14942208 | bytes 4759552 | tf_op jit(solution)/shard_map/add | solution.py:84
  32.8 2.1 reduce_sum.100
  34.9 2.5 %multiply_reduce_fusion.2 = f32[512]{0:T(512)S(1)} fusion(f32[512,1536]{1,0:T(8,128)} %fusion.7, f32[512]{0:T(512)S(1)} %broadcast_multiply_fusion.2), kind=kLoop, calls=%fused_computation.36 | loop fusion | flops 2358784 | bytes 3149824 | tf_op jit(solution)/shard_map/reduce_sum | solution.py:87
  39.0 1.6 copy.18
  44.8 7.5 %collective-permute-done.2 = f32[768,1536]{1,0:T(8,128)S(1)} collective-permute-done((f32[768,1536]{1,0:T(8,128)S(1)}, f32[768,1536]{1,0:T(8,128)S(1)}, u32[]{:S(2)}, u32[]{:S(2)}) %collective-permute-start.2) | collective-permute-done | bytes 4718624 | tf_op jit(solution)/shard_map/ppermute | solution.py:40
  52.3 3.5 %convolution_add_fusion = f32[768,1536]{1,0:T(8,128)} fusion(f32[768,1536]{1,0:T(8,128)S(1)} %collective-permute-done.2, bf16[512,768]{0,1:T(8,128)(2,1)S(1)} %bitcast.44, bf16[512,1536]{1,0:T(8,128)(2,1)S(1)} %copy-done), kind=kOutput, calls=%fused_computation.1 | convolution fusion | flops 1209139200 | bytes 11796480 | tf_op jit(solution)/shard_map/dot_general | solution.py:96
  55.8 4.5 %collective-permute-start.3 = (bf16[4,48,1536]{2,1,0:T(8,128)(2,1)}, bf16[4,48,1536]{2,1,0:T(8,128)(2,1)}, u32[]{:S(2)}, u32[]{:S(2)}) collective-permute-start(bf16[4,48,1536]{2,1,0:T(8,128)(2,1)} %maximum_select_fusion.2), channel_id=1, source_target_pairs={{0,1},{1,0},{2,3},{3,2},{4,5},{5,4},{6,7},{7,6},{8,9},{9,8},{10,11... | collective-permute-start | bytes 1769480 | tf_op jit(solution)/shard_map/ppermute | solution.py:46
  60.3 41.4 %collective-permute-done.3 = bf16[4,48,1536]{2,1,0:T(8,128)(2,1)} collective-permute-done((bf16[4,48,1536]{2,1,0:T(8,128)(2,1)}, bf16[4,48,1536]{2,1,0:T(8,128)(2,1)}, u32[]{:S(2)}, u32[]{:S(2)}) %collective-permute-start.3) | collective-permute-done | bytes 589856 | tf_op jit(solution)/shard_map/ppermute | solution.py:46
  101.7 2.9 %maximum_select_fusion.1 = bf16[8,48,1536]{2,1,0:T(8,128)(2,1)} fusion(bf16[4,48,1536]{2,1,0:T(8,128)(2,1)} %maximum_select_fusion.2, bf16[4,48,1536]{2,1,0:T(8,128)(2,1)} %collective-permute-done.3, pred[]{:T(512)S(6)} %ne.22), kind=kLoop, calls=%fused_computation.45 | loop fusion | flops 1769472 | bytes 2359297 | tf_op jit(solution)/shard_map/jit(_where)/select_n | solution.py:47
  104.6 1.8 collective-permute-start.4
  106.4 34.0 %collective-permute-done.4 = bf16[8,48,1536]{2,1,0:T(8,128)(2,1)} collective-permute-done((bf16[8,48,1536]{2,1,0:T(8,128)(2,1)}, bf16[8,48,1536]{2,1,0:T(8,128)(2,1)}, u32[]{:S(2)}, u32[]{:S(2)}) %collective-permute-start.4) | collective-permute-done | bytes 1179680 | tf_op jit(solution)/shard_map/ppermute | solution.py:46
  140.4 2.5 %maximum_select_fusion = bf16[16,48,1536]{2,1,0:T(8,128)(2,1)S(1)} fusion(bf16[8,48,1536]{2,1,0:T(8,128)(2,1)} %maximum_select_fusion.1, bf16[8,48,1536]{2,1,0:T(8,128)(2,1)} %collective-permute-done.4, pred[]{:T(512)S(6)} %ne.21), kind=kLoop, calls=%fused_computation.39 | loop fusion | flops 3538944 | bytes 4718593 | tf_op jit(solution)/shard_map/jit(_where)/select_n | solution.py:47
  143.0 1.6 copy.19
  144.5 2.5 %collective-permute-start.5 = (bf16[768,1536]{1,0:T(8,128)(2,1)}, bf16[768,1536]{1,0:T(8,128)(2,1)}, u32[]{:S(2)}, u32[]{:S(2)}) collective-permute-start(bf16[768,1536]{1,0:T(8,128)(2,1)} %bitcast.14), channel_id=1, source_target_pairs={{0,16},{16,0},{32,48},{48,32},{64,80},{80,64},{96,112},{112,96},{1... | collective-permute-start | bytes 7077896 | tf_op jit(solution)/shard_map/ppermute | solution.py:40
  147.0 4.5 %collective-permute-done.5 = bf16[768,1536]{1,0:T(8,128)(2,1)} collective-permute-done((bf16[768,1536]{1,0:T(8,128)(2,1)}, bf16[768,1536]{1,0:T(8,128)(2,1)}, u32[]{:S(2)}, u32[]{:S(2)}) %collective-permute-start.5) | collective-permute-done | bytes 2359328 | tf_op jit(solution)/shard_map/ppermute | solution.py:40
  151.5 2.7 %broadcast_select_fusion.1 = (bf16[768,1536]{1,0:T(8,128)(2,1)S(1)}, bf16[768,1536]{1,0:T(8,128)(2,1)S(1)}) fusion(bf16[768,1536]{1,0:T(8,128)(2,1)} %collective-permute-done.5, pred[]{:T(512)S(6)} %eq.24, bf16[2,2,2,2,48,1536]{5,4,3,2,1,0:T(8,128)(2,1)} %copy.19), kind=kLoop, calls=%fused_computation.41 | loop fusion | flops 2359296 | bytes 9437185 | tf_op jit(solution)/shard_map/jit(_where)/select_n | solution.py:106
  154.7 2.7 %copy-done.2 = f32[512,1536]{1,0:T(8,128)S(1)} copy-done((f32[512,1536]{1,0:T(8,128)S(1)}, f32[512,1536]{1,0:T(8,128)}, u32[]{:S(2)}) %copy-start.2) | copy-done | bytes 3145752
  157.4 3.8 %multiply_reduce_fusion = (f32[1536]{0:T(1024)S(1)}, f32[512]{0:T(512)S(1)}, f32[512]{0:T(512)S(1)}, f32[512,1536]{1,0:T(8,128)S(1)}) fusion(f32[512,1536]{1,0:T(8,128)S(1)} %copy-done.2, f32[512]{0:T(512)S(1)} %add_rsqrt_fusion, f32[512]{0:T(512)S(1)} %broadcast_multiply_fusion.2, f32[1536]{0:T(1024)S(1)} %copy-done.6, f32[512]{0:T(512)S(1)} %bitcast.50, ...), kind=kOutput, calls=%fused_computation.31 | convolution fusion | flops 2430072320 | bytes 12605440 | tf_op jit(solution)/shard_map/dot_general | solution.py:110
  161.3 5.5 %fusion.16 = (f32[1536]{0:T(1024)S(1)}, f32[1536]{0:T(1024)S(1)}, f32[1536]{0:T(1024)S(1)}, f32[1536]{0:T(1024)S(1)}, f32[1536]{0:T(1024)S(1)}, /*index=5*/f32[512,1536]{1,0:T(8,128)}) fusion(f32[512]{0:T(512)S(1)} %bitcast.57, bf16[512,1536]{1,0:T(8,128)(2,1)S(1)} %copy-done.3, f32[512]{0:T(512)S(1)} %bitcast.60, f32[512]{0:T(512)S(1)} %bitcast.51, ...), kind=kLoop, calls=%fused_computation.29 | loop fusion | flops 21225984 | bytes 11065344 | tf_op jit(solution)/shard_map/reduce_sum | solution.py:124
  167.0 5.2 %collective-permute-done.6 = f32[6,1536]{1,0:T(8,128)S(1)} collective-permute-done((f32[6,1536]{1,0:T(8,128)S(1)}, f32[6,1536]{1,0:T(8,128)S(1)}, u32[]{:S(2)}, u32[]{:S(2)}) %collective-permute-start.6) | collective-permute-done | bytes 36896 | tf_op jit(solution)/shard_map/ppermute | solution.py:34
  172.3 5.6 %collective-permute-start.7 = (f32[6,1536]{1,0:T(8,128)S(1)}, f32[6,1536]{1,0:T(8,128)S(1)}, u32[]{:S(2)}, u32[]{:S(2)}) collective-permute-start(f32[6,1536]{1,0:T(8,128)S(1)} %add.104), channel_id=1, source_target_pairs={{0,2},{1,3},{2,0},{3,1},{4,6},{5,7},{6,4},{7,5},{8,10},{9,11},{10,... | collective-permute-start | bytes 110600 | tf_op jit(solution)/shard_map/ppermute | solution.py:34
  179.3 1.7 collective-permute-start.8
  182.7 10.3 %multiply_add_fusion = f32[512,1536]{1,0:T(8,128)} fusion(f32[512,1536]{1,0:T(8,128)} %get-tuple-element.42, f32[512]{0:T(512)S(1)} %bitcast.58, f32[1536]{0:T(1024)S(1)} %get-tuple-element.40, f32[512]{0:T(512)S(1)} %bitcast.61, f32[1536]{0:T(1024)S(1)} %get-tuple-element.41, f32[512]{0:T(512)S(1)} %bitcast.52, f32[1536]{0:T(1024)S(1)} %get-tuple-element.38, ...), kind=kLoop, calls=%fused_computation.30 | loop fusion | flops 11010048 | bytes 6332416 | tf_op jit(solution)/shard_map/add | solution.py:128
  193.1 3.9 %collective-permute-start.10 = (f32[6,1536]{1,0:T(8,128)S(1)}, f32[6,1536]{1,0:T(8,128)S(1)}, u32[]{:S(2)}, u32[]{:S(2)}) collective-permute-start(f32[6,1536]{1,0:T(8,128)S(1)} %add.107), channel_id=1, source_target_pairs={{0,16},{16,0},{32,48},{48,32},{64,80},{80,64},{96,112},{112,96},{1... | collective-permute-start | bytes 110600 | tf_op jit(solution)/shard_map/ppermute | solution.py:34
  197.0 4.3 %fusion.33 = f32[512,1536]{1,0:T(8,128)} fusion(bf16[512,1536]{1,0:T(8,128)(2,1)S(1)} %multiply_convert_fusion, bf16[1536,1536]{1,0:T(8,128)(2,1)S(1)} %bitcast.46), kind=kOutput, calls=%fused_computation.93 | convolution fusion | flops 2415919104 | bytes 9437184 | tf_op jit(solution)/shard_map/dot_general | solution.py:109
  203.7 8.3 %collective-permute-done.11 = f32[54,1536]{1,0:T(8,128)S(1)} collective-permute-done((f32[54,1536]{1,0:T(8,128)S(1)}, f32[54,1536]{1,0:T(8,128)S(1)}, u32[]{:S(2)}, u32[]{:S(2)}) %collective-permute-start.11) | collective-permute-done | bytes 331808 | tf_op jit(solution)/shard_map/ppermute | solution.py:34
  212.0 2.7 %collective-permute-start.12 = (f32[54,1536]{1,0:T(8,128)S(1)}, f32[54,1536]{1,0:T(8,128)S(1)}, u32[]{:S(2)}, u32[]{:S(2)}) collective-permute-start(f32[54,1536]{1,0:T(8,128)S(1)} %add.113), channel_id=1, source_target_pairs={{0,64},{16,80},{32,96},{48,112},{64,0},{80,16},{96,32},{112,48},{1... | collective-permute-start | bytes 995336 | tf_op jit(solution)/shard_map/ppermute | solution.py:34
  214.7 7.6 %collective-permute-done.12 = f32[54,1536]{1,0:T(8,128)S(1)} collective-permute-done((f32[54,1536]{1,0:T(8,128)S(1)}, f32[54,1536]{1,0:T(8,128)S(1)}, u32[]{:S(2)}, u32[]{:S(2)}) %collective-permute-start.12) | collective-permute-done | bytes 331808 | tf_op jit(solution)/shard_map/ppermute | solution.py:34
  222.5 7.9 %collective-permute-done.13 = f32[54,1536]{1,0:T(8,128)S(1)} collective-permute-done((f32[54,1536]{1,0:T(8,128)S(1)}, f32[54,1536]{1,0:T(8,128)S(1)}, u32[]{:S(2)}, u32[]{:S(2)}) %collective-permute-start.13) | collective-permute-done | bytes 331808 | tf_op jit(solution)/shard_map/ppermute | solution.py:34
  231.1 2.7 %collective-permute-start.14 = (f32[48,1536]{1,0:T(8,128)S(1)}, f32[48,1536]{1,0:T(8,128)S(1)}, u32[]{:S(2)}, u32[]{:S(2)}) collective-permute-start(f32[48,1536]{1,0:T(8,128)S(1)} %slice.144), channel_id=1, source_target_pairs={{0,16},{16,0},{32,48},{48,32},{64,80},{80,64},{96,112},{112,96},{1... | collective-permute-start | bytes 884744 | tf_op jit(solution)/shard_map/ppermute | solution.py:40
  (73 shorter events, 21.1 us)
Async XLA Ops:
  7.2 34.9 %copy-start = (bf16[512,1536]{1,0:T(8,128)(2,1)S(1)}, bf16[512,1536]{1,0:T(8,128)(2,1)}, u32[]{:S(2)}) copy-start(bf16[512,1536]{1,0:T(8,128)(2,1)} %param.7) | copy-start | bytes 4718596
  7.2 194.1 %reduce-scatter.2.cloned.1.call-start = ((), (), s32[]{:S(2)}) async-start(), calls=%async_computation.1 | async-start | bytes 5013504 | tf_op jit(solution)/shard_map/reduce_scatter | solution.py:100
  8.3 11.9 %collective-permute-start = (bf16[1,48,1536]{2,1,0:T(8,128)(2,1)S(1)}, bf16[1,48,1536]{2,1,0:T(8,128)(2,1)S(1)}, u32[]{:S(2)}, u32[]{:S(2)}) collective-permute-start(bf16[1,48,1536]{2,1,0:T(8,128)(2,1)S(1)} %dynamic-slice_bitcast_fusion), channel_id=1, source_target_pairs={{0,2},{1,3},{2,0},{3,1},{4,6},{5,7},{6,4},{7,5},{8,10},{9,11},{10,... | collective-permute-start | bytes 442376 | tf_op jit(solution)/shard_map/ppermute | solution.py:46
  20.3 11.6 %collective-permute-start.1 = (bf16[2,48,1536]{2,1,0:T(8,128)(2,1)S(1)}, bf16[2,48,1536]{2,1,0:T(8,128)(2,1)S(1)}, u32[]{:S(2)}, u32[]{:S(2)}) collective-permute-start(bf16[2,48,1536]{2,1,0:T(8,128)(2,1)S(1)} %maximum_select_fusion.4), channel_id=1, source_target_pairs={{0,8},{1,9},{2,10},{3,11},{4,12},{5,13},{6,14},{7,15},{8,0},{9,1},... | collective-permute-start | bytes 884744 | tf_op jit(solution)/shard_map/ppermute | solution.py:46
  32.8 4.6 %copy-start.6 = (f32[1536]{0:T(1024)S(1)}, f32[1536]{0:T(1024)}, u32[]{:S(2)}) copy-start(f32[1536]{0:T(1024)} %param.10) | copy-start | bytes 18436
  34.9 2.8 %copy-start.1 = (f32[512,1536]{1,0:T(8,128)S(1)}, f32[512,1536]{1,0:T(8,128)}, u32[]{:S(2)}) copy-start(f32[512,1536]{1,0:T(8,128)} %fusion.7) | copy-start | bytes 9437188
  43.4 8.9 %collective-permute-start.2 = (f32[768,1536]{1,0:T(8,128)S(1)}, f32[768,1536]{1,0:T(8,128)S(1)}, u32[]{:S(2)}, u32[]{:S(2)}) collective-permute-start(f32[768,1536]{1,0:T(8,128)S(1)} %fusion.32), channel_id=1, source_target_pairs={{0,16},{16,0},{32,48},{48,32},{64,80},{80,64},{96,112},{112,96},{1... | collective-permute-start | bytes 14155784 | tf_op jit(solution)/shard_map/ppermute | solution.py:40
  55.8 45.9 %collective-permute-start.3 = (bf16[4,48,1536]{2,1,0:T(8,128)(2,1)}, bf16[4,48,1536]{2,1,0:T(8,128)(2,1)}, u32[]{:S(2)}, u32[]{:S(2)}) collective-permute-start(bf16[4,48,1536]{2,1,0:T(8,128)(2,1)} %maximum_select_fusion.2), channel_id=1, source_target_pairs={{0,1},{1,0},{2,3},{3,2},{4,5},{5,4},{6,7},{7,6},{8,9},{9,8},{10,11... | collective-permute-start | bytes 1769480 | tf_op jit(solution)/shard_map/ppermute | solution.py:46
  104.6 35.8 %collective-permute-start.4 = (bf16[8,48,1536]{2,1,0:T(8,128)(2,1)}, bf16[8,48,1536]{2,1,0:T(8,128)(2,1)}, u32[]{:S(2)}, u32[]{:S(2)}) collective-permute-start(bf16[8,48,1536]{2,1,0:T(8,128)(2,1)} %maximum_select_fusion.1), channel_id=1, source_target_pairs={{0,4},{1,5},{2,6},{3,7},{4,0},{5,1},{6,2},{7,3},{8,12},{9,13},{10,... | collective-permute-start | bytes 3538952 | tf_op jit(solution)/shard_map/ppermute | solution.py:46
  144.5 7.0 %collective-permute-start.5 = (bf16[768,1536]{1,0:T(8,128)(2,1)}, bf16[768,1536]{1,0:T(8,128)(2,1)}, u32[]{:S(2)}, u32[]{:S(2)}) collective-permute-start(bf16[768,1536]{1,0:T(8,128)(2,1)} %bitcast.14), channel_id=1, source_target_pairs={{0,16},{16,0},{32,48},{48,32},{64,80},{80,64},{96,112},{112,96},{1... | collective-permute-start | bytes 7077896 | tf_op jit(solution)/shard_map/ppermute | solution.py:40
  154.3 3.1 %copy-start.2 = (f32[512,1536]{1,0:T(8,128)S(1)}, f32[512,1536]{1,0:T(8,128)}, u32[]{:S(2)}) copy-start(f32[512,1536]{1,0:T(8,128)} %fusion.7) | copy-start | bytes 9437188
  154.7 6.5 %copy-start.4 = (bf16[16,2,48,1536]{3,2,1,0:T(8,128)(2,1)}, bf16[16,2,48,1536]{3,2,1,0:T(8,128)(2,1)S(1)}, u32[]{:S(2)}) copy-start(bf16[16,2,48,1536]{3,2,1,0:T(8,128)(2,1)S(1)} %pad_maximum_fusion) | copy-start | bytes 14155780
  157.4 3.9 %copy-start.3 = (bf16[512,1536]{1,0:T(8,128)(2,1)S(1)}, bf16[512,1536]{1,0:T(8,128)(2,1)}, u32[]{:S(2)}) copy-start(bf16[512,1536]{1,0:T(8,128)(2,1)} %param.6) | copy-start | bytes 4718596
  166.9 5.3 %collective-permute-start.6 = (f32[6,1536]{1,0:T(8,128)S(1)}, f32[6,1536]{1,0:T(8,128)S(1)}, u32[]{:S(2)}, u32[]{:S(2)}) collective-permute-start(f32[6,1536]{1,0:T(8,128)S(1)} %concatenate.48), channel_id=1, source_target_pairs={{0,1},{1,0},{2,3},{3,2},{4,5},{5,4},{6,7},{7,6},{8,9},{9,8},{10,11... | collective-permute-start | bytes 110600 | tf_op jit(solution)/shard_map/ppermute | solution.py:34
  172.3 7.0 %collective-permute-start.7 = (f32[6,1536]{1,0:T(8,128)S(1)}, f32[6,1536]{1,0:T(8,128)S(1)}, u32[]{:S(2)}, u32[]{:S(2)}) collective-permute-start(f32[6,1536]{1,0:T(8,128)S(1)} %add.104), channel_id=1, source_target_pairs={{0,2},{1,3},{2,0},{3,1},{4,6},{5,7},{6,4},{7,5},{8,10},{9,11},{10,... | collective-permute-start | bytes 110600 | tf_op jit(solution)/shard_map/ppermute | solution.py:34
  179.3 3.2 %collective-permute-start.8 = (f32[6,1536]{1,0:T(8,128)S(1)}, f32[6,1536]{1,0:T(8,128)S(1)}, u32[]{:S(2)}, u32[]{:S(2)}) collective-permute-start(f32[6,1536]{1,0:T(8,128)S(1)} %add.105), channel_id=1, source_target_pairs={{0,4},{1,5},{2,6},{3,7},{4,0},{5,1},{6,2},{7,3},{8,12},{9,13},{10,... | collective-permute-start | bytes 110600 | tf_op jit(solution)/shard_map/ppermute | solution.py:34
  182.5 10.6 %collective-permute-start.9 = (f32[6,1536]{1,0:T(8,128)S(1)}, f32[6,1536]{1,0:T(8,128)S(1)}, u32[]{:S(2)}, u32[]{:S(2)}) collective-permute-start(f32[6,1536]{1,0:T(8,128)S(1)} %add.106), channel_id=1, source_target_pairs={{0,8},{1,9},{2,10},{3,11},{4,12},{5,13},{6,14},{7,15},{8,0},{9,1},... | collective-permute-start | bytes 110600 | tf_op jit(solution)/shard_map/ppermute | solution.py:34
  182.7 14.2 %copy-start.5 = (bf16[16,2,48,1536]{3,2,1,0:T(8,128)(2,1)S(1)}, bf16[16,2,48,1536]{3,2,1,0:T(8,128)(2,1)}, u32[]{:S(2)}) copy-start(bf16[16,2,48,1536]{3,2,1,0:T(8,128)(2,1)} %copy-done.4) | copy-start | bytes 14155780
  193.1 8.2 %collective-permute-start.10 = (f32[6,1536]{1,0:T(8,128)S(1)}, f32[6,1536]{1,0:T(8,128)S(1)}, u32[]{:S(2)}, u32[]{:S(2)}) collective-permute-start(f32[6,1536]{1,0:T(8,128)S(1)} %add.107), channel_id=1, source_target_pairs={{0,16},{16,0},{32,48},{48,32},{64,80},{80,64},{96,112},{112,96},{1... | collective-permute-start | bytes 110600 | tf_op jit(solution)/shard_map/ppermute | solution.py:34
  202.3 9.7 %collective-permute-start.11 = (f32[54,1536]{1,0:T(8,128)S(1)}, f32[54,1536]{1,0:T(8,128)S(1)}, u32[]{:S(2)}, u32[]{:S(2)}) collective-permute-start(f32[54,1536]{1,0:T(8,128)S(1)} %constant_dynamic-update-slice_fusion), channel_id=1, source_target_pairs={{0,32},{16,48},{32,0},{48,16},{64,96},{80,112},{96,64},{112,80},{1... | collective-permute-start | bytes 995336 | tf_op jit(solution)/shard_map/ppermute | solution.py:34
  212.0 10.3 %collective-permute-start.12 = (f32[54,1536]{1,0:T(8,128)S(1)}, f32[54,1536]{1,0:T(8,128)S(1)}, u32[]{:S(2)}, u32[]{:S(2)}) collective-permute-start(f32[54,1536]{1,0:T(8,128)S(1)} %add.113), channel_id=1, source_target_pairs={{0,64},{16,80},{32,96},{48,112},{64,0},{80,16},{96,32},{112,48},{1... | collective-permute-start | bytes 995336 | tf_op jit(solution)/shard_map/ppermute | solution.py:34
  222.4 8.0 %collective-permute-start.13 = (f32[54,1536]{1,0:T(8,128)S(1)}, f32[54,1536]{1,0:T(8,128)S(1)}, u32[]{:S(2)}, u32[]{:S(2)}) collective-permute-start(f32[54,1536]{1,0:T(8,128)S(1)} %add.114), channel_id=1, source_target_pairs={{0,128},{16,144},{32,160},{48,176},{64,192},{80,208},{96,224},{112... | collective-permute-start | bytes 995336 | tf_op jit(solution)/shard_map/ppermute | solution.py:34
  231.1 3.9 %collective-permute-start.14 = (f32[48,1536]{1,0:T(8,128)S(1)}, f32[48,1536]{1,0:T(8,128)S(1)}, u32[]{:S(2)}, u32[]{:S(2)}) collective-permute-start(f32[48,1536]{1,0:T(8,128)S(1)} %slice.144), channel_id=1, source_target_pairs={{0,16},{16,0},{32,48},{48,32},{64,80},{80,64},{96,112},{112,96},{1... | collective-permute-start | bytes 884744 | tf_op jit(solution)/shard_map/ppermute | solution.py:40
Sparse Core Ops, SparseCore 0:
  60.4 101.5 reduce-scatter.1

commit v8 on v6

--- a/solution.py
+++ b/solution.py
@@ -75,7 +75,8 @@
     own_half = lax.dynamic_slice_in_dim(out_weight, core * half_rows, half_rows, 0)
     held = doubling_step(own_half[None], "fsdp", masks[0])
     taps = tap_mask(lengths[0], frames, count)
-    held, taps = lax.optimization_barrier((held, taps))
+    sibling_cot = sibling(grad_out)
+    held, taps, sibling_cot = lax.optimization_barrier((held, taps, sibling_cot))
     held = doubling_step(held, "fsdp", masks[1])
     live = taps[half_width][:, None]
     views = shifted(hidden_in, half_width)
@@ -93,14 +94,15 @@
     split_act = activation.reshape(frames, fsdp_count, 2, half_rows)
     keep_act = lax.dynamic_index_in_dim(split_act, core, 2, keepdims=False).reshape(frames, -1)
     send_act = lax.dynamic_index_in_dim(split_act, 1 - core, 2, keepdims=False).reshape(frames, -1)
-    contract = (((0,), (0,)), ((), ()))
-    keep_terms = lax.dot_general(keep_act, grad_out, contract, preferred_element_type=jnp.float32)
-    send_terms = lax.dot_general(send_act, grad_out, contract, preferred_element_type=jnp.float32)
-    held, keep_terms, send_terms, activation = lax.optimization_barrier(
-        (held, keep_terms, send_terms, activation)
+    held, keep_act, send_act, activation = lax.optimization_barrier(
+        (held, keep_act, send_act, activation)
     )
     held = doubling_step(held, "fsdp", masks[3])
-    chip_terms = keep_terms + sibling(send_terms)
+    chip_act = jnp.concatenate([keep_act, sibling(send_act)], axis=0)
+    chip_cot = jnp.concatenate([grad_out, sibling_cot], axis=0)
+    chip_terms = lax.dot_general(
+        chip_act, chip_cot, (((0,), (0,)), ((), ())), preferred_element_type=jnp.float32
+    )
     shard_sum = lax.psum_scatter(chip_terms, "fsdp", scatter_dimension=0, tiled=True)
     held, chip_terms = lax.optimization_barrier((held, chip_terms))
     gathered = doubling_order(held, masks)

time: 214 us -> 210 us (0.981)
  other arithmetic: 47.5 us -> 40.8 us
  waiting for transfers between devices: 91.4 us -> 94.2 us
    ppermute x3 -> x4, waiting for transfers between devices: 12.6 us -> 7 us  [sibling(): return lax.ppermute(x, 'dp', [(i, i ^ 1) for i in range(size)])]
    ppermute x4, waiting for transfers between devices: 48.5 us -> 53.7 us  [doubling_step(): received = lax.ppermute(held, axis, [(i, i ^ mask) for i in range(size)])]
    add x1 -> x0, other arithmetic: 3.1 us -> none  [shards(): chip_terms = keep_terms + sibling(send_terms)]
    ppermute x3 -> x4, starting transfers between devices: 7.76 us -> 10.8 us  [sibling(): return lax.ppermute(x, 'dp', [(i, i ^ 1) for i in range(size)])]
    ppermute x4, starting transfers between devices: 15.4 us -> 13.1 us  [doubling_step(): received = lax.ppermute(held, axis, [(i, i ^ mask) for i in range(size)])]
  transfers between devices with their start and end apart: 16 -> 17, of which waited for: 12 -> 12; matrix products, arithmetic and copies ran while one was open for 26% -> 24% of each run, Pallas kernels for 0% -> 0%
where the time goes in v8:
time: 210 us
  waiting for transfers between devices  94.2 us (45%)
  other arithmetic  40.8 us (19%)
  starting transfers between devices  38.4 us (18%)
  between operations  14.3 us (7%)
  matrix products  12.3 us (6%)
  local copies, waits for them, and re-layouts  9.71 us (5%)
    ppermute x4, waiting for transfers between devices, doubling_step(): received = lax.ppermute(held, axis, [(i, i ^ mask) for i in range(size)])  53.7 us
    ppermute x8, waiting for transfers between devices, butterfly(): x = x + lax.ppermute(x, axis, pairs)  30.8 us
    ppermute x8, starting transfers between devices, butterfly(): x = x + lax.ppermute(x, axis, pairs)  14.4 us
    ppermute x4, starting transfers between devices, doubling_step(): received = lax.ppermute(held, axis, [(i, i ^ mask) for i in range(size)])  13.1 us
    ppermute x4, starting transfers between devices, sibling(): return lax.ppermute(x, 'dp', [(i, i ^ 1) for i in range(size)])  10.8 us
    add x1, other arithmetic, shards(): grad_hidden + conv_kernel[k] * (back_views[count - 1 - k] * taps[count -...  10.3 us
    add x1, other arithmetic, shards(): mixed + conv_kernel[k] * views[k].astype(jnp.float32) * taps[k][:, None]  7.9 us
    ppermute x4, waiting for transfers between devices, sibling(): return lax.ppermute(x, 'dp', [(i, i ^ 1) for i in range(size)])  7 us
  transfers between devices with their start and end apart: 17, of which 12 were waited for; matrix products, arithmetic and copies ran while one was open for 24% of the time, Pallas kernels for 0%

profile of v8, /device:TPU:1, one launch (start us, length us, event | category | flops | bytes accessed | tf_op | source)
XLA Modules:
  0.0 209.7 jit_solution(12480890201464849724)
XLA Ops:
  7.2 3.3 %collective-permute-start.1 = (bf16[512,1536]{1,0:T(8,128)(2,1)}, bf16[512,1536]{1,0:T(8,128)(2,1)S(1)}, u32[]{:S(2)}, u32[]{:S(2)}) collective-permute-start(bf16[512,1536]{1,0:T(8,128)(2,1)} %param.7), channel_id=1, source_target_pairs={{0,16},{16,0},{32,48},{48,32},{64,80},{80,64},{96,112},{112,96},{1... | collective-permute-start | bytes 4718600 | tf_op jit(solution)/shard_map/ppermute | solution.py:40
  10.5 5.4 %collective-permute-start = (bf16[1,48,1536]{2,1,0:T(8,128)(2,1)S(1)}, bf16[1,48,1536]{2,1,0:T(8,128)(2,1)S(1)}, u32[]{:S(2)}, u32[]{:S(2)}) collective-permute-start(bf16[1,48,1536]{2,1,0:T(8,128)(2,1)S(1)} %dynamic-slice_bitcast_fusion), channel_id=1, source_target_pairs={{0,2},{1,3},{2,0},{3,1},{4,6},{5,7},{6,4},{7,5},{8,10},{9,11},{10,... | collective-permute-start | bytes 442376 | tf_op jit(solution)/shard_map/ppermute | solution.py:46
  20.2 3.0 %collective-permute-start.2 = (bf16[2,48,1536]{2,1,0:T(8,128)(2,1)S(1)}, bf16[2,48,1536]{2,1,0:T(8,128)(2,1)S(1)}, u32[]{:S(2)}, u32[]{:S(2)}) collective-permute-start(bf16[2,48,1536]{2,1,0:T(8,128)(2,1)S(1)} %maximum_select_fusion.4), channel_id=1, source_target_pairs={{0,8},{1,9},{2,10},{3,11},{4,12},{5,13},{6,14},{7,15},{8,0},{9,1},... | collective-permute-start | bytes 884744 | tf_op jit(solution)/shard_map/ppermute | solution.py:46
  23.2 7.9 %fusion.7 = f32[512,1536]{1,0:T(8,128)S(1)} fusion(bf16[512,1536]{1,0:T(8,128)(2,1)} %param.6, f32[512]{0:T(512)S(1)} %bitcast.52, f32[1536]{0:T(1024)S(1)} %get-tuple-element.44, f32[512]{0:T(512)S(1)} %bitcast.55, f32[1536]{0:T(1024)S(1)} %get-tuple-element.45, f32[512]{0:T(512)S(1)} %bitcast.44, f32[1536]{0:T(1024)S(1)} %get-tuple-element.42, ...), kind=kLoop, calls=%fused_computation.19 | loop fusion | flops 14942208 | bytes 4759552 | tf_op jit(solution)/shard_map/add | solution.py:85
  32.7 4.2 %collective-permute-start.3 = (bf16[4,48,1536]{2,1,0:T(8,128)(2,1)}, bf16[4,48,1536]{2,1,0:T(8,128)(2,1)}, u32[]{:S(2)}, u32[]{:S(2)}) collective-permute-start(bf16[4,48,1536]{2,1,0:T(8,128)(2,1)} %maximum_select_fusion.2), channel_id=1, source_target_pairs={{0,1},{1,0},{2,3},{3,2},{4,5},{5,4},{6,7},{7,6},{8,9},{9,8},{10,11... | collective-permute-start | bytes 1769480 | tf_op jit(solution)/shard_map/ppermute | solution.py:46
  36.9 2.4 %multiply_convert_fusion = bf16[512,1536]{1,0:T(8,128)(2,1)} fusion(f32[512,1536]{1,0:T(8,128)S(1)} %fusion.7, f32[1536]{0:T(1024)S(1)} %copy-done.5, f32[512]{0:T(512)S(1)} %add_rsqrt_fusion, f32[512]{0:T(512)S(1)} %broadcast_multiply_fusion.2, f32[512]{0:T(512)S(1)} %bitcast.45), kind=kLoop, calls=%fused_computation.37 | loop fusion | flops 7077888 | bytes 4730880 | tf_op jit(solution)/shard_map/convert_element_type | solution.py:93
  39.3 2.6 %copy.18 = bf16[512,1536]{0,1:T(8,128)(2,1)} copy(bf16[512,1536]{1,0:T(8,128)(2,1)} %multiply_convert_fusion) | data formatting | bytes 3145728 | tf_op jit(solution)/shard_map/convert_element_type | solution.py:93
  43.6 18.9 %collective-permute-done.3 = bf16[4,48,1536]{2,1,0:T(8,128)(2,1)} collective-permute-done((bf16[4,48,1536]{2,1,0:T(8,128)(2,1)}, bf16[4,48,1536]{2,1,0:T(8,128)(2,1)}, u32[]{:S(2)}, u32[]{:S(2)}) %collective-permute-start.3) | collective-permute-done | bytes 589856 | tf_op jit(solution)/shard_map/ppermute | solution.py:46
  62.5 2.8 %maximum_select_fusion.1 = bf16[8,48,1536]{2,1,0:T(8,128)(2,1)} fusion(bf16[4,48,1536]{2,1,0:T(8,128)(2,1)} %maximum_select_fusion.2, bf16[4,48,1536]{2,1,0:T(8,128)(2,1)} %collective-permute-done.3, pred[]{:T(512)S(6)} %ne.18), kind=kLoop, calls=%fused_computation.51 | loop fusion | flops 1769472 | bytes 2359297 | tf_op jit(solution)/shard_map/jit(_where)/select_n | solution.py:47
  65.3 1.7 collective-permute-start.4
  67.0 1.9 collective-permute-done.4
  68.9 4.2 %fusion.17 = f32[768,1536]{1,0:T(8,128)} fusion(bf16[512,1536]{1,0:T(8,128)(2,1)S(1)} %copy-done.9, bf16[512,1536]{1,0:T(8,128)(2,1)S(1)} %copy-done.6, bf16[512,768]{0,1:T(8,128)(2,1)S(1)} %collective-permute-done.4, bf16[512,768]{0,1:T(8,128)(2,1)S(1)} %bitcast.42), kind=kOutput, calls=%fused_computation.29 | convolution fusion | flops 2425356288 | bytes 9437184 | tf_op jit(solution)/shard_map/dot_general | solution.py:103
  73.6 34.8 %collective-permute-done.5 = bf16[8,48,1536]{2,1,0:T(8,128)(2,1)} collective-permute-done((bf16[8,48,1536]{2,1,0:T(8,128)(2,1)}, bf16[8,48,1536]{2,1,0:T(8,128)(2,1)}, u32[]{:S(2)}, u32[]{:S(2)}) %collective-permute-start.5) | collective-permute-done | bytes 1179680 | tf_op jit(solution)/shard_map/ppermute | solution.py:46
  108.4 2.6 %maximum_select_fusion = bf16[16,48,1536]{2,1,0:T(8,128)(2,1)S(1)} fusion(bf16[8,48,1536]{2,1,0:T(8,128)(2,1)} %maximum_select_fusion.1, bf16[8,48,1536]{2,1,0:T(8,128)(2,1)} %collective-permute-done.5, pred[]{:T(512)S(6)} %ne.22), kind=kLoop, calls=%fused_computation.42 | loop fusion | flops 3538944 | bytes 4718593 | tf_op jit(solution)/shard_map/jit(_where)/select_n | solution.py:47
  112.6 1.7 collective-permute-start.6
  114.2 4.5 %collective-permute-done.6 = bf16[768,1536]{1,0:T(8,128)(2,1)} collective-permute-done((bf16[768,1536]{1,0:T(8,128)(2,1)}, bf16[768,1536]{1,0:T(8,128)(2,1)}, u32[]{:S(2)}, u32[]{:S(2)}) %collective-permute-start.6) | collective-permute-done | bytes 2359328 | tf_op jit(solution)/shard_map/ppermute | solution.py:40
  118.7 2.7 %broadcast_select_fusion.1 = (bf16[768,1536]{1,0:T(8,128)(2,1)S(1)}, bf16[768,1536]{1,0:T(8,128)(2,1)S(1)}) fusion(bf16[768,1536]{1,0:T(8,128)(2,1)} %collective-permute-done.6, pred[]{:T(512)S(6)} %eq.24, bf16[2,2,2,2,48,1536]{5,4,3,2,1,0:T(8,128)(2,1)} %copy.19), kind=kLoop, calls=%fused_computation.44 | loop fusion | flops 2359296 | bytes 9437185 | tf_op jit(solution)/shard_map/jit(_where)/select_n | solution.py:110
  122.9 3.8 %multiply_reduce_fusion = (f32[1536]{0:T(1024)S(1)}, f32[512]{0:T(512)S(1)}, f32[512]{0:T(512)S(1)}, f32[512,1536]{1,0:T(8,128)S(1)}) fusion(f32[512,1536]{1,0:T(8,128)S(1)} %fusion.7, f32[512]{0:T(512)S(1)} %add_rsqrt_fusion, f32[512]{0:T(512)S(1)} %broadcast_multiply_fusion.2, f32[1536]{0:T(1024)S(1)} %copy-done.5, f32[512]{0:T(512)S(1)} %bitcast.46, ...), kind=kOutput, calls=%fused_computation.34 | convolution fusion | flops 2430072320 | bytes 12605440 | tf_op jit(solution)/shard_map/dot_general | solution.py:114
  126.8 5.4 %fusion.16 = (f32[1536]{0:T(1024)S(1)}, f32[1536]{0:T(1024)S(1)}, f32[1536]{0:T(1024)S(1)}, f32[1536]{0:T(1024)S(1)}, f32[1536]{0:T(1024)S(1)}, /*index=5*/f32[512,1536]{1,0:T(8,128)}) fusion(f32[512]{0:T(512)S(1)} %bitcast.53, bf16[512,1536]{1,0:T(8,128)(2,1)S(1)} %copy-done.1, f32[512]{0:T(512)S(1)} %bitcast.56, f32[512]{0:T(512)S(1)} %bitcast.47, ...), kind=kLoop, calls=%fused_computation.28 | loop fusion | flops 21225984 | bytes 11065344 | tf_op jit(solution)/shard_map/reduce_sum | solution.py:128
  132.4 6.8 %collective-permute-done.7 = f32[6,1536]{1,0:T(8,128)S(1)} collective-permute-done((f32[6,1536]{1,0:T(8,128)S(1)}, f32[6,1536]{1,0:T(8,128)S(1)}, u32[]{:S(2)}, u32[]{:S(2)}) %collective-permute-start.7) | collective-permute-done | bytes 36896 | tf_op jit(solution)/shard_map/ppermute | solution.py:34
  139.3 5.6 %collective-permute-start.8 = (f32[6,1536]{1,0:T(8,128)S(1)}, f32[6,1536]{1,0:T(8,128)S(1)}, u32[]{:S(2)}, u32[]{:S(2)}) collective-permute-start(f32[6,1536]{1,0:T(8,128)S(1)} %add.100), channel_id=1, source_target_pairs={{0,2},{1,3},{2,0},{3,1},{4,6},{5,7},{6,4},{7,5},{8,10},{9,11},{10,... | collective-permute-start | bytes 110600 | tf_op jit(solution)/shard_map/ppermute | solution.py:34
  144.9 1.7 collective-permute-done.8
  146.9 2.7 %collective-permute-done.9 = f32[6,1536]{1,0:T(8,128)S(1)} collective-permute-done((f32[6,1536]{1,0:T(8,128)S(1)}, f32[6,1536]{1,0:T(8,128)S(1)}, u32[]{:S(2)}, u32[]{:S(2)}) %collective-permute-start.9) | collective-permute-done | bytes 36896 | tf_op jit(solution)/shard_map/ppermute | solution.py:34
  151.0 10.3 %multiply_add_fusion = f32[512,1536]{1,0:T(8,128)} fusion(f32[512,1536]{1,0:T(8,128)} %get-tuple-element.46, f32[512]{0:T(512)S(1)} %bitcast.54, f32[1536]{0:T(1024)S(1)} %get-tuple-element.44, f32[512]{0:T(512)S(1)} %bitcast.57, f32[1536]{0:T(1024)S(1)} %get-tuple-element.45, f32[512]{0:T(512)S(1)} %bitcast.48, f32[1536]{0:T(1024)S(1)} %get-tuple-element.42, ...), kind=kLoop, calls=%fused_computation.33 | loop fusion | flops 11010048 | bytes 6332416 | tf_op jit(solution)/shard_map/add | solution.py:132
  161.3 2.9 %collective-permute-start.11 = (f32[6,1536]{1,0:T(8,128)S(1)}, f32[6,1536]{1,0:T(8,128)S(1)}, u32[]{:S(2)}, u32[]{:S(2)}) collective-permute-start(f32[6,1536]{1,0:T(8,128)S(1)} %add.103), channel_id=1, source_target_pairs={{0,16},{16,0},{32,48},{48,32},{64,80},{80,64},{96,112},{112,96},{1... | collective-permute-start | bytes 110600 | tf_op jit(solution)/shard_map/ppermute | solution.py:34
  164.3 4.3 %fusion.40 = f32[512,1536]{1,0:T(8,128)} fusion(bf16[512,1536]{1,0:T(8,128)(2,1)S(1)} %copy-done.2, bf16[1536,1536]{1,0:T(8,128)(2,1)S(1)} %bitcast.41), kind=kOutput, calls=%fused_computation.99 | convolution fusion | flops 2415919104 | bytes 9437184 | tf_op jit(solution)/shard_map/dot_general | solution.py:113
  168.5 2.7 %reduce-scatter.2.cloned.1.call-done = f32[48,1536]{1,0:T(8,128)} async-done(((f32[768,1536]{1,0:T(8,128)}), f32[48,1536]{1,0:T(8,128)}) %reduce-scatter.2.cloned.1.call-update) | async-done | bytes 294928 | tf_op jit(solution)/shard_map/reduce_scatter | solution.py:106
  173.6 6.9 %collective-permute-done.12 = f32[54,1536]{1,0:T(8,128)S(1)} collective-permute-done((f32[54,1536]{1,0:T(8,128)S(1)}, f32[54,1536]{1,0:T(8,128)S(1)}, u32[]{:S(2)}, u32[]{:S(2)}) %collective-permute-start.12) | collective-permute-done | bytes 331808 | tf_op jit(solution)/shard_map/ppermute | solution.py:34
  180.5 2.7 %collective-permute-start.13 = (f32[54,1536]{1,0:T(8,128)S(1)}, f32[54,1536]{1,0:T(8,128)S(1)}, u32[]{:S(2)}, u32[]{:S(2)}) collective-permute-start(f32[54,1536]{1,0:T(8,128)S(1)} %add.109), channel_id=1, source_target_pairs={{0,64},{16,80},{32,96},{48,112},{64,0},{80,16},{96,32},{112,48},{1... | collective-permute-start | bytes 995336 | tf_op jit(solution)/shard_map/ppermute | solution.py:34
  183.2 6.2 %collective-permute-done.13 = f32[54,1536]{1,0:T(8,128)S(1)} collective-permute-done((f32[54,1536]{1,0:T(8,128)S(1)}, f32[54,1536]{1,0:T(8,128)S(1)}, u32[]{:S(2)}, u32[]{:S(2)}) %collective-permute-start.13) | collective-permute-done | bytes 331808 | tf_op jit(solution)/shard_map/ppermute | solution.py:34
  189.6 6.4 %collective-permute-done.14 = f32[54,1536]{1,0:T(8,128)S(1)} collective-permute-done((f32[54,1536]{1,0:T(8,128)S(1)}, f32[54,1536]{1,0:T(8,128)S(1)}, u32[]{:S(2)}, u32[]{:S(2)}) %collective-permute-start.14) | collective-permute-done | bytes 331808 | tf_op jit(solution)/shard_map/ppermute | solution.py:34
  196.7 4.1 %collective-permute-start.15 = (f32[48,1536]{1,0:T(8,128)S(1)}, f32[48,1536]{1,0:T(8,128)S(1)}, u32[]{:S(2)}, u32[]{:S(2)}) collective-permute-start(f32[48,1536]{1,0:T(8,128)S(1)} %slice.144), channel_id=1, source_target_pairs={{0,16},{16,0},{32,48},{48,32},{64,80},{80,64},{96,112},{112,96},{1... | collective-permute-start | bytes 884744 | tf_op jit(solution)/shard_map/ppermute | solution.py:40
  (80 shorter events, 18.1 us)
Async XLA Ops:
  7.2 3.4 %copy-start = (bf16[96,1536]{1,0:T(8,128)(2,1)S(1)}, bf16[96,1536]{1,0:T(8,128)(2,1)}, u32[]{:S(2)}) copy-start(bf16[96,1536]{1,0:T(8,128)(2,1)} %param.11) | copy-start | bytes 884740
  7.2 164.1 %reduce-scatter.2.cloned.1.call-start = ((), (), s32[]{:S(2)}) async-start(), calls=%async_computation.1 | async-start | bytes 5013504 | tf_op jit(solution)/shard_map/reduce_scatter | solution.py:106
  7.2 12.9 %collective-permute-start.1 = (bf16[512,1536]{1,0:T(8,128)(2,1)}, bf16[512,1536]{1,0:T(8,128)(2,1)S(1)}, u32[]{:S(2)}, u32[]{:S(2)}) collective-permute-start(bf16[512,1536]{1,0:T(8,128)(2,1)} %param.7), channel_id=1, source_target_pairs={{0,16},{16,0},{32,48},{48,32},{64,80},{80,64},{96,112},{112,96},{1... | collective-permute-start | bytes 4718600 | tf_op jit(solution)/shard_map/ppermute | solution.py:40
  10.5 9.6 %collective-permute-start = (bf16[1,48,1536]{2,1,0:T(8,128)(2,1)S(1)}, bf16[1,48,1536]{2,1,0:T(8,128)(2,1)S(1)}, u32[]{:S(2)}, u32[]{:S(2)}) collective-permute-start(bf16[1,48,1536]{2,1,0:T(8,128)(2,1)S(1)} %dynamic-slice_bitcast_fusion), channel_id=1, source_target_pairs={{0,2},{1,3},{2,0},{3,1},{4,6},{5,7},{6,4},{7,5},{8,10},{9,11},{10,... | collective-permute-start | bytes 442376 | tf_op jit(solution)/shard_map/ppermute | solution.py:46
  20.1 3.0 %copy-start.8 = (bf16[512,1536]{1,0:T(8,128)(2,1)}, bf16[512,1536]{1,0:T(8,128)(2,1)S(1)}, u32[]{:S(2)}) copy-start(bf16[512,1536]{1,0:T(8,128)(2,1)S(1)} %collective-permute-done.1) | copy-start | bytes 4718596
  20.2 10.9 %collective-permute-start.2 = (bf16[2,48,1536]{2,1,0:T(8,128)(2,1)S(1)}, bf16[2,48,1536]{2,1,0:T(8,128)(2,1)S(1)}, u32[]{:S(2)}, u32[]{:S(2)}) collective-permute-start(bf16[2,48,1536]{2,1,0:T(8,128)(2,1)S(1)} %maximum_select_fusion.4), channel_id=1, source_target_pairs={{0,8},{1,9},{2,10},{3,11},{4,12},{5,13},{6,14},{7,15},{8,0},{9,1},... | collective-permute-start | bytes 884744 | tf_op jit(solution)/shard_map/ppermute | solution.py:46
  32.0 4.9 %copy-start.5 = (f32[1536]{0:T(1024)S(1)}, f32[1536]{0:T(1024)}, u32[]{:S(2)}) copy-start(f32[1536]{0:T(1024)} %param.10) | copy-start | bytes 18436
  32.7 29.8 %collective-permute-start.3 = (bf16[4,48,1536]{2,1,0:T(8,128)(2,1)}, bf16[4,48,1536]{2,1,0:T(8,128)(2,1)}, u32[]{:S(2)}, u32[]{:S(2)}) collective-permute-start(bf16[4,48,1536]{2,1,0:T(8,128)(2,1)} %maximum_select_fusion.2), channel_id=1, source_target_pairs={{0,1},{1,0},{2,3},{3,2},{4,5},{5,4},{6,7},{7,6},{8,9},{9,8},{10,11... | collective-permute-start | bytes 1769480 | tf_op jit(solution)/shard_map/ppermute | solution.py:46
  41.9 27.0 %copy-start.6 = (bf16[512,1536]{1,0:T(8,128)(2,1)S(1)}, bf16[512,1536]{1,0:T(8,128)(2,1)}, u32[]{:S(2)}) copy-start(bf16[512,1536]{1,0:T(8,128)(2,1)} %param.7) | copy-start | bytes 4718596
  41.9 27.0 %copy-start.9 = (bf16[512,1536]{1,0:T(8,128)(2,1)S(1)}, bf16[512,1536]{1,0:T(8,128)(2,1)}, u32[]{:S(2)}) copy-start(bf16[512,1536]{1,0:T(8,128)(2,1)} %copy-done.8) | copy-start | bytes 4718596
  65.3 3.6 %collective-permute-start.4 = (bf16[512,768]{0,1:T(8,128)(2,1)S(1)}, bf16[512,768]{0,1:T(8,128)(2,1)S(1)}, u32[]{:S(2)}, u32[]{:S(2)}) collective-permute-start(bf16[512,768]{0,1:T(8,128)(2,1)S(1)} %bitcast.43), channel_id=1, source_target_pairs={{0,16},{16,0},{32,48},{48,32},{64,80},{80,64},{96,112},{112,96},{1... | collective-permute-start | bytes 2359304 | tf_op jit(solution)/shard_map/ppermute | solution.py:40
  73.2 35.2 %collective-permute-start.5 = (bf16[8,48,1536]{2,1,0:T(8,128)(2,1)}, bf16[8,48,1536]{2,1,0:T(8,128)(2,1)}, u32[]{:S(2)}, u32[]{:S(2)}) collective-permute-start(bf16[8,48,1536]{2,1,0:T(8,128)(2,1)} %maximum_select_fusion.1), channel_id=1, source_target_pairs={{0,4},{1,5},{2,6},{3,7},{4,0},{5,1},{6,2},{7,3},{8,12},{9,13},{10,... | collective-permute-start | bytes 3538952 | tf_op jit(solution)/shard_map/ppermute | solution.py:46
  112.6 6.2 %collective-permute-start.6 = (bf16[768,1536]{1,0:T(8,128)(2,1)}, bf16[768,1536]{1,0:T(8,128)(2,1)}, u32[]{:S(2)}, u32[]{:S(2)}) collective-permute-start(bf16[768,1536]{1,0:T(8,128)(2,1)} %bitcast.14), channel_id=1, source_target_pairs={{0,16},{16,0},{32,48},{48,32},{64,80},{80,64},{96,112},{112,96},{1... | collective-permute-start | bytes 7077896 | tf_op jit(solution)/shard_map/ppermute | solution.py:40
  121.4 1.5 copy-start.7
  121.9 4.9 %copy-start.3 = (bf16[16,2,48,1536]{3,2,1,0:T(8,128)(2,1)}, bf16[16,2,48,1536]{3,2,1,0:T(8,128)(2,1)S(1)}, u32[]{:S(2)}) copy-start(bf16[16,2,48,1536]{3,2,1,0:T(8,128)(2,1)S(1)} %pad_maximum_fusion) | copy-start | bytes 14155780
  122.9 3.9 %copy-start.1 = (bf16[512,1536]{1,0:T(8,128)(2,1)S(1)}, bf16[512,1536]{1,0:T(8,128)(2,1)}, u32[]{:S(2)}) copy-start(bf16[512,1536]{1,0:T(8,128)(2,1)} %param.6) | copy-start | bytes 4718596
  132.3 6.9 %collective-permute-start.7 = (f32[6,1536]{1,0:T(8,128)S(1)}, f32[6,1536]{1,0:T(8,128)S(1)}, u32[]{:S(2)}, u32[]{:S(2)}) collective-permute-start(f32[6,1536]{1,0:T(8,128)S(1)} %concatenate.56), channel_id=1, source_target_pairs={{0,1},{1,0},{2,3},{3,2},{4,5},{5,4},{6,7},{7,6},{8,9},{9,8},{10,11... | collective-permute-start | bytes 110600 | tf_op jit(solution)/shard_map/ppermute | solution.py:34
  139.3 7.3 %collective-permute-start.8 = (f32[6,1536]{1,0:T(8,128)S(1)}, f32[6,1536]{1,0:T(8,128)S(1)}, u32[]{:S(2)}, u32[]{:S(2)}) collective-permute-start(f32[6,1536]{1,0:T(8,128)S(1)} %add.100), channel_id=1, source_target_pairs={{0,2},{1,3},{2,0},{3,1},{4,6},{5,7},{6,4},{7,5},{8,10},{9,11},{10,... | collective-permute-start | bytes 110600 | tf_op jit(solution)/shard_map/ppermute | solution.py:34
  146.6 3.0 %collective-permute-start.9 = (f32[6,1536]{1,0:T(8,128)S(1)}, f32[6,1536]{1,0:T(8,128)S(1)}, u32[]{:S(2)}, u32[]{:S(2)}) collective-permute-start(f32[6,1536]{1,0:T(8,128)S(1)} %add.101), channel_id=1, source_target_pairs={{0,4},{1,5},{2,6},{3,7},{4,0},{5,1},{6,2},{7,3},{8,12},{9,13},{10,... | collective-permute-start | bytes 110600 | tf_op jit(solution)/shard_map/ppermute | solution.py:34
  149.6 11.7 %collective-permute-start.10 = (f32[6,1536]{1,0:T(8,128)S(1)}, f32[6,1536]{1,0:T(8,128)S(1)}, u32[]{:S(2)}, u32[]{:S(2)}) collective-permute-start(f32[6,1536]{1,0:T(8,128)S(1)} %add.102), channel_id=1, source_target_pairs={{0,8},{1,9},{2,10},{3,11},{4,12},{5,13},{6,14},{7,15},{8,0},{9,1},... | collective-permute-start | bytes 110600 | tf_op jit(solution)/shard_map/ppermute | solution.py:34
  151.0 13.3 %copy-start.2 = (bf16[512,1536]{1,0:T(8,128)(2,1)S(1)}, bf16[512,1536]{1,0:T(8,128)(2,1)}, u32[]{:S(2)}) copy-start(bf16[512,1536]{1,0:T(8,128)(2,1)} %multiply_convert_fusion) | copy-start | bytes 4718596
  151.0 13.3 %copy-start.4 = (bf16[16,2,48,1536]{3,2,1,0:T(8,128)(2,1)S(1)}, bf16[16,2,48,1536]{3,2,1,0:T(8,128)(2,1)}, u32[]{:S(2)}) copy-start(bf16[16,2,48,1536]{3,2,1,0:T(8,128)(2,1)} %copy-done.3) | copy-start | bytes 14155780
  161.3 7.2 %collective-permute-start.11 = (f32[6,1536]{1,0:T(8,128)S(1)}, f32[6,1536]{1,0:T(8,128)S(1)}, u32[]{:S(2)}, u32[]{:S(2)}) collective-permute-start(f32[6,1536]{1,0:T(8,128)S(1)} %add.103), channel_id=1, source_target_pairs={{0,16},{16,0},{32,48},{48,32},{64,80},{80,64},{96,112},{112,96},{1... | collective-permute-start | bytes 110600 | tf_op jit(solution)/shard_map/ppermute | solution.py:34
  172.3 8.2 %collective-permute-start.12 = (f32[54,1536]{1,0:T(8,128)S(1)}, f32[54,1536]{1,0:T(8,128)S(1)}, u32[]{:S(2)}, u32[]{:S(2)}) collective-permute-start(f32[54,1536]{1,0:T(8,128)S(1)} %constant_dynamic-update-slice_fusion), channel_id=1, source_target_pairs={{0,32},{16,48},{32,0},{48,16},{64,96},{80,112},{96,64},{112,80},{1... | collective-permute-start | bytes 995336 | tf_op jit(solution)/shard_map/ppermute | solution.py:34
  180.5 8.9 %collective-permute-start.13 = (f32[54,1536]{1,0:T(8,128)S(1)}, f32[54,1536]{1,0:T(8,128)S(1)}, u32[]{:S(2)}, u32[]{:S(2)}) collective-permute-start(f32[54,1536]{1,0:T(8,128)S(1)} %add.109), channel_id=1, source_target_pairs={{0,64},{16,80},{32,96},{48,112},{64,0},{80,16},{96,32},{112,48},{1... | collective-permute-start | bytes 995336 | tf_op jit(solution)/shard_map/ppermute | solution.py:34
  189.5 6.5 %collective-permute-start.14 = (f32[54,1536]{1,0:T(8,128)S(1)}, f32[54,1536]{1,0:T(8,128)S(1)}, u32[]{:S(2)}, u32[]{:S(2)}) collective-permute-start(f32[54,1536]{1,0:T(8,128)S(1)} %add.110), channel_id=1, source_target_pairs={{0,128},{16,144},{32,160},{48,176},{64,192},{80,208},{96,224},{112... | collective-permute-start | bytes 995336 | tf_op jit(solution)/shard_map/ppermute | solution.py:34
  196.7 5.3 %collective-permute-start.15 = (f32[48,1536]{1,0:T(8,128)S(1)}, f32[48,1536]{1,0:T(8,128)S(1)}, u32[]{:S(2)}, u32[]{:S(2)}) collective-permute-start(f32[48,1536]{1,0:T(8,128)S(1)} %slice.144), channel_id=1, source_target_pairs={{0,16},{16,0},{32,48},{48,32},{64,80},{80,64},{96,112},{112,96},{1... | collective-permute-start | bytes 884744 | tf_op jit(solution)/shard_map/ppermute | solution.py:40
Sparse Core Ops, SparseCore 0:
  73.3 97.9 reduce-scatter.1

commit v9 on v8

--- a/solution.py
+++ b/solution.py
@@ -94,15 +94,13 @@
     split_act = activation.reshape(frames, fsdp_count, 2, half_rows)
     keep_act = lax.dynamic_index_in_dim(split_act, core, 2, keepdims=False).reshape(frames, -1)
     send_act = lax.dynamic_index_in_dim(split_act, 1 - core, 2, keepdims=False).reshape(frames, -1)
-    held, keep_act, send_act, activation = lax.optimization_barrier(
-        (held, keep_act, send_act, activation)
-    )
-    held = doubling_step(held, "fsdp", masks[3])
     chip_act = jnp.concatenate([keep_act, sibling(send_act)], axis=0)
     chip_cot = jnp.concatenate([grad_out, sibling_cot], axis=0)
     chip_terms = lax.dot_general(
         chip_act, chip_cot, (((0,), (0,)), ((), ())), preferred_element_type=jnp.float32
     )
+    held, chip_terms, activation = lax.optimization_barrier((held, chip_terms, activation))
+    held = doubling_step(held, "fsdp", masks[3])
     shard_sum = lax.psum_scatter(chip_terms, "fsdp", scatter_dimension=0, tiled=True)
     held, chip_terms = lax.optimization_barrier((held, chip_terms))
     gathered = doubling_order(held, masks)

time: 210 us -> 211 us (level)
  waiting for transfers between devices: 94.2 us -> 88.6 us
  matrix products: 12.3 us -> 15.2 us
  starting transfers between devices: 38.4 us -> 40.9 us
    ppermute x4, waiting for transfers between devices: 53.7 us -> 48.4 us  [doubling_step(): received = lax.ppermute(held, axis, [(i, i ^ mask) for i in range(size)])]
    dot_general x1, matrix products: 4.24 us -> 7.08 us  [shards(): lax.dot_general(chip_act, chip_cot, (((0,), (0,)), ((), ())), preferred_e...]
  transfers between devices with their start and end apart: 17 -> 17, of which waited for: 12 -> 11; matrix products, arithmetic and copies ran while one was open for 24% -> 26% of each run, Pallas kernels for 0% -> 0%
where the time goes in v9:
time: 211 us
  waiting for transfers between devices  88.6 us (42%)
  starting transfers between devices  40.9 us (19%)
  other arithmetic  40.8 us (19%)
  matrix products  15.2 us (7%)
  between operations  14.3 us (7%)
  local copies, waits for them, and re-layouts  10.7 us (5%)
    ppermute x4, waiting for transfers between devices, doubling_step(): received = lax.ppermute(held, axis, [(i, i ^ mask) for i in range(size)])  48.4 us
    ppermute x8, waiting for transfers between devices, butterfly(): x = x + lax.ppermute(x, axis, pairs)  31 us
    ppermute x8, starting transfers between devices, butterfly(): x = x + lax.ppermute(x, axis, pairs)  14.9 us
    ppermute x4, starting transfers between devices, doubling_step(): received = lax.ppermute(held, axis, [(i, i ^ mask) for i in range(size)])  13.1 us
    ppermute x4, starting transfers between devices, sibling(): return lax.ppermute(x, 'dp', [(i, i ^ 1) for i in range(size)])  12.8 us
    add x1, other arithmetic, shards(): grad_hidden + conv_kernel[k] * (back_views[count - 1 - k] * taps[count -...  10.3 us
    add x1, other arithmetic, shards(): mixed + conv_kernel[k] * views[k].astype(jnp.float32) * taps[k][:, None]  7.9 us
    dot_general x1, matrix products, shards(): lax.dot_general(chip_act, chip_cot, (((0,), (0,)), ((), ())), preferred_e...  7.08 us
  transfers between devices with their start and end apart: 17, of which 11 were waited for; matrix products, arithmetic and copies ran while one was open for 26% of the time, Pallas kernels for 0%

profile of v9, /device:TPU:1, one launch (start us, length us, event | category | flops | bytes accessed | tf_op | source)
XLA Modules:
  0.0 210.6 jit_solution(1751608545326150816)
XLA Ops:
  7.2 3.3 %collective-permute-start.1 = (bf16[512,1536]{1,0:T(8,128)(2,1)}, bf16[512,1536]{1,0:T(8,128)(2,1)S(1)}, u32[]{:S(2)}, u32[]{:S(2)}) collective-permute-start(bf16[512,1536]{1,0:T(8,128)(2,1)} %param.7), channel_id=1, source_target_pairs={{0,16},{16,0},{32,48},{48,32},{64,80},{80,64},{96,112},{112,96},{1... | collective-permute-start | bytes 4718600 | tf_op jit(solution)/shard_map/ppermute | solution.py:40
  10.5 5.4 %collective-permute-start = (bf16[1,48,1536]{2,1,0:T(8,128)(2,1)S(1)}, bf16[1,48,1536]{2,1,0:T(8,128)(2,1)S(1)}, u32[]{:S(2)}, u32[]{:S(2)}) collective-permute-start(bf16[1,48,1536]{2,1,0:T(8,128)(2,1)S(1)} %dynamic-slice_bitcast_fusion), channel_id=1, source_target_pairs={{0,2},{1,3},{2,0},{3,1},{4,6},{5,7},{6,4},{7,5},{8,10},{9,11},{10,... | collective-permute-start | bytes 442376 | tf_op jit(solution)/shard_map/ppermute | solution.py:46
  20.2 3.0 %collective-permute-start.2 = (bf16[2,48,1536]{2,1,0:T(8,128)(2,1)S(1)}, bf16[2,48,1536]{2,1,0:T(8,128)(2,1)S(1)}, u32[]{:S(2)}, u32[]{:S(2)}) collective-permute-start(bf16[2,48,1536]{2,1,0:T(8,128)(2,1)S(1)} %maximum_select_fusion.4), channel_id=1, source_target_pairs={{0,8},{1,9},{2,10},{3,11},{4,12},{5,13},{6,14},{7,15},{8,0},{9,1},... | collective-permute-start | bytes 884744 | tf_op jit(solution)/shard_map/ppermute | solution.py:46
  23.2 7.9 %fusion.7 = f32[512,1536]{1,0:T(8,128)S(1)} fusion(bf16[512,1536]{1,0:T(8,128)(2,1)} %param.6, f32[512]{0:T(512)S(1)} %bitcast.51, f32[1536]{0:T(1024)S(1)} %get-tuple-element.42, f32[512]{0:T(512)S(1)} %bitcast.54, f32[1536]{0:T(1024)S(1)} %get-tuple-element.43, f32[512]{0:T(512)S(1)} %bitcast.43, f32[1536]{0:T(1024)S(1)} %get-tuple-element.40, ...), kind=kLoop, calls=%fused_computation.19 | loop fusion | flops 14942208 | bytes 4759552 | tf_op jit(solution)/shard_map/add | solution.py:85
  32.7 4.2 %collective-permute-start.3 = (bf16[4,48,1536]{2,1,0:T(8,128)(2,1)}, bf16[4,48,1536]{2,1,0:T(8,128)(2,1)}, u32[]{:S(2)}, u32[]{:S(2)}) collective-permute-start(bf16[4,48,1536]{2,1,0:T(8,128)(2,1)} %maximum_select_fusion.2), channel_id=1, source_target_pairs={{0,1},{1,0},{2,3},{3,2},{4,5},{5,4},{6,7},{7,6},{8,9},{9,8},{10,11... | collective-permute-start | bytes 1769480 | tf_op jit(solution)/shard_map/ppermute | solution.py:46
  36.9 2.4 %multiply_convert_fusion = bf16[512,1536]{1,0:T(8,128)(2,1)} fusion(f32[512,1536]{1,0:T(8,128)S(1)} %fusion.7, f32[1536]{0:T(1024)S(1)} %copy-done.5, f32[512]{0:T(512)S(1)} %add_rsqrt_fusion, f32[512]{0:T(512)S(1)} %broadcast_multiply_fusion.2, f32[512]{0:T(512)S(1)} %bitcast.44), kind=kLoop, calls=%fused_computation.37 | loop fusion | flops 7077888 | bytes 4730880 | tf_op jit(solution)/shard_map/convert_element_type | solution.py:93
  39.3 2.6 %copy.18 = bf16[512,1536]{0,1:T(8,128)(2,1)} copy(bf16[512,1536]{1,0:T(8,128)(2,1)} %multiply_convert_fusion) | data formatting | bytes 3145728 | tf_op jit(solution)/shard_map/convert_element_type | solution.py:93
  41.9 2.6 %constant_dynamic-slice_fusion.1 = (bf16[512,16,1,48]{0,3,2,1:T(8,128)(2,1)}, bf16[512,16,1,48]{0,3,2,1:T(8,128)(2,1)}) fusion(bf16[512,16,2,48]{0,3,2,1:T(8,128)(2,1)} %bitcast.39, s32[]{:T(128)S(6)} %select_n.77, s32[]{:T(128)S(6)} %select_n.78), kind=kLoop, calls=%fused_computation.96 | loop fusion | bytes 3145736 | tf_op jit(solution)/shard_map/jit(dynamic_index_in_dim)/dynamic_slice | solution.py:95
  44.6 1.8 collective-permute-start.4
  46.4 16.1 %collective-permute-done.3 = bf16[4,48,1536]{2,1,0:T(8,128)(2,1)} collective-permute-done((bf16[4,48,1536]{2,1,0:T(8,128)(2,1)}, bf16[4,48,1536]{2,1,0:T(8,128)(2,1)}, u32[]{:S(2)}, u32[]{:S(2)}) %collective-permute-start.3) | collective-permute-done | bytes 589856 | tf_op jit(solution)/shard_map/ppermute | solution.py:46
  62.5 2.8 %maximum_select_fusion.1 = bf16[8,48,1536]{2,1,0:T(8,128)(2,1)} fusion(bf16[4,48,1536]{2,1,0:T(8,128)(2,1)} %maximum_select_fusion.2, bf16[4,48,1536]{2,1,0:T(8,128)(2,1)} %collective-permute-done.3, pred[]{:T(512)S(6)} %ne.18), kind=kLoop, calls=%fused_computation.51 | loop fusion | flops 1769472 | bytes 2359297 | tf_op jit(solution)/shard_map/jit(_where)/select_n | solution.py:47
  65.3 7.1 %fusion.17 = f32[768,1536]{1,0:T(8,128)} fusion(bf16[512,1536]{1,0:T(8,128)(2,1)} %copy-done.7, bf16[512,1536]{1,0:T(8,128)(2,1)} %param.7, bf16[512,768]{0,1:T(8,128)(2,1)} %collective-permute-done.4, bf16[512,768]{0,1:T(8,128)(2,1)} %bitcast.42), kind=kOutput, calls=%fused_computation.29 | convolution fusion | flops 2425356288 | bytes 9437184 | tf_op jit(solution)/shard_map/dot_general | solution.py:99
  72.9 32.3 %collective-permute-done.5 = bf16[8,48,1536]{2,1,0:T(8,128)(2,1)} collective-permute-done((bf16[8,48,1536]{2,1,0:T(8,128)(2,1)}, bf16[8,48,1536]{2,1,0:T(8,128)(2,1)}, u32[]{:S(2)}, u32[]{:S(2)}) %collective-permute-start.5) | collective-permute-done | bytes 1179680 | tf_op jit(solution)/shard_map/ppermute | solution.py:46
  105.2 2.6 %maximum_select_fusion = bf16[16,48,1536]{2,1,0:T(8,128)(2,1)S(1)} fusion(bf16[8,48,1536]{2,1,0:T(8,128)(2,1)} %maximum_select_fusion.1, bf16[8,48,1536]{2,1,0:T(8,128)(2,1)} %collective-permute-done.5, pred[]{:T(512)S(6)} %ne.22), kind=kLoop, calls=%fused_computation.42 | loop fusion | flops 3538944 | bytes 4718593 | tf_op jit(solution)/shard_map/jit(_where)/select_n | solution.py:47
  109.3 3.5 %collective-permute-start.6 = (bf16[768,1536]{1,0:T(8,128)(2,1)}, bf16[768,1536]{1,0:T(8,128)(2,1)}, u32[]{:S(2)}, u32[]{:S(2)}) collective-permute-start(bf16[768,1536]{1,0:T(8,128)(2,1)} %bitcast.14), channel_id=1, source_target_pairs={{0,16},{16,0},{32,48},{48,32},{64,80},{80,64},{96,112},{112,96},{1... | collective-permute-start | bytes 7077896 | tf_op jit(solution)/shard_map/ppermute | solution.py:40
  112.9 4.5 %collective-permute-done.6 = bf16[768,1536]{1,0:T(8,128)(2,1)} collective-permute-done((bf16[768,1536]{1,0:T(8,128)(2,1)}, bf16[768,1536]{1,0:T(8,128)(2,1)}, u32[]{:S(2)}, u32[]{:S(2)}) %collective-permute-start.6) | collective-permute-done | bytes 2359328 | tf_op jit(solution)/shard_map/ppermute | solution.py:40
  117.4 2.7 %broadcast_select_fusion.1 = (bf16[768,1536]{1,0:T(8,128)(2,1)S(1)}, bf16[768,1536]{1,0:T(8,128)(2,1)S(1)}) fusion(bf16[768,1536]{1,0:T(8,128)(2,1)} %collective-permute-done.6, pred[]{:T(512)S(6)} %eq.24, bf16[2,2,2,2,48,1536]{5,4,3,2,1,0:T(8,128)(2,1)} %copy.19), kind=kLoop, calls=%fused_computation.44 | loop fusion | flops 2359296 | bytes 9437185 | tf_op jit(solution)/shard_map/jit(_where)/select_n | solution.py:108
  121.6 3.8 %multiply_reduce_fusion = (f32[1536]{0:T(1024)S(1)}, f32[512]{0:T(512)S(1)}, f32[512]{0:T(512)S(1)}, f32[512,1536]{1,0:T(8,128)S(1)}) fusion(f32[512,1536]{1,0:T(8,128)S(1)} %fusion.7, f32[512]{0:T(512)S(1)} %add_rsqrt_fusion, f32[512]{0:T(512)S(1)} %broadcast_multiply_fusion.2, f32[1536]{0:T(1024)S(1)} %copy-done.5, f32[512]{0:T(512)S(1)} %bitcast.45, ...), kind=kOutput, calls=%fused_computation.34 | convolution fusion | flops 2430072320 | bytes 12605440 | tf_op jit(solution)/shard_map/dot_general | solution.py:112
  125.5 5.4 %fusion.16 = (f32[1536]{0:T(1024)S(1)}, f32[1536]{0:T(1024)S(1)}, f32[1536]{0:T(1024)S(1)}, f32[1536]{0:T(1024)S(1)}, f32[1536]{0:T(1024)S(1)}, /*index=5*/f32[512,1536]{1,0:T(8,128)}) fusion(f32[512]{0:T(512)S(1)} %bitcast.52, bf16[512,1536]{1,0:T(8,128)(2,1)S(1)} %copy-done.1, f32[512]{0:T(512)S(1)} %bitcast.55, f32[512]{0:T(512)S(1)} %bitcast.46, ...), kind=kLoop, calls=%fused_computation.28 | loop fusion | flops 21225984 | bytes 11065344 | tf_op jit(solution)/shard_map/reduce_sum | solution.py:126
  131.1 7.1 %collective-permute-done.7 = f32[6,1536]{1,0:T(8,128)S(1)} collective-permute-done((f32[6,1536]{1,0:T(8,128)S(1)}, f32[6,1536]{1,0:T(8,128)S(1)}, u32[]{:S(2)}, u32[]{:S(2)}) %collective-permute-start.7) | collective-permute-done | bytes 36896 | tf_op jit(solution)/shard_map/ppermute | solution.py:34
  138.2 4.8 %collective-permute-start.8 = (f32[6,1536]{1,0:T(8,128)S(1)}, f32[6,1536]{1,0:T(8,128)S(1)}, u32[]{:S(2)}, u32[]{:S(2)}) collective-permute-start(f32[6,1536]{1,0:T(8,128)S(1)} %add.100), channel_id=1, source_target_pairs={{0,2},{1,3},{2,0},{3,1},{4,6},{5,7},{6,4},{7,5},{8,10},{9,11},{10,... | collective-permute-start | bytes 110600 | tf_op jit(solution)/shard_map/ppermute | solution.py:34
  143.0 2.3 %collective-permute-done.8 = f32[6,1536]{1,0:T(8,128)S(1)} collective-permute-done((f32[6,1536]{1,0:T(8,128)S(1)}, f32[6,1536]{1,0:T(8,128)S(1)}, u32[]{:S(2)}, u32[]{:S(2)}) %collective-permute-start.8) | collective-permute-done | bytes 36896 | tf_op jit(solution)/shard_map/ppermute | solution.py:34
  145.4 2.9 %collective-permute-done.9 = f32[6,1536]{1,0:T(8,128)S(1)} collective-permute-done((f32[6,1536]{1,0:T(8,128)S(1)}, f32[6,1536]{1,0:T(8,128)S(1)}, u32[]{:S(2)}, u32[]{:S(2)}) %collective-permute-start.9) | collective-permute-done | bytes 36896 | tf_op jit(solution)/shard_map/ppermute | solution.py:34
  149.9 10.3 %multiply_add_fusion = f32[512,1536]{1,0:T(8,128)} fusion(f32[512,1536]{1,0:T(8,128)} %get-tuple-element.44, f32[512]{0:T(512)S(1)} %bitcast.53, f32[1536]{0:T(1024)S(1)} %get-tuple-element.42, f32[512]{0:T(512)S(1)} %bitcast.56, f32[1536]{0:T(1024)S(1)} %get-tuple-element.43, f32[512]{0:T(512)S(1)} %bitcast.47, f32[1536]{0:T(1024)S(1)} %get-tuple-element.40, ...), kind=kLoop, calls=%fused_computation.33 | loop fusion | flops 11010048 | bytes 6332416 | tf_op jit(solution)/shard_map/add | solution.py:130
  160.2 3.4 %collective-permute-start.11 = (f32[6,1536]{1,0:T(8,128)S(1)}, f32[6,1536]{1,0:T(8,128)S(1)}, u32[]{:S(2)}, u32[]{:S(2)}) collective-permute-start(f32[6,1536]{1,0:T(8,128)S(1)} %add.103), channel_id=1, source_target_pairs={{0,16},{16,0},{32,48},{48,32},{64,80},{80,64},{96,112},{112,96},{1... | collective-permute-start | bytes 110600 | tf_op jit(solution)/shard_map/ppermute | solution.py:34
  163.6 4.3 %fusion.40 = f32[512,1536]{1,0:T(8,128)} fusion(bf16[512,1536]{1,0:T(8,128)(2,1)S(1)} %copy-done.2, bf16[1536,1536]{1,0:T(8,128)(2,1)S(1)} %bitcast.41), kind=kOutput, calls=%fused_computation.99 | convolution fusion | flops 2415919104 | bytes 9437184 | tf_op jit(solution)/shard_map/dot_general | solution.py:111
  167.9 4.1 %reduce-scatter.2.cloned.1.call-done = f32[48,1536]{1,0:T(8,128)} async-done(((f32[768,1536]{1,0:T(8,128)}), f32[48,1536]{1,0:T(8,128)}) %reduce-scatter.2.cloned.1.call-update) | async-done | bytes 294928 | tf_op jit(solution)/shard_map/reduce_scatter | solution.py:104
  174.7 6.5 %collective-permute-done.12 = f32[54,1536]{1,0:T(8,128)S(1)} collective-permute-done((f32[54,1536]{1,0:T(8,128)S(1)}, f32[54,1536]{1,0:T(8,128)S(1)}, u32[]{:S(2)}, u32[]{:S(2)}) %collective-permute-start.12) | collective-permute-done | bytes 331808 | tf_op jit(solution)/shard_map/ppermute | solution.py:34
  181.3 3.2 %collective-permute-start.13 = (f32[54,1536]{1,0:T(8,128)S(1)}, f32[54,1536]{1,0:T(8,128)S(1)}, u32[]{:S(2)}, u32[]{:S(2)}) collective-permute-start(f32[54,1536]{1,0:T(8,128)S(1)} %add.109), channel_id=1, source_target_pairs={{0,64},{16,80},{32,96},{48,112},{64,0},{80,16},{96,32},{112,48},{1... | collective-permute-start | bytes 995336 | tf_op jit(solution)/shard_map/ppermute | solution.py:34
  184.4 5.8 %collective-permute-done.13 = f32[54,1536]{1,0:T(8,128)S(1)} collective-permute-done((f32[54,1536]{1,0:T(8,128)S(1)}, f32[54,1536]{1,0:T(8,128)S(1)}, u32[]{:S(2)}, u32[]{:S(2)}) %collective-permute-start.13) | collective-permute-done | bytes 331808 | tf_op jit(solution)/shard_map/ppermute | solution.py:34
  190.4 6.4 %collective-permute-done.14 = f32[54,1536]{1,0:T(8,128)S(1)} collective-permute-done((f32[54,1536]{1,0:T(8,128)S(1)}, f32[54,1536]{1,0:T(8,128)S(1)}, u32[]{:S(2)}, u32[]{:S(2)}) %collective-permute-start.14) | collective-permute-done | bytes 331808 | tf_op jit(solution)/shard_map/ppermute | solution.py:34
  197.5 4.2 %collective-permute-start.15 = (f32[48,1536]{1,0:T(8,128)S(1)}, f32[48,1536]{1,0:T(8,128)S(1)}, u32[]{:S(2)}, u32[]{:S(2)}) collective-permute-start(f32[48,1536]{1,0:T(8,128)S(1)} %slice.144), channel_id=1, source_target_pairs={{0,16},{16,0},{32,48},{48,32},{64,80},{80,64},{96,112},{112,96},{1... | collective-permute-start | bytes 884744 | tf_op jit(solution)/shard_map/ppermute | solution.py:40
  (76 shorter events, 16.7 us)
Async XLA Ops:
  7.2 3.4 %copy-start = (bf16[96,1536]{1,0:T(8,128)(2,1)S(1)}, bf16[96,1536]{1,0:T(8,128)(2,1)}, u32[]{:S(2)}) copy-start(bf16[96,1536]{1,0:T(8,128)(2,1)} %param.11) | copy-start | bytes 884740
  7.2 164.9 %reduce-scatter.2.cloned.1.call-start = ((), (), s32[]{:S(2)}) async-start(), calls=%async_computation.1 | async-start | bytes 5013504 | tf_op jit(solution)/shard_map/reduce_scatter | solution.py:104
  7.2 12.9 %collective-permute-start.1 = (bf16[512,1536]{1,0:T(8,128)(2,1)}, bf16[512,1536]{1,0:T(8,128)(2,1)S(1)}, u32[]{:S(2)}, u32[]{:S(2)}) collective-permute-start(bf16[512,1536]{1,0:T(8,128)(2,1)} %param.7), channel_id=1, source_target_pairs={{0,16},{16,0},{32,48},{48,32},{64,80},{80,64},{96,112},{112,96},{1... | collective-permute-start | bytes 4718600 | tf_op jit(solution)/shard_map/ppermute | solution.py:40
  10.5 9.6 %collective-permute-start = (bf16[1,48,1536]{2,1,0:T(8,128)(2,1)S(1)}, bf16[1,48,1536]{2,1,0:T(8,128)(2,1)S(1)}, u32[]{:S(2)}, u32[]{:S(2)}) collective-permute-start(bf16[1,48,1536]{2,1,0:T(8,128)(2,1)S(1)} %dynamic-slice_bitcast_fusion), channel_id=1, source_target_pairs={{0,2},{1,3},{2,0},{3,1},{4,6},{5,7},{6,4},{7,5},{8,10},{9,11},{10,... | collective-permute-start | bytes 442376 | tf_op jit(solution)/shard_map/ppermute | solution.py:46
  20.1 3.0 %copy-start.7 = (bf16[512,1536]{1,0:T(8,128)(2,1)}, bf16[512,1536]{1,0:T(8,128)(2,1)S(1)}, u32[]{:S(2)}) copy-start(bf16[512,1536]{1,0:T(8,128)(2,1)S(1)} %collective-permute-done.1) | copy-start | bytes 4718596
  20.2 10.9 %collective-permute-start.2 = (bf16[2,48,1536]{2,1,0:T(8,128)(2,1)S(1)}, bf16[2,48,1536]{2,1,0:T(8,128)(2,1)S(1)}, u32[]{:S(2)}, u32[]{:S(2)}) collective-permute-start(bf16[2,48,1536]{2,1,0:T(8,128)(2,1)S(1)} %maximum_select_fusion.4), channel_id=1, source_target_pairs={{0,8},{1,9},{2,10},{3,11},{4,12},{5,13},{6,14},{7,15},{8,0},{9,1},... | collective-permute-start | bytes 884744 | tf_op jit(solution)/shard_map/ppermute | solution.py:46
  32.0 4.9 %copy-start.5 = (f32[1536]{0:T(1024)S(1)}, f32[1536]{0:T(1024)}, u32[]{:S(2)}) copy-start(f32[1536]{0:T(1024)} %param.10) | copy-start | bytes 18436
  32.7 29.8 %collective-permute-start.3 = (bf16[4,48,1536]{2,1,0:T(8,128)(2,1)}, bf16[4,48,1536]{2,1,0:T(8,128)(2,1)}, u32[]{:S(2)}, u32[]{:S(2)}) collective-permute-start(bf16[4,48,1536]{2,1,0:T(8,128)(2,1)} %maximum_select_fusion.2), channel_id=1, source_target_pairs={{0,1},{1,0},{2,3},{3,2},{4,5},{5,4},{6,7},{7,6},{8,9},{9,8},{10,11... | collective-permute-start | bytes 1769480 | tf_op jit(solution)/shard_map/ppermute | solution.py:46
  44.6 20.8 %collective-permute-start.4 = (bf16[512,768]{0,1:T(8,128)(2,1)}, bf16[512,768]{0,1:T(8,128)(2,1)}, u32[]{:S(2)}, u32[]{:S(2)}) collective-permute-start(bf16[512,768]{0,1:T(8,128)(2,1)} %bitcast.11), channel_id=1, source_target_pairs={{0,16},{16,0},{32,48},{48,32},{64,80},{80,64},{96,112},{112,96},{1... | collective-permute-start | bytes 2359304 | tf_op jit(solution)/shard_map/ppermute | solution.py:40
  72.4 32.8 %collective-permute-start.5 = (bf16[8,48,1536]{2,1,0:T(8,128)(2,1)}, bf16[8,48,1536]{2,1,0:T(8,128)(2,1)}, u32[]{:S(2)}, u32[]{:S(2)}) collective-permute-start(bf16[8,48,1536]{2,1,0:T(8,128)(2,1)} %maximum_select_fusion.1), channel_id=1, source_target_pairs={{0,4},{1,5},{2,6},{3,7},{4,0},{5,1},{6,2},{7,3},{8,12},{9,13},{10,... | collective-permute-start | bytes 3538952 | tf_op jit(solution)/shard_map/ppermute | solution.py:46
  109.3 8.0 %collective-permute-start.6 = (bf16[768,1536]{1,0:T(8,128)(2,1)}, bf16[768,1536]{1,0:T(8,128)(2,1)}, u32[]{:S(2)}, u32[]{:S(2)}) collective-permute-start(bf16[768,1536]{1,0:T(8,128)(2,1)} %bitcast.14), channel_id=1, source_target_pairs={{0,16},{16,0},{32,48},{48,32},{64,80},{80,64},{96,112},{112,96},{1... | collective-permute-start | bytes 7077896 | tf_op jit(solution)/shard_map/ppermute | solution.py:40
  120.1 1.5 copy-start.6
  120.6 4.9 %copy-start.3 = (bf16[16,2,48,1536]{3,2,1,0:T(8,128)(2,1)}, bf16[16,2,48,1536]{3,2,1,0:T(8,128)(2,1)S(1)}, u32[]{:S(2)}) copy-start(bf16[16,2,48,1536]{3,2,1,0:T(8,128)(2,1)S(1)} %pad_maximum_fusion) | copy-start | bytes 14155780
  121.6 3.9 %copy-start.1 = (bf16[512,1536]{1,0:T(8,128)(2,1)S(1)}, bf16[512,1536]{1,0:T(8,128)(2,1)}, u32[]{:S(2)}) copy-start(bf16[512,1536]{1,0:T(8,128)(2,1)} %param.6) | copy-start | bytes 4718596
  131.0 7.2 %collective-permute-start.7 = (f32[6,1536]{1,0:T(8,128)S(1)}, f32[6,1536]{1,0:T(8,128)S(1)}, u32[]{:S(2)}, u32[]{:S(2)}) collective-permute-start(f32[6,1536]{1,0:T(8,128)S(1)} %concatenate.56), channel_id=1, source_target_pairs={{0,1},{1,0},{2,3},{3,2},{4,5},{5,4},{6,7},{7,6},{8,9},{9,8},{10,11... | collective-permute-start | bytes 110600 | tf_op jit(solution)/shard_map/ppermute | solution.py:34
  138.2 7.1 %collective-permute-start.8 = (f32[6,1536]{1,0:T(8,128)S(1)}, f32[6,1536]{1,0:T(8,128)S(1)}, u32[]{:S(2)}, u32[]{:S(2)}) collective-permute-start(f32[6,1536]{1,0:T(8,128)S(1)} %add.100), channel_id=1, source_target_pairs={{0,2},{1,3},{2,0},{3,1},{4,6},{5,7},{6,4},{7,5},{8,10},{9,11},{10,... | collective-permute-start | bytes 110600 | tf_op jit(solution)/shard_map/ppermute | solution.py:34
  145.3 3.0 %collective-permute-start.9 = (f32[6,1536]{1,0:T(8,128)S(1)}, f32[6,1536]{1,0:T(8,128)S(1)}, u32[]{:S(2)}, u32[]{:S(2)}) collective-permute-start(f32[6,1536]{1,0:T(8,128)S(1)} %add.101), channel_id=1, source_target_pairs={{0,4},{1,5},{2,6},{3,7},{4,0},{5,1},{6,2},{7,3},{8,12},{9,13},{10,... | collective-permute-start | bytes 110600 | tf_op jit(solution)/shard_map/ppermute | solution.py:34
  148.4 11.8 %collective-permute-start.10 = (f32[6,1536]{1,0:T(8,128)S(1)}, f32[6,1536]{1,0:T(8,128)S(1)}, u32[]{:S(2)}, u32[]{:S(2)}) collective-permute-start(f32[6,1536]{1,0:T(8,128)S(1)} %add.102), channel_id=1, source_target_pairs={{0,8},{1,9},{2,10},{3,11},{4,12},{5,13},{6,14},{7,15},{8,0},{9,1},... | collective-permute-start | bytes 110600 | tf_op jit(solution)/shard_map/ppermute | solution.py:34
  149.9 13.8 %copy-start.2 = (bf16[512,1536]{1,0:T(8,128)(2,1)S(1)}, bf16[512,1536]{1,0:T(8,128)(2,1)}, u32[]{:S(2)}) copy-start(bf16[512,1536]{1,0:T(8,128)(2,1)} %multiply_convert_fusion) | copy-start | bytes 4718596
  149.9 13.8 %copy-start.4 = (bf16[16,2,48,1536]{3,2,1,0:T(8,128)(2,1)S(1)}, bf16[16,2,48,1536]{3,2,1,0:T(8,128)(2,1)}, u32[]{:S(2)}) copy-start(bf16[16,2,48,1536]{3,2,1,0:T(8,128)(2,1)} %copy-done.3) | copy-start | bytes 14155780
  160.2 7.7 %collective-permute-start.11 = (f32[6,1536]{1,0:T(8,128)S(1)}, f32[6,1536]{1,0:T(8,128)S(1)}, u32[]{:S(2)}, u32[]{:S(2)}) collective-permute-start(f32[6,1536]{1,0:T(8,128)S(1)} %add.103), channel_id=1, source_target_pairs={{0,16},{16,0},{32,48},{48,32},{64,80},{80,64},{96,112},{112,96},{1... | collective-permute-start | bytes 110600 | tf_op jit(solution)/shard_map/ppermute | solution.py:34
  173.1 8.2 %collective-permute-start.12 = (f32[54,1536]{1,0:T(8,128)S(1)}, f32[54,1536]{1,0:T(8,128)S(1)}, u32[]{:S(2)}, u32[]{:S(2)}) collective-permute-start(f32[54,1536]{1,0:T(8,128)S(1)} %constant_dynamic-update-slice_fusion), channel_id=1, source_target_pairs={{0,32},{16,48},{32,0},{48,16},{64,96},{80,112},{96,64},{112,80},{1... | collective-permute-start | bytes 995336 | tf_op jit(solution)/shard_map/ppermute | solution.py:34
  181.3 9.0 %collective-permute-start.13 = (f32[54,1536]{1,0:T(8,128)S(1)}, f32[54,1536]{1,0:T(8,128)S(1)}, u32[]{:S(2)}, u32[]{:S(2)}) collective-permute-start(f32[54,1536]{1,0:T(8,128)S(1)} %add.109), channel_id=1, source_target_pairs={{0,64},{16,80},{32,96},{48,112},{64,0},{80,16},{96,32},{112,48},{1... | collective-permute-start | bytes 995336 | tf_op jit(solution)/shard_map/ppermute | solution.py:34
  190.3 6.5 %collective-permute-start.14 = (f32[54,1536]{1,0:T(8,128)S(1)}, f32[54,1536]{1,0:T(8,128)S(1)}, u32[]{:S(2)}, u32[]{:S(2)}) collective-permute-start(f32[54,1536]{1,0:T(8,128)S(1)} %add.110), channel_id=1, source_target_pairs={{0,128},{16,144},{32,160},{48,176},{64,192},{80,208},{96,224},{112... | collective-permute-start | bytes 995336 | tf_op jit(solution)/shard_map/ppermute | solution.py:34
  197.5 5.4 %collective-permute-start.15 = (f32[48,1536]{1,0:T(8,128)S(1)}, f32[48,1536]{1,0:T(8,128)S(1)}, u32[]{:S(2)}, u32[]{:S(2)}) collective-permute-start(f32[48,1536]{1,0:T(8,128)S(1)} %slice.144), channel_id=1, source_target_pairs={{0,16},{16,0},{32,48},{48,32},{64,80},{80,64},{96,112},{112,96},{1... | collective-permute-start | bytes 884744 | tf_op jit(solution)/shard_map/ppermute | solution.py:40
Sparse Core Ops, SparseCore 0:
  72.6 99.4 reduce-scatter.1

commit v10 on v8

--- a/solution.py
+++ b/solution.py
@@ -100,7 +100,8 @@
     held = doubling_step(held, "fsdp", masks[3])
     chip_act = jnp.concatenate([keep_act, sibling(send_act)], axis=0)
     chip_cot = jnp.concatenate([grad_out, sibling_cot], axis=0)
-    chip_terms = lax.dot_general(
+    factor = 1.0 / math.sqrt(frames * dp_count * fsdp_count)
+    chip_terms = factor * lax.dot_general(
         chip_act, chip_cot, (((0,), (0,)), ((), ())), preferred_element_type=jnp.float32
     )
     shard_sum = lax.psum_scatter(chip_terms, "fsdp", scatter_dimension=0, tiled=True)
@@ -132,7 +133,7 @@
         grad_hidden = grad_hidden + conv_kernel[k] * (
             back_views[count - 1 - k] * taps[count - 1 - k][:, None]
         )
-    small = jnp.concatenate([jnp.stack(kernel_rows), gain_grad[None]], axis=0)
+    small = factor * jnp.concatenate([jnp.stack(kernel_rows), gain_grad[None]], axis=0)
     small = butterfly(small, "fsdp", (1, 2, 4, 8))
     small = butterfly(small, "dp", (1,))
     shard_sum, small, output, grad_hidden = lax.optimization_barrier(
@@ -147,14 +148,7 @@
         jnp.concatenate([half_sum, other_sum], axis=0),
         jnp.concatenate([other_sum, half_sum], axis=0),
     )
-    factor = 1.0 / math.sqrt(frames * dp_count * fsdp_count)
-    return (
-        output,
-        grad_hidden,
-        weight_sum * factor,
-        small[:count] * factor,
-        small[count] * factor,
-    )
+    return (output, grad_hidden, weight_sum, small[:count], small[count])
 
 
 def solution(mesh):

time: 210 us -> 211 us (level)
  waiting for transfers between devices: 94.2 us -> 98 us
  starting transfers between devices: 38.4 us -> 35.2 us
    ppermute x4, waiting for transfers between devices: 53.7 us -> 44.8 us  [doubling_step(): received = lax.ppermute(held, axis, [(i, i ^ mask) for i in range(size)])]
    reduce_scatter x1, waiting for transfers between devices: 2.73 us -> 10.6 us  [shards(): lax.psum_scatter(chip_terms, 'fsdp', scatter_dimension=0, tiled=True)]
    ppermute x8, waiting for transfers between devices: 30.8 us -> 36.5 us  [butterfly(): x = x + lax.ppermute(x, axis, pairs)]
    ppermute x8, starting transfers between devices: 14.4 us -> 11.7 us  [butterfly(): x = x + lax.ppermute(x, axis, pairs)]
    mul x3 -> x1, other arithmetic: 2.12 us -> 0.01 us  [shards(): factor * jnp.concatenate([jnp.stack(kernel_rows), gain_grad[None]], axis=0)]
  transfers between devices with their start and end apart: 17 -> 17, of which waited for: 12 -> 11; matrix products, arithmetic and copies ran while one was open for 24% -> 26% of each run, Pallas kernels for 0% -> 0%
where the time goes in v10:
time: 211 us
  waiting for transfers between devices  98 us (46%)
  other arithmetic  39.6 us (19%)
  starting transfers between devices  35.2 us (17%)
  between operations  14.4 us (7%)
  matrix products  12.3 us (6%)
  local copies, waits for them, and re-layouts  11.1 us (5%)
    ppermute x4, waiting for transfers between devices, doubling_step(): received = lax.ppermute(held, axis, [(i, i ^ mask) for i in range(size)])  44.8 us
    ppermute x8, waiting for transfers between devices, butterfly(): x = x + lax.ppermute(x, axis, pairs)  36.5 us
    ppermute x4, starting transfers between devices, doubling_step(): received = lax.ppermute(held, axis, [(i, i ^ mask) for i in range(size)])  13.1 us
    ppermute x8, starting transfers between devices, butterfly(): x = x + lax.ppermute(x, axis, pairs)  11.7 us
    reduce_scatter x1, waiting for transfers between devices, shards(): lax.psum_scatter(chip_terms, 'fsdp', scatter_dimension=0, tiled=True)  10.6 us
    ppermute x4, starting transfers between devices, sibling(): return lax.ppermute(x, 'dp', [(i, i ^ 1) for i in range(size)])  10.4 us
    add x1, other arithmetic, shards(): grad_hidden + conv_kernel[k] * (back_views[count - 1 - k] * taps[count -...  10.3 us
    add x1, other arithmetic, shards(): mixed + conv_kernel[k] * views[k].astype(jnp.float32) * taps[k][:, None]  7.9 us
  transfers between devices with their start and end apart: 17, of which 11 were waited for; matrix products, arithmetic and copies ran while one was open for 26% of the time, Pallas kernels for 0%

profile of v10, /device:TPU:1, one launch (start us, length us, event | category | flops | bytes accessed | tf_op | source)
XLA Modules:
  0.0 210.6 jit_solution(10238308053787265265)
XLA Ops:
  7.2 3.3 %collective-permute-start.1 = (bf16[512,1536]{1,0:T(8,128)(2,1)}, bf16[512,1536]{1,0:T(8,128)(2,1)S(1)}, u32[]{:S(2)}, u32[]{:S(2)}) collective-permute-start(bf16[512,1536]{1,0:T(8,128)(2,1)} %param.7), channel_id=1, source_target_pairs={{0,16},{16,0},{32,48},{48,32},{64,80},{80,64},{96,112},{112,96},{1... | collective-permute-start | bytes 4718600 | tf_op jit(solution)/shard_map/ppermute | solution.py:40
  10.5 5.4 %collective-permute-start = (bf16[1,48,1536]{2,1,0:T(8,128)(2,1)S(1)}, bf16[1,48,1536]{2,1,0:T(8,128)(2,1)S(1)}, u32[]{:S(2)}, u32[]{:S(2)}) collective-permute-start(bf16[1,48,1536]{2,1,0:T(8,128)(2,1)S(1)} %dynamic-slice_bitcast_fusion), channel_id=1, source_target_pairs={{0,2},{1,3},{2,0},{3,1},{4,6},{5,7},{6,4},{7,5},{8,10},{9,11},{10,... | collective-permute-start | bytes 442376 | tf_op jit(solution)/shard_map/ppermute | solution.py:46
  20.2 3.0 %collective-permute-start.2 = (bf16[2,48,1536]{2,1,0:T(8,128)(2,1)S(1)}, bf16[2,48,1536]{2,1,0:T(8,128)(2,1)S(1)}, u32[]{:S(2)}, u32[]{:S(2)}) collective-permute-start(bf16[2,48,1536]{2,1,0:T(8,128)(2,1)S(1)} %maximum_select_fusion.4), channel_id=1, source_target_pairs={{0,8},{1,9},{2,10},{3,11},{4,12},{5,13},{6,14},{7,15},{8,0},{9,1},... | collective-permute-start | bytes 884744 | tf_op jit(solution)/shard_map/ppermute | solution.py:46
  23.2 7.9 %fusion.7 = f32[512,1536]{1,0:T(8,128)S(1)} fusion(bf16[512,1536]{1,0:T(8,128)(2,1)} %param.6, f32[512]{0:T(512)S(1)} %bitcast.52, f32[1536]{0:T(1024)S(1)} %get-tuple-element.44, f32[512]{0:T(512)S(1)} %bitcast.55, f32[1536]{0:T(1024)S(1)} %get-tuple-element.45, f32[512]{0:T(512)S(1)} %bitcast.44, f32[1536]{0:T(1024)S(1)} %get-tuple-element.42, ...), kind=kLoop, calls=%fused_computation.20 | loop fusion | flops 14942208 | bytes 4759552 | tf_op jit(solution)/shard_map/add | solution.py:85
  32.7 4.2 %collective-permute-start.3 = (bf16[4,48,1536]{2,1,0:T(8,128)(2,1)}, bf16[4,48,1536]{2,1,0:T(8,128)(2,1)}, u32[]{:S(2)}, u32[]{:S(2)}) collective-permute-start(bf16[4,48,1536]{2,1,0:T(8,128)(2,1)} %maximum_select_fusion.2), channel_id=1, source_target_pairs={{0,1},{1,0},{2,3},{3,2},{4,5},{5,4},{6,7},{7,6},{8,9},{9,8},{10,11... | collective-permute-start | bytes 1769480 | tf_op jit(solution)/shard_map/ppermute | solution.py:46
  36.9 2.4 %multiply_convert_fusion = bf16[512,1536]{1,0:T(8,128)(2,1)} fusion(f32[512,1536]{1,0:T(8,128)S(1)} %fusion.7, f32[1536]{0:T(1024)S(1)} %copy-done.5, f32[512]{0:T(512)S(1)} %add_rsqrt_fusion, f32[512]{0:T(512)S(1)} %broadcast_multiply_fusion.3, f32[512]{0:T(512)S(1)} %bitcast.45), kind=kLoop, calls=%fused_computation.37 | loop fusion | flops 7077888 | bytes 4730880 | tf_op jit(solution)/shard_map/convert_element_type | solution.py:93
  39.3 2.6 %copy.18 = bf16[512,1536]{0,1:T(8,128)(2,1)} copy(bf16[512,1536]{1,0:T(8,128)(2,1)} %multiply_convert_fusion) | data formatting | bytes 3145728 | tf_op jit(solution)/shard_map/convert_element_type | solution.py:93
  41.9 1.6 constant_dynamic-slice_fusion
  43.6 18.9 %collective-permute-done.3 = bf16[4,48,1536]{2,1,0:T(8,128)(2,1)} collective-permute-done((bf16[4,48,1536]{2,1,0:T(8,128)(2,1)}, bf16[4,48,1536]{2,1,0:T(8,128)(2,1)}, u32[]{:S(2)}, u32[]{:S(2)}) %collective-permute-start.3) | collective-permute-done | bytes 589856 | tf_op jit(solution)/shard_map/ppermute | solution.py:46
  62.5 2.8 %maximum_select_fusion.1 = bf16[8,48,1536]{2,1,0:T(8,128)(2,1)} fusion(bf16[4,48,1536]{2,1,0:T(8,128)(2,1)} %maximum_select_fusion.2, bf16[4,48,1536]{2,1,0:T(8,128)(2,1)} %collective-permute-done.3, pred[]{:T(512)S(6)} %ne.18), kind=kLoop, calls=%fused_computation.51 | loop fusion | flops 1769472 | bytes 2359297 | tf_op jit(solution)/shard_map/jit(_where)/select_n | solution.py:47
  65.3 1.7 collective-permute-start.4
  68.9 4.2 %convolution_multiply_fusion = f32[768,1536]{1,0:T(8,128)} fusion(bf16[512,1536]{1,0:T(8,128)(2,1)S(1)} %copy-done.9, bf16[512,1536]{1,0:T(8,128)(2,1)S(1)} %copy-done.6, bf16[512,768]{0,1:T(8,128)(2,1)S(1)} %collective-permute-done.4, bf16[512,768]{0,1:T(8,128)(2,1)S(1)} %bitcast.42), kind=kOutput, calls=%fused_computation.1 | convolution fusion | flops 2426535936 | bytes 9437184 | tf_op jit(solution)/shard_map/dot_general | solution.py:104
  73.2 25.9 %collective-permute-done.5 = bf16[8,48,1536]{2,1,0:T(8,128)(2,1)} collective-permute-done((bf16[8,48,1536]{2,1,0:T(8,128)(2,1)}, bf16[8,48,1536]{2,1,0:T(8,128)(2,1)}, u32[]{:S(2)}, u32[]{:S(2)}) %collective-permute-start.5) | collective-permute-done | bytes 1179680 | tf_op jit(solution)/shard_map/ppermute | solution.py:46
  99.0 2.7 %maximum_select_fusion = bf16[16,48,1536]{2,1,0:T(8,128)(2,1)S(1)} fusion(bf16[8,48,1536]{2,1,0:T(8,128)(2,1)} %maximum_select_fusion.1, bf16[8,48,1536]{2,1,0:T(8,128)(2,1)} %collective-permute-done.5, pred[]{:T(512)S(6)} %ne.22), kind=kLoop, calls=%fused_computation.42 | loop fusion | flops 3538944 | bytes 4718593 | tf_op jit(solution)/shard_map/jit(_where)/select_n | solution.py:47
  101.7 1.6 copy.19
  104.6 4.5 %collective-permute-done.6 = bf16[768,1536]{1,0:T(8,128)(2,1)} collective-permute-done((bf16[768,1536]{1,0:T(8,128)(2,1)}, bf16[768,1536]{1,0:T(8,128)(2,1)}, u32[]{:S(2)}, u32[]{:S(2)}) %collective-permute-start.6) | collective-permute-done | bytes 2359328 | tf_op jit(solution)/shard_map/ppermute | solution.py:40
  109.1 2.7 %broadcast_select_fusion.1 = (bf16[768,1536]{1,0:T(8,128)(2,1)S(1)}, bf16[768,1536]{1,0:T(8,128)(2,1)S(1)}) fusion(bf16[768,1536]{1,0:T(8,128)(2,1)} %collective-permute-done.6, pred[]{:T(512)S(6)} %eq.24, bf16[2,2,2,2,48,1536]{5,4,3,2,1,0:T(8,128)(2,1)} %copy.19), kind=kLoop, calls=%fused_computation.44 | loop fusion | flops 2359296 | bytes 9437185 | tf_op jit(solution)/shard_map/jit(_where)/select_n | solution.py:111
  113.5 3.8 %multiply_reduce_fusion = (f32[1536]{0:T(1024)S(1)}, f32[512]{0:T(512)S(1)}, f32[512]{0:T(512)S(1)}, f32[512,1536]{1,0:T(8,128)S(1)}) fusion(f32[512,1536]{1,0:T(8,128)S(1)} %fusion.7, f32[512]{0:T(512)S(1)} %add_rsqrt_fusion, f32[512]{0:T(512)S(1)} %broadcast_multiply_fusion.3, f32[1536]{0:T(1024)S(1)} %copy-done.5, f32[512]{0:T(512)S(1)} %bitcast.46, ...), kind=kOutput, calls=%fused_computation.34 | convolution fusion | flops 2430072320 | bytes 12605440 | tf_op jit(solution)/shard_map/dot_general | solution.py:115
  117.3 5.4 %fusion.16 = (f32[1536]{0:T(1024)S(1)}, f32[1536]{0:T(1024)S(1)}, f32[1536]{0:T(1024)S(1)}, f32[1536]{0:T(1024)S(1)}, f32[1536]{0:T(1024)S(1)}, /*index=5*/f32[512,1536]{1,0:T(8,128)}) fusion(f32[512]{0:T(512)S(1)} %bitcast.53, bf16[512,1536]{1,0:T(8,128)(2,1)S(1)} %copy-done.1, f32[512]{0:T(512)S(1)} %bitcast.56, f32[512]{0:T(512)S(1)} %bitcast.47, ...), kind=kLoop, calls=%fused_computation.29 | loop fusion | flops 21225984 | bytes 11065344 | tf_op jit(solution)/shard_map/reduce_sum | solution.py:129
  123.0 7.9 %collective-permute-done.7 = f32[6,1536]{1,0:T(8,128)S(1)} collective-permute-done((f32[6,1536]{1,0:T(8,128)S(1)}, f32[6,1536]{1,0:T(8,128)S(1)}, u32[]{:S(2)}, u32[]{:S(2)}) %collective-permute-start.7) | collective-permute-done | bytes 36896 | tf_op jit(solution)/shard_map/ppermute | solution.py:34
  130.9 5.6 %collective-permute-start.8 = (f32[6,1536]{1,0:T(8,128)S(1)}, f32[6,1536]{1,0:T(8,128)S(1)}, u32[]{:S(2)}, u32[]{:S(2)}) collective-permute-start(f32[6,1536]{1,0:T(8,128)S(1)} %fusion.36), channel_id=1, source_target_pairs={{0,2},{1,3},{2,0},{3,1},{4,6},{5,7},{6,4},{7,5},{8,10},{9,11},{10,... | collective-permute-start | bytes 110600 | tf_op jit(solution)/shard_map/ppermute | solution.py:34
  136.5 5.4 %collective-permute-done.8 = f32[6,1536]{1,0:T(8,128)S(1)} collective-permute-done((f32[6,1536]{1,0:T(8,128)S(1)}, f32[6,1536]{1,0:T(8,128)S(1)}, u32[]{:S(2)}, u32[]{:S(2)}) %collective-permute-start.8) | collective-permute-done | bytes 36896 | tf_op jit(solution)/shard_map/ppermute | solution.py:34
  142.0 3.2 %collective-permute-done.9 = f32[6,1536]{1,0:T(8,128)S(1)} collective-permute-done((f32[6,1536]{1,0:T(8,128)S(1)}, f32[6,1536]{1,0:T(8,128)S(1)}, u32[]{:S(2)}, u32[]{:S(2)}) %collective-permute-start.9) | collective-permute-done | bytes 36896 | tf_op jit(solution)/shard_map/ppermute | solution.py:34
  145.3 10.3 %multiply_add_fusion = f32[512,1536]{1,0:T(8,128)} fusion(f32[512,1536]{1,0:T(8,128)} %get-tuple-element.46, f32[512]{0:T(512)S(1)} %bitcast.54, f32[1536]{0:T(1024)S(1)} %get-tuple-element.44, f32[512]{0:T(512)S(1)} %bitcast.57, f32[1536]{0:T(1024)S(1)} %get-tuple-element.45, f32[512]{0:T(512)S(1)} %bitcast.48, f32[1536]{0:T(1024)S(1)} %get-tuple-element.42, ...), kind=kLoop, calls=%fused_computation.33 | loop fusion | flops 11010048 | bytes 6332416 | tf_op jit(solution)/shard_map/add | solution.py:133
  155.7 2.0 collective-permute-start.11
  157.7 4.3 %fusion.38 = f32[512,1536]{1,0:T(8,128)} fusion(bf16[512,1536]{1,0:T(8,128)(2,1)S(1)} %copy-done.2, bf16[1536,1536]{1,0:T(8,128)(2,1)S(1)} %bitcast.41), kind=kOutput, calls=%fused_computation.98 | convolution fusion | flops 2415919104 | bytes 9437184 | tf_op jit(solution)/shard_map/dot_general | solution.py:114
  162.0 10.6 %reduce-scatter.2.cloned.1.call-done = f32[48,1536]{1,0:T(8,128)} async-done(((f32[768,1536]{1,0:T(8,128)}), f32[48,1536]{1,0:T(8,128)}) %reduce-scatter.2.cloned.1.call-update) | async-done | bytes 294928 | tf_op jit(solution)/shard_map/reduce_scatter | solution.py:107
  174.8 7.1 %collective-permute-done.12 = f32[54,1536]{1,0:T(8,128)S(1)} collective-permute-done((f32[54,1536]{1,0:T(8,128)S(1)}, f32[54,1536]{1,0:T(8,128)S(1)}, u32[]{:S(2)}, u32[]{:S(2)}) %collective-permute-start.12) | collective-permute-done | bytes 331808 | tf_op jit(solution)/shard_map/ppermute | solution.py:34
  181.9 2.4 %collective-permute-start.13 = (f32[54,1536]{1,0:T(8,128)S(1)}, f32[54,1536]{1,0:T(8,128)S(1)}, u32[]{:S(2)}, u32[]{:S(2)}) collective-permute-start(f32[54,1536]{1,0:T(8,128)S(1)} %add.109), channel_id=1, source_target_pairs={{0,64},{16,80},{32,96},{48,112},{64,0},{80,16},{96,32},{112,48},{1... | collective-permute-start | bytes 995336 | tf_op jit(solution)/shard_map/ppermute | solution.py:34
  184.4 6.5 %collective-permute-done.13 = f32[54,1536]{1,0:T(8,128)S(1)} collective-permute-done((f32[54,1536]{1,0:T(8,128)S(1)}, f32[54,1536]{1,0:T(8,128)S(1)}, u32[]{:S(2)}, u32[]{:S(2)}) %collective-permute-start.13) | collective-permute-done | bytes 331808 | tf_op jit(solution)/shard_map/ppermute | solution.py:34
  191.0 6.5 %collective-permute-done.14 = f32[54,1536]{1,0:T(8,128)S(1)} collective-permute-done((f32[54,1536]{1,0:T(8,128)S(1)}, f32[54,1536]{1,0:T(8,128)S(1)}, u32[]{:S(2)}, u32[]{:S(2)}) %collective-permute-start.14) | collective-permute-done | bytes 331808 | tf_op jit(solution)/shard_map/ppermute | solution.py:34
  197.6 4.1 %collective-permute-start.15 = (f32[48,1536]{1,0:T(8,128)S(1)}, f32[48,1536]{1,0:T(8,128)S(1)}, u32[]{:S(2)}, u32[]{:S(2)}) collective-permute-start(f32[48,1536]{1,0:T(8,128)S(1)} %slice.144), channel_id=1, source_target_pairs={{0,16},{16,0},{32,48},{48,32},{64,80},{80,64},{96,112},{112,96},{1... | collective-permute-start | bytes 884744 | tf_op jit(solution)/shard_map/ppermute | solution.py:40
  (81 shorter events, 15.6 us)
Async XLA Ops:
  7.2 3.4 %copy-start = (bf16[96,1536]{1,0:T(8,128)(2,1)S(1)}, bf16[96,1536]{1,0:T(8,128)(2,1)}, u32[]{:S(2)}) copy-start(bf16[96,1536]{1,0:T(8,128)(2,1)} %param.11) | copy-start | bytes 884740
  7.2 165.4 %reduce-scatter.2.cloned.1.call-start = ((), (), s32[]{:S(2)}) async-start(), calls=%async_computation.1 | async-start | bytes 5013504 | tf_op jit(solution)/shard_map/reduce_scatter | solution.py:107
  7.2 12.9 %collective-permute-start.1 = (bf16[512,1536]{1,0:T(8,128)(2,1)}, bf16[512,1536]{1,0:T(8,128)(2,1)S(1)}, u32[]{:S(2)}, u32[]{:S(2)}) collective-permute-start(bf16[512,1536]{1,0:T(8,128)(2,1)} %param.7), channel_id=1, source_target_pairs={{0,16},{16,0},{32,48},{48,32},{64,80},{80,64},{96,112},{112,96},{1... | collective-permute-start | bytes 4718600 | tf_op jit(solution)/shard_map/ppermute | solution.py:40
  10.5 9.6 %collective-permute-start = (bf16[1,48,1536]{2,1,0:T(8,128)(2,1)S(1)}, bf16[1,48,1536]{2,1,0:T(8,128)(2,1)S(1)}, u32[]{:S(2)}, u32[]{:S(2)}) collective-permute-start(bf16[1,48,1536]{2,1,0:T(8,128)(2,1)S(1)} %dynamic-slice_bitcast_fusion), channel_id=1, source_target_pairs={{0,2},{1,3},{2,0},{3,1},{4,6},{5,7},{6,4},{7,5},{8,10},{9,11},{10,... | collective-permute-start | bytes 442376 | tf_op jit(solution)/shard_map/ppermute | solution.py:46
  20.1 3.0 %copy-start.8 = (bf16[512,1536]{1,0:T(8,128)(2,1)}, bf16[512,1536]{1,0:T(8,128)(2,1)S(1)}, u32[]{:S(2)}) copy-start(bf16[512,1536]{1,0:T(8,128)(2,1)S(1)} %collective-permute-done.1) | copy-start | bytes 4718596
  20.2 10.9 %collective-permute-start.2 = (bf16[2,48,1536]{2,1,0:T(8,128)(2,1)S(1)}, bf16[2,48,1536]{2,1,0:T(8,128)(2,1)S(1)}, u32[]{:S(2)}, u32[]{:S(2)}) collective-permute-start(bf16[2,48,1536]{2,1,0:T(8,128)(2,1)S(1)} %maximum_select_fusion.4), channel_id=1, source_target_pairs={{0,8},{1,9},{2,10},{3,11},{4,12},{5,13},{6,14},{7,15},{8,0},{9,1},... | collective-permute-start | bytes 884744 | tf_op jit(solution)/shard_map/ppermute | solution.py:46
  32.0 4.9 %copy-start.5 = (f32[1536]{0:T(1024)S(1)}, f32[1536]{0:T(1024)}, u32[]{:S(2)}) copy-start(f32[1536]{0:T(1024)} %param.10) | copy-start | bytes 18436
  32.7 29.8 %collective-permute-start.3 = (bf16[4,48,1536]{2,1,0:T(8,128)(2,1)}, bf16[4,48,1536]{2,1,0:T(8,128)(2,1)}, u32[]{:S(2)}, u32[]{:S(2)}) collective-permute-start(bf16[4,48,1536]{2,1,0:T(8,128)(2,1)} %maximum_select_fusion.2), channel_id=1, source_target_pairs={{0,1},{1,0},{2,3},{3,2},{4,5},{5,4},{6,7},{7,6},{8,9},{9,8},{10,11... | collective-permute-start | bytes 1769480 | tf_op jit(solution)/shard_map/ppermute | solution.py:46
  41.9 27.0 %copy-start.6 = (bf16[512,1536]{1,0:T(8,128)(2,1)S(1)}, bf16[512,1536]{1,0:T(8,128)(2,1)}, u32[]{:S(2)}) copy-start(bf16[512,1536]{1,0:T(8,128)(2,1)} %param.7) | copy-start | bytes 4718596
  41.9 27.0 %copy-start.9 = (bf16[512,1536]{1,0:T(8,128)(2,1)S(1)}, bf16[512,1536]{1,0:T(8,128)(2,1)}, u32[]{:S(2)}) copy-start(bf16[512,1536]{1,0:T(8,128)(2,1)} %copy-done.8) | copy-start | bytes 4718596
  65.3 3.6 %collective-permute-start.4 = (bf16[512,768]{0,1:T(8,128)(2,1)S(1)}, bf16[512,768]{0,1:T(8,128)(2,1)S(1)}, u32[]{:S(2)}, u32[]{:S(2)}) collective-permute-start(bf16[512,768]{0,1:T(8,128)(2,1)S(1)} %bitcast.43), channel_id=1, source_target_pairs={{0,16},{16,0},{32,48},{48,32},{64,80},{80,64},{96,112},{112,96},{1... | collective-permute-start | bytes 2359304 | tf_op jit(solution)/shard_map/ppermute | solution.py:40
  67.0 32.1 %collective-permute-start.5 = (bf16[8,48,1536]{2,1,0:T(8,128)(2,1)}, bf16[8,48,1536]{2,1,0:T(8,128)(2,1)}, u32[]{:S(2)}, u32[]{:S(2)}) collective-permute-start(bf16[8,48,1536]{2,1,0:T(8,128)(2,1)} %maximum_select_fusion.1), channel_id=1, source_target_pairs={{0,4},{1,5},{2,6},{3,7},{4,0},{5,1},{6,2},{7,3},{8,12},{9,13},{10,... | collective-permute-start | bytes 3538952 | tf_op jit(solution)/shard_map/ppermute | solution.py:46
  103.3 5.8 %collective-permute-start.6 = (bf16[768,1536]{1,0:T(8,128)(2,1)}, bf16[768,1536]{1,0:T(8,128)(2,1)}, u32[]{:S(2)}, u32[]{:S(2)}) collective-permute-start(bf16[768,1536]{1,0:T(8,128)(2,1)} %bitcast.14), channel_id=1, source_target_pairs={{0,16},{16,0},{32,48},{48,32},{64,80},{80,64},{96,112},{112,96},{1... | collective-permute-start | bytes 7077896 | tf_op jit(solution)/shard_map/ppermute | solution.py:40
  111.8 1.6 copy-start.7
  112.3 5.0 %copy-start.3 = (bf16[16,2,48,1536]{3,2,1,0:T(8,128)(2,1)}, bf16[16,2,48,1536]{3,2,1,0:T(8,128)(2,1)S(1)}, u32[]{:S(2)}) copy-start(bf16[16,2,48,1536]{3,2,1,0:T(8,128)(2,1)S(1)} %pad_maximum_fusion) | copy-start | bytes 14155780
  113.5 3.9 %copy-start.1 = (bf16[512,1536]{1,0:T(8,128)(2,1)S(1)}, bf16[512,1536]{1,0:T(8,128)(2,1)}, u32[]{:S(2)}) copy-start(bf16[512,1536]{1,0:T(8,128)(2,1)} %param.6) | copy-start | bytes 4718596
  122.9 8.0 %collective-permute-start.7 = (f32[6,1536]{1,0:T(8,128)S(1)}, f32[6,1536]{1,0:T(8,128)S(1)}, u32[]{:S(2)}, u32[]{:S(2)}) collective-permute-start(f32[6,1536]{1,0:T(8,128)S(1)} %broadcast_multiply_fusion), channel_id=1, source_target_pairs={{0,1},{1,0},{2,3},{3,2},{4,5},{5,4},{6,7},{7,6},{8,9},{9,8},{10,11... | collective-permute-start | bytes 110600 | tf_op jit(solution)/shard_map/ppermute | solution.py:34
  130.9 11.0 %collective-permute-start.8 = (f32[6,1536]{1,0:T(8,128)S(1)}, f32[6,1536]{1,0:T(8,128)S(1)}, u32[]{:S(2)}, u32[]{:S(2)}) collective-permute-start(f32[6,1536]{1,0:T(8,128)S(1)} %fusion.36), channel_id=1, source_target_pairs={{0,2},{1,3},{2,0},{3,1},{4,6},{5,7},{6,4},{7,5},{8,10},{9,11},{10,... | collective-permute-start | bytes 110600 | tf_op jit(solution)/shard_map/ppermute | solution.py:34
  141.9 3.3 %collective-permute-start.9 = (f32[6,1536]{1,0:T(8,128)S(1)}, f32[6,1536]{1,0:T(8,128)S(1)}, u32[]{:S(2)}, u32[]{:S(2)}) collective-permute-start(f32[6,1536]{1,0:T(8,128)S(1)} %add.101), channel_id=1, source_target_pairs={{0,4},{1,5},{2,6},{3,7},{4,0},{5,1},{6,2},{7,3},{8,12},{9,13},{10,... | collective-permute-start | bytes 110600 | tf_op jit(solution)/shard_map/ppermute | solution.py:34
  145.2 10.4 %collective-permute-start.10 = (f32[6,1536]{1,0:T(8,128)S(1)}, f32[6,1536]{1,0:T(8,128)S(1)}, u32[]{:S(2)}, u32[]{:S(2)}) collective-permute-start(f32[6,1536]{1,0:T(8,128)S(1)} %add.102), channel_id=1, source_target_pairs={{0,8},{1,9},{2,10},{3,11},{4,12},{5,13},{6,14},{7,15},{8,0},{9,1},... | collective-permute-start | bytes 110600 | tf_op jit(solution)/shard_map/ppermute | solution.py:34
  145.3 12.4 %copy-start.2 = (bf16[512,1536]{1,0:T(8,128)(2,1)S(1)}, bf16[512,1536]{1,0:T(8,128)(2,1)}, u32[]{:S(2)}) copy-start(bf16[512,1536]{1,0:T(8,128)(2,1)} %multiply_convert_fusion) | copy-start | bytes 4718596
  145.3 12.4 %copy-start.4 = (bf16[16,2,48,1536]{3,2,1,0:T(8,128)(2,1)S(1)}, bf16[16,2,48,1536]{3,2,1,0:T(8,128)(2,1)}, u32[]{:S(2)}) copy-start(bf16[16,2,48,1536]{3,2,1,0:T(8,128)(2,1)} %copy-done.3) | copy-start | bytes 14155780
  155.7 6.3 %collective-permute-start.11 = (f32[6,1536]{1,0:T(8,128)S(1)}, f32[6,1536]{1,0:T(8,128)S(1)}, u32[]{:S(2)}, u32[]{:S(2)}) collective-permute-start(f32[6,1536]{1,0:T(8,128)S(1)} %add.103), channel_id=1, source_target_pairs={{0,16},{16,0},{32,48},{48,32},{64,80},{80,64},{96,112},{112,96},{1... | collective-permute-start | bytes 110600 | tf_op jit(solution)/shard_map/ppermute | solution.py:34
  173.6 8.3 %collective-permute-start.12 = (f32[54,1536]{1,0:T(8,128)S(1)}, f32[54,1536]{1,0:T(8,128)S(1)}, u32[]{:S(2)}, u32[]{:S(2)}) collective-permute-start(f32[54,1536]{1,0:T(8,128)S(1)} %constant_dynamic-update-slice_fusion), channel_id=1, source_target_pairs={{0,32},{16,48},{32,0},{48,16},{64,96},{80,112},{96,64},{112,80},{1... | collective-permute-start | bytes 995336 | tf_op jit(solution)/shard_map/ppermute | solution.py:34
  181.9 8.9 %collective-permute-start.13 = (f32[54,1536]{1,0:T(8,128)S(1)}, f32[54,1536]{1,0:T(8,128)S(1)}, u32[]{:S(2)}, u32[]{:S(2)}) collective-permute-start(f32[54,1536]{1,0:T(8,128)S(1)} %add.109), channel_id=1, source_target_pairs={{0,64},{16,80},{32,96},{48,112},{64,0},{80,16},{96,32},{112,48},{1... | collective-permute-start | bytes 995336 | tf_op jit(solution)/shard_map/ppermute | solution.py:34
  190.9 6.6 %collective-permute-start.14 = (f32[54,1536]{1,0:T(8,128)S(1)}, f32[54,1536]{1,0:T(8,128)S(1)}, u32[]{:S(2)}, u32[]{:S(2)}) collective-permute-start(f32[54,1536]{1,0:T(8,128)S(1)} %add.110), channel_id=1, source_target_pairs={{0,128},{16,144},{32,160},{48,176},{64,192},{80,208},{96,224},{112... | collective-permute-start | bytes 995336 | tf_op jit(solution)/shard_map/ppermute | solution.py:34
  197.6 5.3 %collective-permute-start.15 = (f32[48,1536]{1,0:T(8,128)S(1)}, f32[48,1536]{1,0:T(8,128)S(1)}, u32[]{:S(2)}, u32[]{:S(2)}) collective-permute-start(f32[48,1536]{1,0:T(8,128)S(1)} %slice.144), channel_id=1, source_target_pairs={{0,16},{16,0},{32,48},{48,32},{64,80},{80,64},{96,112},{112,96},{1... | collective-permute-start | bytes 884744 | tf_op jit(solution)/shard_map/ppermute | solution.py:40
Sparse Core Ops, SparseCore 0:
  73.3 99.2 reduce-scatter.1

commit v11 on v8

--- a/solution.py
+++ b/solution.py
@@ -71,7 +71,7 @@
     rows = out_weight.shape[0]
     half_rows = rows // 2
     core = lax.axis_index("dp") % 2
-    masks = (2, 8, 1, 4)
+    masks = (2, 1, 8, 4)
     own_half = lax.dynamic_slice_in_dim(out_weight, core * half_rows, half_rows, 0)
     held = doubling_step(own_half[None], "fsdp", masks[0])
     taps = tap_mask(lengths[0], frames, count)

time: 210 us -> 203 us (0.967)
  waiting for transfers between devices: 94.2 us -> 82.6 us
  starting transfers between devices: 38.4 us -> 42.8 us
    ppermute x4, waiting for transfers between devices: 53.7 us -> 43.5 us  [doubling_step(): received = lax.ppermute(held, axis, [(i, i ^ mask) for i in range(size)])]
    ppermute x8, starting transfers between devices: 14.4 us -> 17 us  [butterfly(): x = x + lax.ppermute(x, axis, pairs)]
  transfers between devices with their start and end apart: 17 -> 17, of which waited for: 12 -> 13; matrix products, arithmetic and copies ran while one was open for 24% -> 25% of each run, Pallas kernels for 0% -> 0%
where the time goes in v11:
time: 203 us; the launch traced here: 202 us
  waiting for transfers between devices  82.6 us (41%)
  starting transfers between devices  42.8 us (21%)
  other arithmetic  40.8 us (20%)
  between operations  14.3 us (7%)
  matrix products  12.3 us (6%)
  local copies, waits for them, and re-layouts  9.68 us (5%)
    ppermute x4, waiting for transfers between devices, doubling_step(): received = lax.ppermute(held, axis, [(i, i ^ mask) for i in range(size)])  43.5 us
    ppermute x8, waiting for transfers between devices, butterfly(): x = x + lax.ppermute(x, axis, pairs)  29.1 us
    ppermute x8, starting transfers between devices, butterfly(): x = x + lax.ppermute(x, axis, pairs)  17 us
    ppermute x4, starting transfers between devices, doubling_step(): received = lax.ppermute(held, axis, [(i, i ^ mask) for i in range(size)])  14.1 us
    ppermute x4, starting transfers between devices, sibling(): return lax.ppermute(x, 'dp', [(i, i ^ 1) for i in range(size)])  11.6 us
    add x1, other arithmetic, shards(): grad_hidden + conv_kernel[k] * (back_views[count - 1 - k] * taps[count -...  10.3 us
    add x1, other arithmetic, shards(): mixed + conv_kernel[k] * views[k].astype(jnp.float32) * taps[k][:, None]  7.9 us
    ppermute x4, waiting for transfers between devices, sibling(): return lax.ppermute(x, 'dp', [(i, i ^ 1) for i in range(size)])  7 us
  transfers between devices with their start and end apart: 17, of which 13 were waited for; matrix products, arithmetic and copies ran while one was open for 25% of the time, Pallas kernels for 0%

profile of v11, /device:TPU:1, one launch (start us, length us, event | category | flops | bytes accessed | tf_op | source)
XLA Modules:
  0.0 202.5 jit_solution(16745666495230732707)
XLA Ops:
  7.2 3.3 %collective-permute-start.1 = (bf16[512,1536]{1,0:T(8,128)(2,1)}, bf16[512,1536]{1,0:T(8,128)(2,1)S(1)}, u32[]{:S(2)}, u32[]{:S(2)}) collective-permute-start(bf16[512,1536]{1,0:T(8,128)(2,1)} %param.7), channel_id=1, source_target_pairs={{0,16},{16,0},{32,48},{48,32},{64,80},{80,64},{96,112},{112,96},{1... | collective-permute-start | bytes 4718600 | tf_op jit(solution)/shard_map/ppermute | solution.py:40
  10.5 5.4 %collective-permute-start = (bf16[1,48,1536]{2,1,0:T(8,128)(2,1)S(1)}, bf16[1,48,1536]{2,1,0:T(8,128)(2,1)S(1)}, u32[]{:S(2)}, u32[]{:S(2)}) collective-permute-start(bf16[1,48,1536]{2,1,0:T(8,128)(2,1)S(1)} %dynamic-slice_bitcast_fusion), channel_id=1, source_target_pairs={{0,2},{1,3},{2,0},{3,1},{4,6},{5,7},{6,4},{7,5},{8,10},{9,11},{10,... | collective-permute-start | bytes 442376 | tf_op jit(solution)/shard_map/ppermute | solution.py:46
  20.2 4.2 %collective-permute-start.2 = (bf16[2,48,1536]{2,1,0:T(8,128)(2,1)S(1)}, bf16[2,48,1536]{2,1,0:T(8,128)(2,1)S(1)}, u32[]{:S(2)}, u32[]{:S(2)}) collective-permute-start(bf16[2,48,1536]{2,1,0:T(8,128)(2,1)S(1)} %maximum_select_fusion.4), channel_id=1, source_target_pairs={{0,1},{1,0},{2,3},{3,2},{4,5},{5,4},{6,7},{7,6},{8,9},{9,8},{10,11... | collective-permute-start | bytes 884744 | tf_op jit(solution)/shard_map/ppermute | solution.py:46
  24.4 7.9 %fusion.7 = f32[512,1536]{1,0:T(8,128)S(1)} fusion(bf16[512,1536]{1,0:T(8,128)(2,1)} %param.6, f32[512]{0:T(512)S(1)} %bitcast.52, f32[1536]{0:T(1024)S(1)} %get-tuple-element.44, f32[512]{0:T(512)S(1)} %bitcast.55, f32[1536]{0:T(1024)S(1)} %get-tuple-element.45, f32[512]{0:T(512)S(1)} %bitcast.44, f32[1536]{0:T(1024)S(1)} %get-tuple-element.42, ...), kind=kLoop, calls=%fused_computation.19 | loop fusion | flops 14942208 | bytes 4759552 | tf_op jit(solution)/shard_map/add | solution.py:85
  32.3 4.6 %collective-permute-done.2 = bf16[2,48,1536]{2,1,0:T(8,128)(2,1)S(1)} collective-permute-done((bf16[2,48,1536]{2,1,0:T(8,128)(2,1)S(1)}, bf16[2,48,1536]{2,1,0:T(8,128)(2,1)S(1)}, u32[]{:S(2)}, u32[]{:S(2)}) %collective-permute-start.2) | collective-permute-done | bytes 294944 | tf_op jit(solution)/shard_map/ppermute | solution.py:46
  38.5 3.0 %collective-permute-start.3 = (bf16[4,48,1536]{2,1,0:T(8,128)(2,1)}, bf16[4,48,1536]{2,1,0:T(8,128)(2,1)}, u32[]{:S(2)}, u32[]{:S(2)}) collective-permute-start(bf16[4,48,1536]{2,1,0:T(8,128)(2,1)} %maximum_select_fusion.2), channel_id=1, source_target_pairs={{0,8},{1,9},{2,10},{3,11},{4,12},{5,13},{6,14},{7,15},{8,0},{9,1},... | collective-permute-start | bytes 1769480 | tf_op jit(solution)/shard_map/ppermute | solution.py:46
  41.6 2.4 %multiply_convert_fusion = bf16[512,1536]{1,0:T(8,128)(2,1)} fusion(f32[512,1536]{1,0:T(8,128)S(1)} %fusion.7, f32[1536]{0:T(1024)S(1)} %copy-done.5, f32[512]{0:T(512)S(1)} %add_rsqrt_fusion, f32[512]{0:T(512)S(1)} %broadcast_multiply_fusion.2, f32[512]{0:T(512)S(1)} %bitcast.45), kind=kLoop, calls=%fused_computation.37 | loop fusion | flops 7077888 | bytes 4730880 | tf_op jit(solution)/shard_map/convert_element_type | solution.py:93
  44.0 2.6 %copy.18 = bf16[512,1536]{0,1:T(8,128)(2,1)} copy(bf16[512,1536]{1,0:T(8,128)(2,1)} %multiply_convert_fusion) | data formatting | bytes 3145728 | tf_op jit(solution)/shard_map/convert_element_type | solution.py:93
  48.2 5.4 %collective-permute-done.3 = bf16[4,48,1536]{2,1,0:T(8,128)(2,1)} collective-permute-done((bf16[4,48,1536]{2,1,0:T(8,128)(2,1)}, bf16[4,48,1536]{2,1,0:T(8,128)(2,1)}, u32[]{:S(2)}, u32[]{:S(2)}) %collective-permute-start.3) | collective-permute-done | bytes 589856 | tf_op jit(solution)/shard_map/ppermute | solution.py:46
  53.6 2.8 %maximum_select_fusion.1 = bf16[8,48,1536]{2,1,0:T(8,128)(2,1)} fusion(bf16[4,48,1536]{2,1,0:T(8,128)(2,1)} %maximum_select_fusion.2, bf16[4,48,1536]{2,1,0:T(8,128)(2,1)} %collective-permute-done.3, pred[]{:T(512)S(6)} %ne.18), kind=kLoop, calls=%fused_computation.51 | loop fusion | flops 1769472 | bytes 2359297 | tf_op jit(solution)/shard_map/jit(_where)/select_n | solution.py:47
  56.4 2.6 %collective-permute-start.4 = (bf16[512,768]{0,1:T(8,128)(2,1)S(1)}, bf16[512,768]{0,1:T(8,128)(2,1)S(1)}, u32[]{:S(2)}, u32[]{:S(2)}) collective-permute-start(bf16[512,768]{0,1:T(8,128)(2,1)S(1)} %bitcast.43), channel_id=1, source_target_pairs={{0,16},{16,0},{32,48},{48,32},{64,80},{80,64},{96,112},{112,96},{1... | collective-permute-start | bytes 2359304 | tf_op jit(solution)/shard_map/ppermute | solution.py:40
  59.0 1.9 collective-permute-done.4
  60.9 4.2 %fusion.17 = f32[768,1536]{1,0:T(8,128)} fusion(bf16[512,1536]{1,0:T(8,128)(2,1)S(1)} %copy-done.9, bf16[512,1536]{1,0:T(8,128)(2,1)S(1)} %copy-done.6, bf16[512,768]{0,1:T(8,128)(2,1)S(1)} %collective-permute-done.4, bf16[512,768]{0,1:T(8,128)(2,1)S(1)} %bitcast.42), kind=kOutput, calls=%fused_computation.29 | convolution fusion | flops 2425356288 | bytes 9437184 | tf_op jit(solution)/shard_map/dot_general | solution.py:103
  66.6 33.4 %collective-permute-done.5 = bf16[8,48,1536]{2,1,0:T(8,128)(2,1)} collective-permute-done((bf16[8,48,1536]{2,1,0:T(8,128)(2,1)}, bf16[8,48,1536]{2,1,0:T(8,128)(2,1)}, u32[]{:S(2)}, u32[]{:S(2)}) %collective-permute-start.5) | collective-permute-done | bytes 1179680 | tf_op jit(solution)/shard_map/ppermute | solution.py:46
  100.0 2.6 %maximum_select_fusion = bf16[16,48,1536]{2,1,0:T(8,128)(2,1)S(1)} fusion(bf16[8,48,1536]{2,1,0:T(8,128)(2,1)} %maximum_select_fusion.1, bf16[8,48,1536]{2,1,0:T(8,128)(2,1)} %collective-permute-done.5, pred[]{:T(512)S(6)} %ne.22), kind=kLoop, calls=%fused_computation.42 | loop fusion | flops 3538944 | bytes 4718593 | tf_op jit(solution)/shard_map/jit(_where)/select_n | solution.py:47
  105.4 4.5 %collective-permute-done.6 = bf16[768,1536]{1,0:T(8,128)(2,1)} collective-permute-done((bf16[768,1536]{1,0:T(8,128)(2,1)}, bf16[768,1536]{1,0:T(8,128)(2,1)}, u32[]{:S(2)}, u32[]{:S(2)}) %collective-permute-start.6) | collective-permute-done | bytes 2359328 | tf_op jit(solution)/shard_map/ppermute | solution.py:40
  109.9 2.7 %broadcast_select_fusion.1 = (bf16[768,1536]{1,0:T(8,128)(2,1)S(1)}, bf16[768,1536]{1,0:T(8,128)(2,1)S(1)}) fusion(bf16[768,1536]{1,0:T(8,128)(2,1)} %collective-permute-done.6, pred[]{:T(512)S(6)} %eq.24, bf16[2,2,2,2,48,1536]{5,4,3,2,1,0:T(8,128)(2,1)} %copy.19), kind=kLoop, calls=%fused_computation.44 | loop fusion | flops 2359296 | bytes 9437185 | tf_op jit(solution)/shard_map/jit(_where)/select_n | solution.py:110
  114.1 3.8 %multiply_reduce_fusion = (f32[1536]{0:T(1024)S(1)}, f32[512]{0:T(512)S(1)}, f32[512]{0:T(512)S(1)}, f32[512,1536]{1,0:T(8,128)S(1)}) fusion(f32[512,1536]{1,0:T(8,128)S(1)} %fusion.7, f32[512]{0:T(512)S(1)} %add_rsqrt_fusion, f32[512]{0:T(512)S(1)} %broadcast_multiply_fusion.2, f32[1536]{0:T(1024)S(1)} %copy-done.5, f32[512]{0:T(512)S(1)} %bitcast.46, ...), kind=kOutput, calls=%fused_computation.34 | convolution fusion | flops 2430072320 | bytes 12605440 | tf_op jit(solution)/shard_map/dot_general | solution.py:114
  118.0 5.4 %fusion.16 = (f32[1536]{0:T(1024)S(1)}, f32[1536]{0:T(1024)S(1)}, f32[1536]{0:T(1024)S(1)}, f32[1536]{0:T(1024)S(1)}, f32[1536]{0:T(1024)S(1)}, /*index=5*/f32[512,1536]{1,0:T(8,128)}) fusion(f32[512]{0:T(512)S(1)} %bitcast.53, bf16[512,1536]{1,0:T(8,128)(2,1)S(1)} %copy-done.1, f32[512]{0:T(512)S(1)} %bitcast.56, f32[512]{0:T(512)S(1)} %bitcast.47, ...), kind=kLoop, calls=%fused_computation.28 | loop fusion | flops 21225984 | bytes 11065344 | tf_op jit(solution)/shard_map/reduce_sum | solution.py:128
  123.6 6.9 %collective-permute-done.7 = f32[6,1536]{1,0:T(8,128)S(1)} collective-permute-done((f32[6,1536]{1,0:T(8,128)S(1)}, f32[6,1536]{1,0:T(8,128)S(1)}, u32[]{:S(2)}, u32[]{:S(2)}) %collective-permute-start.7) | collective-permute-done | bytes 36896 | tf_op jit(solution)/shard_map/ppermute | solution.py:34
  130.5 4.9 %collective-permute-start.8 = (f32[6,1536]{1,0:T(8,128)S(1)}, f32[6,1536]{1,0:T(8,128)S(1)}, u32[]{:S(2)}, u32[]{:S(2)}) collective-permute-start(f32[6,1536]{1,0:T(8,128)S(1)} %add.100), channel_id=1, source_target_pairs={{0,2},{1,3},{2,0},{3,1},{4,6},{5,7},{6,4},{7,5},{8,10},{9,11},{10,... | collective-permute-start | bytes 110600 | tf_op jit(solution)/shard_map/ppermute | solution.py:34
  135.4 2.3 %collective-permute-done.8 = f32[6,1536]{1,0:T(8,128)S(1)} collective-permute-done((f32[6,1536]{1,0:T(8,128)S(1)}, f32[6,1536]{1,0:T(8,128)S(1)}, u32[]{:S(2)}, u32[]{:S(2)}) %collective-permute-start.8) | collective-permute-done | bytes 36896 | tf_op jit(solution)/shard_map/ppermute | solution.py:34
  140.7 3.5 %collective-permute-start.10 = (f32[6,1536]{1,0:T(8,128)S(1)}, f32[6,1536]{1,0:T(8,128)S(1)}, u32[]{:S(2)}, u32[]{:S(2)}) collective-permute-start(f32[6,1536]{1,0:T(8,128)S(1)} %add.102), channel_id=1, source_target_pairs={{0,8},{1,9},{2,10},{3,11},{4,12},{5,13},{6,14},{7,15},{8,0},{9,1},... | collective-permute-start | bytes 110600 | tf_op jit(solution)/shard_map/ppermute | solution.py:34
  144.2 10.3 %multiply_add_fusion = f32[512,1536]{1,0:T(8,128)} fusion(f32[512,1536]{1,0:T(8,128)} %get-tuple-element.46, f32[512]{0:T(512)S(1)} %bitcast.54, f32[1536]{0:T(1024)S(1)} %get-tuple-element.44, f32[512]{0:T(512)S(1)} %bitcast.57, f32[1536]{0:T(1024)S(1)} %get-tuple-element.45, f32[512]{0:T(512)S(1)} %bitcast.48, f32[1536]{0:T(1024)S(1)} %get-tuple-element.42, ...), kind=kLoop, calls=%fused_computation.33 | loop fusion | flops 11010048 | bytes 6332416 | tf_op jit(solution)/shard_map/add | solution.py:132
  154.5 2.2 %collective-permute-start.11 = (f32[6,1536]{1,0:T(8,128)S(1)}, f32[6,1536]{1,0:T(8,128)S(1)}, u32[]{:S(2)}, u32[]{:S(2)}) collective-permute-start(f32[6,1536]{1,0:T(8,128)S(1)} %add.103), channel_id=1, source_target_pairs={{0,16},{16,0},{32,48},{48,32},{64,80},{80,64},{96,112},{112,96},{1... | collective-permute-start | bytes 110600 | tf_op jit(solution)/shard_map/ppermute | solution.py:34
  156.8 4.3 %fusion.40 = f32[512,1536]{1,0:T(8,128)} fusion(bf16[512,1536]{1,0:T(8,128)(2,1)S(1)} %copy-done.2, bf16[1536,1536]{1,0:T(8,128)(2,1)S(1)} %bitcast.41), kind=kOutput, calls=%fused_computation.99 | convolution fusion | flops 2415919104 | bytes 9437184 | tf_op jit(solution)/shard_map/dot_general | solution.py:113
  161.1 3.0 %reduce-scatter.2.cloned.1.call-done = f32[48,1536]{1,0:T(8,128)} async-done(((f32[768,1536]{1,0:T(8,128)}), f32[48,1536]{1,0:T(8,128)}) %reduce-scatter.2.cloned.1.call-update) | async-done | bytes 294928 | tf_op jit(solution)/shard_map/reduce_scatter | solution.py:106
  166.7 6.5 %collective-permute-done.12 = f32[54,1536]{1,0:T(8,128)S(1)} collective-permute-done((f32[54,1536]{1,0:T(8,128)S(1)}, f32[54,1536]{1,0:T(8,128)S(1)}, u32[]{:S(2)}, u32[]{:S(2)}) %collective-permute-start.12) | collective-permute-done | bytes 331808 | tf_op jit(solution)/shard_map/ppermute | solution.py:34
  173.2 3.1 %collective-permute-start.13 = (f32[54,1536]{1,0:T(8,128)S(1)}, f32[54,1536]{1,0:T(8,128)S(1)}, u32[]{:S(2)}, u32[]{:S(2)}) collective-permute-start(f32[54,1536]{1,0:T(8,128)S(1)} %add.109), channel_id=1, source_target_pairs={{0,64},{16,80},{32,96},{48,112},{64,0},{80,16},{96,32},{112,48},{1... | collective-permute-start | bytes 995336 | tf_op jit(solution)/shard_map/ppermute | solution.py:34
  176.4 5.7 %collective-permute-done.13 = f32[54,1536]{1,0:T(8,128)S(1)} collective-permute-done((f32[54,1536]{1,0:T(8,128)S(1)}, f32[54,1536]{1,0:T(8,128)S(1)}, u32[]{:S(2)}, u32[]{:S(2)}) %collective-permute-start.13) | collective-permute-done | bytes 331808 | tf_op jit(solution)/shard_map/ppermute | solution.py:34
  182.2 6.1 %collective-permute-done.14 = f32[54,1536]{1,0:T(8,128)S(1)} collective-permute-done((f32[54,1536]{1,0:T(8,128)S(1)}, f32[54,1536]{1,0:T(8,128)S(1)}, u32[]{:S(2)}, u32[]{:S(2)}) %collective-permute-start.14) | collective-permute-done | bytes 331808 | tf_op jit(solution)/shard_map/ppermute | solution.py:34
  189.0 4.5 %collective-permute-start.15 = (f32[48,1536]{1,0:T(8,128)S(1)}, f32[48,1536]{1,0:T(8,128)S(1)}, u32[]{:S(2)}, u32[]{:S(2)}) collective-permute-start(f32[48,1536]{1,0:T(8,128)S(1)} %slice.144), channel_id=1, source_target_pairs={{0,16},{16,0},{32,48},{48,32},{64,80},{80,64},{96,112},{112,96},{1... | collective-permute-start | bytes 884744 | tf_op jit(solution)/shard_map/ppermute | solution.py:40
  (80 shorter events, 21.9 us)
Async XLA Ops:
  7.2 3.4 %copy-start = (bf16[96,1536]{1,0:T(8,128)(2,1)S(1)}, bf16[96,1536]{1,0:T(8,128)(2,1)}, u32[]{:S(2)}) copy-start(bf16[96,1536]{1,0:T(8,128)(2,1)} %param.11) | copy-start | bytes 884740
  7.2 156.9 %reduce-scatter.2.cloned.1.call-start = ((), (), s32[]{:S(2)}) async-start(), calls=%async_computation.1 | async-start | bytes 5013504 | tf_op jit(solution)/shard_map/reduce_scatter | solution.py:106
  7.2 12.9 %collective-permute-start.1 = (bf16[512,1536]{1,0:T(8,128)(2,1)}, bf16[512,1536]{1,0:T(8,128)(2,1)S(1)}, u32[]{:S(2)}, u32[]{:S(2)}) collective-permute-start(bf16[512,1536]{1,0:T(8,128)(2,1)} %param.7), channel_id=1, source_target_pairs={{0,16},{16,0},{32,48},{48,32},{64,80},{80,64},{96,112},{112,96},{1... | collective-permute-start | bytes 4718600 | tf_op jit(solution)/shard_map/ppermute | solution.py:40
  10.5 9.6 %collective-permute-start = (bf16[1,48,1536]{2,1,0:T(8,128)(2,1)S(1)}, bf16[1,48,1536]{2,1,0:T(8,128)(2,1)S(1)}, u32[]{:S(2)}, u32[]{:S(2)}) collective-permute-start(bf16[1,48,1536]{2,1,0:T(8,128)(2,1)S(1)} %dynamic-slice_bitcast_fusion), channel_id=1, source_target_pairs={{0,2},{1,3},{2,0},{3,1},{4,6},{5,7},{6,4},{7,5},{8,10},{9,11},{10,... | collective-permute-start | bytes 442376 | tf_op jit(solution)/shard_map/ppermute | solution.py:46
  20.1 4.2 %copy-start.8 = (bf16[512,1536]{1,0:T(8,128)(2,1)}, bf16[512,1536]{1,0:T(8,128)(2,1)S(1)}, u32[]{:S(2)}) copy-start(bf16[512,1536]{1,0:T(8,128)(2,1)S(1)} %collective-permute-done.1) | copy-start | bytes 4718596
  20.2 16.8 %collective-permute-start.2 = (bf16[2,48,1536]{2,1,0:T(8,128)(2,1)S(1)}, bf16[2,48,1536]{2,1,0:T(8,128)(2,1)S(1)}, u32[]{:S(2)}, u32[]{:S(2)}) collective-permute-start(bf16[2,48,1536]{2,1,0:T(8,128)(2,1)S(1)} %maximum_select_fusion.4), channel_id=1, source_target_pairs={{0,1},{1,0},{2,3},{3,2},{4,5},{5,4},{6,7},{7,6},{8,9},{9,8},{10,11... | collective-permute-start | bytes 884744 | tf_op jit(solution)/shard_map/ppermute | solution.py:46
  37.9 3.7 %copy-start.5 = (f32[1536]{0:T(1024)S(1)}, f32[1536]{0:T(1024)}, u32[]{:S(2)}) copy-start(f32[1536]{0:T(1024)} %param.10) | copy-start | bytes 18436
  38.5 15.1 %collective-permute-start.3 = (bf16[4,48,1536]{2,1,0:T(8,128)(2,1)}, bf16[4,48,1536]{2,1,0:T(8,128)(2,1)}, u32[]{:S(2)}, u32[]{:S(2)}) collective-permute-start(bf16[4,48,1536]{2,1,0:T(8,128)(2,1)} %maximum_select_fusion.2), channel_id=1, source_target_pairs={{0,8},{1,9},{2,10},{3,11},{4,12},{5,13},{6,14},{7,15},{8,0},{9,1},... | collective-permute-start | bytes 1769480 | tf_op jit(solution)/shard_map/ppermute | solution.py:46
  46.6 14.3 %copy-start.6 = (bf16[512,1536]{1,0:T(8,128)(2,1)S(1)}, bf16[512,1536]{1,0:T(8,128)(2,1)}, u32[]{:S(2)}) copy-start(bf16[512,1536]{1,0:T(8,128)(2,1)} %param.7) | copy-start | bytes 4718596
  46.6 14.3 %copy-start.9 = (bf16[512,1536]{1,0:T(8,128)(2,1)S(1)}, bf16[512,1536]{1,0:T(8,128)(2,1)}, u32[]{:S(2)}) copy-start(bf16[512,1536]{1,0:T(8,128)(2,1)} %copy-done.8) | copy-start | bytes 4718596
  56.4 4.5 %collective-permute-start.4 = (bf16[512,768]{0,1:T(8,128)(2,1)S(1)}, bf16[512,768]{0,1:T(8,128)(2,1)S(1)}, u32[]{:S(2)}, u32[]{:S(2)}) collective-permute-start(bf16[512,768]{0,1:T(8,128)(2,1)S(1)} %bitcast.43), channel_id=1, source_target_pairs={{0,16},{16,0},{32,48},{48,32},{64,80},{80,64},{96,112},{112,96},{1... | collective-permute-start | bytes 2359304 | tf_op jit(solution)/shard_map/ppermute | solution.py:40
  65.2 34.8 %collective-permute-start.5 = (bf16[8,48,1536]{2,1,0:T(8,128)(2,1)}, bf16[8,48,1536]{2,1,0:T(8,128)(2,1)}, u32[]{:S(2)}, u32[]{:S(2)}) collective-permute-start(bf16[8,48,1536]{2,1,0:T(8,128)(2,1)} %maximum_select_fusion.1), channel_id=1, source_target_pairs={{0,4},{1,5},{2,6},{3,7},{4,0},{5,1},{6,2},{7,3},{8,12},{9,13},{10,... | collective-permute-start | bytes 3538952 | tf_op jit(solution)/shard_map/ppermute | solution.py:46
  104.2 5.8 %collective-permute-start.6 = (bf16[768,1536]{1,0:T(8,128)(2,1)}, bf16[768,1536]{1,0:T(8,128)(2,1)}, u32[]{:S(2)}, u32[]{:S(2)}) collective-permute-start(bf16[768,1536]{1,0:T(8,128)(2,1)} %bitcast.14), channel_id=1, source_target_pairs={{0,16},{16,0},{32,48},{48,32},{64,80},{80,64},{96,112},{112,96},{1... | collective-permute-start | bytes 7077896 | tf_op jit(solution)/shard_map/ppermute | solution.py:40
  112.7 1.4 copy-start.7
  113.1 4.8 %copy-start.3 = (bf16[16,2,48,1536]{3,2,1,0:T(8,128)(2,1)}, bf16[16,2,48,1536]{3,2,1,0:T(8,128)(2,1)S(1)}, u32[]{:S(2)}) copy-start(bf16[16,2,48,1536]{3,2,1,0:T(8,128)(2,1)S(1)} %pad_maximum_fusion) | copy-start | bytes 14155780
  114.1 3.9 %copy-start.1 = (bf16[512,1536]{1,0:T(8,128)(2,1)S(1)}, bf16[512,1536]{1,0:T(8,128)(2,1)}, u32[]{:S(2)}) copy-start(bf16[512,1536]{1,0:T(8,128)(2,1)} %param.6) | copy-start | bytes 4718596
  123.5 7.0 %collective-permute-start.7 = (f32[6,1536]{1,0:T(8,128)S(1)}, f32[6,1536]{1,0:T(8,128)S(1)}, u32[]{:S(2)}, u32[]{:S(2)}) collective-permute-start(f32[6,1536]{1,0:T(8,128)S(1)} %concatenate.56), channel_id=1, source_target_pairs={{0,1},{1,0},{2,3},{3,2},{4,5},{5,4},{6,7},{7,6},{8,9},{9,8},{10,11... | collective-permute-start | bytes 110600 | tf_op jit(solution)/shard_map/ppermute | solution.py:34
  130.5 7.2 %collective-permute-start.8 = (f32[6,1536]{1,0:T(8,128)S(1)}, f32[6,1536]{1,0:T(8,128)S(1)}, u32[]{:S(2)}, u32[]{:S(2)}) collective-permute-start(f32[6,1536]{1,0:T(8,128)S(1)} %add.100), channel_id=1, source_target_pairs={{0,2},{1,3},{2,0},{3,1},{4,6},{5,7},{6,4},{7,5},{8,10},{9,11},{10,... | collective-permute-start | bytes 110600 | tf_op jit(solution)/shard_map/ppermute | solution.py:34
  137.7 3.0 %collective-permute-start.9 = (f32[6,1536]{1,0:T(8,128)S(1)}, f32[6,1536]{1,0:T(8,128)S(1)}, u32[]{:S(2)}, u32[]{:S(2)}) collective-permute-start(f32[6,1536]{1,0:T(8,128)S(1)} %add.101), channel_id=1, source_target_pairs={{0,4},{1,5},{2,6},{3,7},{4,0},{5,1},{6,2},{7,3},{8,12},{9,13},{10,... | collective-permute-start | bytes 110600 | tf_op jit(solution)/shard_map/ppermute | solution.py:34
  140.7 13.8 %collective-permute-start.10 = (f32[6,1536]{1,0:T(8,128)S(1)}, f32[6,1536]{1,0:T(8,128)S(1)}, u32[]{:S(2)}, u32[]{:S(2)}) collective-permute-start(f32[6,1536]{1,0:T(8,128)S(1)} %add.102), channel_id=1, source_target_pairs={{0,8},{1,9},{2,10},{3,11},{4,12},{5,13},{6,14},{7,15},{8,0},{9,1},... | collective-permute-start | bytes 110600 | tf_op jit(solution)/shard_map/ppermute | solution.py:34
  144.2 12.5 %copy-start.2 = (bf16[512,1536]{1,0:T(8,128)(2,1)S(1)}, bf16[512,1536]{1,0:T(8,128)(2,1)}, u32[]{:S(2)}) copy-start(bf16[512,1536]{1,0:T(8,128)(2,1)} %multiply_convert_fusion) | copy-start | bytes 4718596
  144.2 12.5 %copy-start.4 = (bf16[16,2,48,1536]{3,2,1,0:T(8,128)(2,1)S(1)}, bf16[16,2,48,1536]{3,2,1,0:T(8,128)(2,1)}, u32[]{:S(2)}) copy-start(bf16[16,2,48,1536]{3,2,1,0:T(8,128)(2,1)} %copy-done.3) | copy-start | bytes 14155780
  154.5 6.5 %collective-permute-start.11 = (f32[6,1536]{1,0:T(8,128)S(1)}, f32[6,1536]{1,0:T(8,128)S(1)}, u32[]{:S(2)}, u32[]{:S(2)}) collective-permute-start(f32[6,1536]{1,0:T(8,128)S(1)} %add.103), channel_id=1, source_target_pairs={{0,16},{16,0},{32,48},{48,32},{64,80},{80,64},{96,112},{112,96},{1... | collective-permute-start | bytes 110600 | tf_op jit(solution)/shard_map/ppermute | solution.py:34
  165.0 8.2 %collective-permute-start.12 = (f32[54,1536]{1,0:T(8,128)S(1)}, f32[54,1536]{1,0:T(8,128)S(1)}, u32[]{:S(2)}, u32[]{:S(2)}) collective-permute-start(f32[54,1536]{1,0:T(8,128)S(1)} %constant_dynamic-update-slice_fusion), channel_id=1, source_target_pairs={{0,32},{16,48},{32,0},{48,16},{64,96},{80,112},{96,64},{112,80},{1... | collective-permute-start | bytes 995336 | tf_op jit(solution)/shard_map/ppermute | solution.py:34
  173.2 8.8 %collective-permute-start.13 = (f32[54,1536]{1,0:T(8,128)S(1)}, f32[54,1536]{1,0:T(8,128)S(1)}, u32[]{:S(2)}, u32[]{:S(2)}) collective-permute-start(f32[54,1536]{1,0:T(8,128)S(1)} %add.109), channel_id=1, source_target_pairs={{0,64},{16,80},{32,96},{48,112},{64,0},{80,16},{96,32},{112,48},{1... | collective-permute-start | bytes 995336 | tf_op jit(solution)/shard_map/ppermute | solution.py:34
  182.1 6.2 %collective-permute-start.14 = (f32[54,1536]{1,0:T(8,128)S(1)}, f32[54,1536]{1,0:T(8,128)S(1)}, u32[]{:S(2)}, u32[]{:S(2)}) collective-permute-start(f32[54,1536]{1,0:T(8,128)S(1)} %add.110), channel_id=1, source_target_pairs={{0,128},{16,144},{32,160},{48,176},{64,192},{80,208},{96,224},{112... | collective-permute-start | bytes 995336 | tf_op jit(solution)/shard_map/ppermute | solution.py:34
  189.0 5.7 %collective-permute-start.15 = (f32[48,1536]{1,0:T(8,128)S(1)}, f32[48,1536]{1,0:T(8,128)S(1)}, u32[]{:S(2)}, u32[]{:S(2)}) collective-permute-start(f32[48,1536]{1,0:T(8,128)S(1)} %slice.144), channel_id=1, source_target_pairs={{0,16},{16,0},{32,48},{48,32},{64,80},{80,64},{96,112},{112,96},{1... | collective-permute-start | bytes 884744 | tf_op jit(solution)/shard_map/ppermute | solution.py:40
Sparse Core Ops, SparseCore 0:
  65.3 98.7 reduce-scatter.1
